TPU v7x, 512 devices: a whole 4x4x16 slice. The times are simulated.
512 devices in a mesh: harm: 16 (over y, x), tile: 32 (over z, core).
Axes of the slice: x: 4, y: 4, z: 16, core: 2. Of those that a mesh axis runs over, the one named last changes fastest.
Arguments:
- q_old: float32 [128, 10, 128, 256], P('harm', None, 'tile'), may hold values from -37 to 37
- base_rate: float32 [5, 128, 256], P(None, 'tile'), may hold values from 1 to 1.3
- freq_table: int32 [128], replicated, may hold values from 0 to 127, each once
- wall_flags: int32 [128], P('tile'), may hold values 0 or 1
Outputs:
- q_new: float32 [128, 10, 128, 256], P('harm', None, 'tile')
Inputs may be any that keep to these rules, and one draw needn't show every extreme that they name: `freq_table`: each of 0 to 127 appears once.
All inputs are finite; a program needn't handle non-finite values. No bound on the sum of `wall_flags` on one device may be relied on, other than what follows from the above.
Results may differ from a plain program's by a relative error of at most 0.00017.
Values sent between devices are 32-bit elements; how exact they have to be, the bound alone decides.
No kernel may reach another device: no remote copies, remote signals or barrier semaphores. Data moves between devices by JAX's collectives and lax.ppermute only.
A program may use at most 64 MiB of HBM per device.

v0:
```python
import math

import jax
import jax.numpy as jnp
from jax import lax
from jax.sharding import PartitionSpec as P

ITERS = 2
SWEEPS = 4


coupling = 0.24
forcing_gain = 0.5
marching = 1.0
frequency_scale = 0.5


def extended(cells, sides, width):
    for axis, dim in sides:
        count = lax.axis_size(axis)
        head = lax.slice_in_dim(cells, 0, width, axis=dim)
        tail = lax.slice_in_dim(cells, cells.shape[dim] - width, cells.shape[dim], axis=dim)
        cells = jnp.concatenate(
            [
                lax.ppermute(tail, axis, [(i, (i + 1) % count) for i in range(count)]),
                cells,
                lax.ppermute(head, axis, [((i + 1) % count, i) for i in range(count)]),
            ],
            axis=dim,
        )
    return cells


def build_tables(frequencies):
    harm_count = frequencies.shape[0]
    sample_count = 2 * harm_count
    sample_index = jnp.arange(sample_count, dtype=jnp.int32)
    phase_index = sample_index[:, None] * frequencies[None, :] % sample_count
    angles = phase_index.astype(jnp.float32) * (2.0 * math.pi / sample_count)
    pairs = jnp.stack([jnp.cos(angles), -jnp.sin(angles)], axis=2).reshape(
        sample_count, 2 * harm_count
    )
    forward = pairs / math.sqrt(harm_count)
    backward = pairs.T / math.sqrt(sample_count)
    return (forward, backward)


def spectral_forcing(coefficients, forward, backward):
    harm_count = coefficients.shape[0]
    var_count = coefficients.shape[1] // 2
    cell_count = coefficients.shape[2]
    stacked = coefficients.reshape(2 * harm_count, var_count * cell_count)
    samples = jnp.dot(
        forward, stacked, precision=lax.Precision.HIGHEST, preferred_element_type=jnp.float32
    )
    samples = samples.reshape(forward.shape[0], var_count, cell_count)
    product = jnp.roll(samples, -1, axis=1) * jnp.roll(samples, -2, axis=1)
    folded = jnp.dot(
        backward,
        product.reshape(forward.shape[0], var_count * cell_count),
        precision=lax.Precision.HIGHEST,
        preferred_element_type=jnp.float32,
    )
    return folded.reshape(harm_count, 2 * var_count, cell_count)


def normal_sum(iterate, below_edge, above_edge):
    low_side = jnp.concatenate([below_edge, iterate[..., :-1]], axis=-1)
    high_side = jnp.concatenate([iterate[..., 1:], above_edge], axis=-1)
    return low_side + high_side


def relax(source, base_rate, frequency, beside):
    var_count = base_rate.shape[0]
    numerator = source + coupling * beside
    num_real = numerator[:, :var_count]
    num_imag = numerator[:, var_count:]
    rate_col = frequency[:, None, None, None]
    denominator = base_rate * base_rate + rate_col * rate_col
    new_real = (num_real * base_rate + num_imag * rate_col) / denominator
    new_imag = (num_imag * base_rate - num_real * rate_col) / denominator
    return jnp.concatenate([new_real, new_imag], axis=1)


def correction_terms(iterate, previous):
    var_count = previous.shape[1] // 2
    old_real = previous[:, :var_count]
    old_imag = previous[:, var_count:]
    it_real = iterate[:, :var_count]
    it_imag = iterate[:, var_count:]
    proj_real = jnp.sum(old_real * it_real + old_imag * it_imag, axis=(1, 2, 3))
    proj_imag = jnp.sum(old_real * it_imag - old_imag * it_real, axis=(1, 2, 3))
    norm_old = jnp.sum(old_real * old_real + old_imag * old_imag, axis=(1, 2, 3))
    return (proj_real, proj_imag, norm_old)


def apply_correction(iterate, previous, totals):
    proj_real, proj_imag, norm_old = totals
    var_count = previous.shape[1] // 2
    old_real = previous[:, :var_count]
    old_imag = previous[:, var_count:]
    shift_real = ((proj_real - norm_old) / norm_old)[:, None, None, None]
    shift_imag = (proj_imag / norm_old)[:, None, None, None]
    new_real = iterate[:, :var_count] - (shift_real * old_real - shift_imag * old_imag)
    new_imag = iterate[:, var_count:] - (shift_real * old_imag + shift_imag * old_real)
    return jnp.concatenate([new_real, new_imag], axis=1)


def shards(q_old, base_rate, freq_table, wall_flags):
    forward, backward = build_tables(freq_table)
    frequency_all = freq_table.astype(jnp.float32) * (frequency_scale / freq_table.shape[0])
    harm_rank = lax.axis_index("harm")
    local_harms = q_old.shape[0]
    frequency = lax.dynamic_slice_in_dim(frequency_all, harm_rank * local_harms, local_harms)
    keep_mask = (1 - wall_flags).astype(jnp.float32)[None, None, :, None]
    field = q_old
    for outer_step in range(ITERS):
        slab_block = lax.all_to_all(field, "harm", split_axis=3, concat_axis=0, tiled=True)
        harm_count, chan_count, row_count, depth = slab_block.shape
        forced = spectral_forcing(
            slab_block.reshape(harm_count, chan_count, row_count * depth), forward, backward
        )
        forced = forced.reshape(harm_count, chan_count, row_count, depth)
        forcing = lax.all_to_all(forced, "harm", split_axis=0, concat_axis=3, tiled=True)
        source = marching * q_old + forcing_gain * forcing
        iterate = field
        for sweep_step in range(SWEEPS):
            span_padded = extended(iterate, (("tile", 2),), 1)
            beside = span_padded[:, :, :-2] + span_padded[:, :, 2:]
            beside = beside + normal_sum(
                iterate, iterate[..., :1] * keep_mask, jnp.zeros_like(iterate[..., :1])
            )
            iterate = relax(source, base_rate, frequency, beside)
        totals = lax.psum(correction_terms(iterate, q_old), "tile")
        field = apply_correction(iterate, q_old, totals)
    return field


def solution(mesh):
    placed = (P("harm", None, "tile", None), P(None, "tile", None), P(), P("tile"))
    return jax.shard_map(
        shards, mesh=mesh, in_specs=placed, out_specs=P("harm", None, "tile", None), check_vma=False
    )
```

profile of v0, /device:TPU:1, one launch (start us, length us, event | category | flops | bytes accessed | tf_op | source)
XLA Modules:
  0.0 292.1 jit_solution(6001948968496916243)
XLA Ops:
  0.0 5.3 %copy.123 = f32[8,10,4,256]{1,0,2,3:T(8,128)} copy(f32[8,10,4,256]{3,2,1,0:T(4,128)} %param.4) | data formatting | bytes 655360 | tf_op args[0]
  5.3 5.9 %reshape.146 = f32[16,1,5120]{2,1,0:T(1,128)} reshape(f32[256,4,8,10]{3,2,1,0:T(8,128)} %bitcast.45) | data formatting | bytes 655360
  11.2 8.0 %all-to-all-start = ((f32[16,1,5120]{2,1,0:T(1,128)}), f32[16,1,5120]{2,1,0:T(1,128)S(1)}, u32[]{:S(2)}, u32[]{:S(2)}) async-start(f32[16,1,5120]{2,1,0:T(1,128)} %reshape.146), calls=%async_computation | async-start | bytes 655360 | tf_op jit(solution)/shard_map/all_to_all | solution.py:118
  20.0 2.5 collective-permute-start
  29.0 5.8 %reshape.147 = f32[256,4,8,10]{3,2,1,0:T(8,128)} reshape(f32[16,5120]{1,0:T(8,128)S(1)} %reduce) | data formatting | bytes 655360
  34.8 5.1 %copy.124 = f32[8,10,4,16,16]{4,2,1,0,3:T(4,128)S(1)} copy(f32[8,10,4,16,16]{1,0,2,4,3:T(8,128)} %bitcast.46) | data formatting | bytes 655360 | tf_op jit(solution)/shard_map/all_to_all | solution.py:118
  45.0 2.3 reshape_reshape.13
  47.3 2.7 reshape.148
  50.0 6.6 %all-to-all-start.1 = ((f32[16,1,5120]{2,1,0:T(1,128)}), f32[16,1,5120]{2,1,0:T(1,128)S(1)}, u32[]{:S(2)}, u32[]{:S(2)}) async-start(f32[16,1,5120]{2,1,0:T(1,128)} %reshape.148), calls=%async_computation.1 | async-start | bytes 655360 | tf_op jit(solution)/shard_map/all_to_all | solution.py:124
  57.6 6.9 %all-to-all-done.1 = f32[16,1,5120]{2,1,0:T(1,128)S(1)} async-done(((f32[16,1,5120]{2,1,0:T(1,128)}), f32[16,1,5120]{2,1,0:T(1,128)S(1)}, u32[]{:S(2)}, u32[]{:S(2)}) %all-to-all-start.1) | async-done | bytes 327712 | tf_op jit(solution)/shard_map/all_to_all | solution.py:124
  66.6 2.8 reshape.149
  76.5 2.7 mul.233
  80.7 3.7 %collective-permute-start.2 = (f32[8,10,1,256]{3,0,2,1:T(8,128)S(1)}, f32[8,10,1,256]{3,0,2,1:T(8,128)S(1)}, u32[]{:S(2)}, u32[]{:S(2)}) collective-permute-start(f32[8,10,1,256]{3,0,2,1:T(8,128)S(1)} %get-tuple-element.55), channel_id=1, source_target_pairs={{0,1},{1,2},{2,3},{3,4},{4,5},{5,6},{6,7},{7,8},{8,9},{9,10},{10,1... | collective-permute-start | bytes 245768 | tf_op jit(solution)/shard_map/ppermute | solution.py:25
  84.4 4.3 %collective-permute-start.3 = (f32[8,10,1,256]{3,0,2,1:T(8,128)S(1)}, f32[8,10,1,256]{3,0,2,1:T(8,128)S(1)}, u32[]{:S(2)}, u32[]{:S(2)}) collective-permute-start(f32[8,10,1,256]{3,0,2,1:T(8,128)S(1)} %get-tuple-element.56), channel_id=1, source_target_pairs={{1,0},{2,1},{3,2},{4,3},{5,4},{6,5},{7,6},{8,7},{9,8},{10,9},{11,1... | collective-permute-start | bytes 245768 | tf_op jit(solution)/shard_map/ppermute | solution.py:27
  90.2 4.1 %collective-permute-start.5 = (f32[8,10,1,256]{3,0,2,1:T(8,128)S(1)}, f32[8,10,1,256]{3,0,2,1:T(8,128)S(1)}, u32[]{:S(2)}, u32[]{:S(2)}) collective-permute-start(f32[8,10,1,256]{3,0,2,1:T(8,128)S(1)} %get-tuple-element.54), channel_id=1, source_target_pairs={{1,0},{2,1},{3,2},{4,3},{5,4},{6,5},{7,6},{8,7},{9,8},{10,9},{11,1... | collective-permute-start | bytes 245768 | tf_op jit(solution)/shard_map/ppermute | solution.py:27
  95.8 4.1 %collective-permute-start.7 = (f32[8,10,1,256]{3,0,2,1:T(8,128)S(1)}, f32[8,10,1,256]{3,0,2,1:T(8,128)S(1)}, u32[]{:S(2)}, u32[]{:S(2)}) collective-permute-start(f32[8,10,1,256]{3,0,2,1:T(8,128)S(1)} %get-tuple-element.52), channel_id=1, source_target_pairs={{1,0},{2,1},{3,2},{4,3},{5,4},{6,5},{7,6},{8,7},{9,8},{10,9},{11,1... | collective-permute-start | bytes 245768 | tf_op jit(solution)/shard_map/ppermute | solution.py:27
  101.4 49.3 %all-reduce.9 = (f32[8]{0:T(128)S(1)}, f32[8]{0:T(128)S(1)}, f32[8]{0:T(128)S(1)}) all-reduce(f32[8]{0:T(128)S(1)} %get-tuple-element.8, f32[8]{0:T(128)S(1)} %get-tuple-element.9, f32[8]{0:T(128)S(1)} %get-tuple-element.7), channel_id=1, replica_groups=mesh['harm'=16,'tile'=32] {'tile'}, use_global_device_ids=true, to_apply=%region_5.6 | all-reduce | flops 24 | bytes 192 | tf_op jit(solution)/shard_map/psum | solution.py:134
  151.0 4.5 %copy.141 = f32[8,10,4,256]{1,0,2,3:T(8,128)} copy(f32[8,10,4,256]{3,0,2,1:T(8,128)S(1)} %pad_maximum_fusion) | data formatting | bytes 655360 | tf_op jit(solution)/shard_map/concatenate | solution.py:106
  155.4 5.8 %reshape.150 = f32[16,1,5120]{2,1,0:T(1,128)} reshape(f32[256,4,8,10]{3,2,1,0:T(8,128)} %bitcast.44) | data formatting | bytes 655360
  161.3 3.7 %all-to-all-start.2 = ((f32[16,1,5120]{2,1,0:T(1,128)}), f32[16,1,5120]{2,1,0:T(1,128)S(1)}, u32[]{:S(2)}, u32[]{:S(2)}) async-start(f32[16,1,5120]{2,1,0:T(1,128)} %reshape.150), calls=%async_computation.2 | async-start | bytes 655360 | tf_op jit(solution)/shard_map/all_to_all | solution.py:118
  169.3 3.6 %all-to-all-done.2 = f32[16,1,5120]{2,1,0:T(1,128)S(1)} async-done(((f32[16,1,5120]{2,1,0:T(1,128)}), f32[16,1,5120]{2,1,0:T(1,128)S(1)}, u32[]{:S(2)}, u32[]{:S(2)}) %all-to-all-start.2) | async-done | bytes 327712 | tf_op jit(solution)/shard_map/all_to_all | solution.py:118
  174.2 5.8 %reshape.151 = f32[256,4,8,10]{3,2,1,0:T(8,128)} reshape(f32[16,5120]{1,0:T(8,128)S(1)} %reduce.2) | data formatting | bytes 655360
  180.0 5.1 %copy.142 = f32[8,10,4,16,16]{4,2,1,0,3:T(4,128)S(1)} copy(f32[8,10,4,16,16]{1,0,2,4,3:T(8,128)} %bitcast.47) | data formatting | bytes 655360 | tf_op jit(solution)/shard_map/all_to_all | solution.py:118
  192.5 2.7 reshape.152
  195.2 3.8 %all-to-all-start.3 = ((f32[16,1,5120]{2,1,0:T(1,128)}), f32[16,1,5120]{2,1,0:T(1,128)S(1)}, u32[]{:S(2)}, u32[]{:S(2)}) async-start(f32[16,1,5120]{2,1,0:T(1,128)} %reshape.152), calls=%async_computation.3 | async-start | bytes 655360 | tf_op jit(solution)/shard_map/all_to_all | solution.py:124
  199.9 6.8 %all-to-all-done.3 = f32[16,1,5120]{2,1,0:T(1,128)S(1)} async-done(((f32[16,1,5120]{2,1,0:T(1,128)}), f32[16,1,5120]{2,1,0:T(1,128)S(1)}, u32[]{:S(2)}, u32[]{:S(2)}) %all-to-all-start.3) | async-done | bytes 327712 | tf_op jit(solution)/shard_map/all_to_all | solution.py:124
  208.9 2.8 reshape.153
  218.8 2.7 mul.527
  223.0 4.0 %collective-permute-start.10 = (f32[8,10,1,256]{3,0,2,1:T(8,128)S(1)}, f32[8,10,1,256]{3,0,2,1:T(8,128)S(1)}, u32[]{:S(2)}, u32[]{:S(2)}) collective-permute-start(f32[8,10,1,256]{3,0,2,1:T(8,128)S(1)} %get-tuple-element.45), channel_id=1, source_target_pairs={{0,1},{1,2},{2,3},{3,4},{4,5},{5,6},{6,7},{7,8},{8,9},{9,10},{10,1... | collective-permute-start | bytes 245768 | tf_op jit(solution)/shard_map/ppermute | solution.py:25
  231.4 3.1 %collective-permute-start.13 = (f32[8,10,1,256]{3,0,2,1:T(8,128)S(1)}, f32[8,10,1,256]{3,0,2,1:T(8,128)S(1)}, u32[]{:S(2)}, u32[]{:S(2)}) collective-permute-start(f32[8,10,1,256]{3,0,2,1:T(8,128)S(1)} %get-tuple-element.44), channel_id=1, source_target_pairs={{1,0},{2,1},{3,2},{4,3},{5,4},{6,5},{7,6},{8,7},{9,8},{10,9},{11,1... | collective-permute-start | bytes 245768 | tf_op jit(solution)/shard_map/ppermute | solution.py:27
  235.9 4.1 %collective-permute-start.15 = (f32[8,10,1,256]{3,0,2,1:T(8,128)S(1)}, f32[8,10,1,256]{3,0,2,1:T(8,128)S(1)}, u32[]{:S(2)}, u32[]{:S(2)}) collective-permute-start(f32[8,10,1,256]{3,0,2,1:T(8,128)S(1)} %get-tuple-element.42), channel_id=1, source_target_pairs={{1,0},{2,1},{3,2},{4,3},{5,4},{6,5},{7,6},{8,7},{9,8},{10,9},{11,1... | collective-permute-start | bytes 245768 | tf_op jit(solution)/shard_map/ppermute | solution.py:27
  241.5 49.3 %all-reduce.8 = (f32[8]{0:T(128)S(1)}, f32[8]{0:T(128)S(1)}) all-reduce(f32[8]{0:T(128)S(1)} %get-tuple-element.6, f32[8]{0:T(128)S(1)} %get-tuple-element.5), channel_id=1, replica_groups=mesh['harm'=16,'tile'=32] {'tile'}, use_global_device_ids=true, to_apply=%region_9.10 | all-reduce | flops 16 | bytes 128 | tf_op jit(solution)/shard_map/psum | solution.py:134
  (147 shorter events, 61.2 us)
Async XLA Ops:
  5.3 13.9 %copy-start = (f32[8,10,4,256]{3,2,1,0:T(4,128)S(1)}, f32[8,10,4,256]{3,2,1,0:T(4,128)}, u32[]{:S(2)}) copy-start(f32[8,10,4,256]{3,2,1,0:T(4,128)} %param.4) | copy-start | bytes 983044
  5.3 17.5 %copy-start.14 = (s32[128]{0:T(128)S(1)}, s32[128]{0:T(128)}, u32[]{:S(2)}) copy-start(s32[128]{0:T(128)} %param.6) | copy-start | bytes 1540
  5.3 18.1 %copy-start.15 = (s32[4]{0:T(128)S(1)}, s32[4]{0:T(128)}, u32[]{:S(2)}) copy-start(s32[4]{0:T(128)} %param.7) | copy-start | bytes 52
  11.2 13.7 %copy-start.4 = (f32[5,4,256]{2,1,0:T(4,128)S(1)}, f32[5,4,256]{2,1,0:T(4,128)}, u32[]{:S(2)}) copy-start(f32[5,4,256]{2,1,0:T(4,128)} %param.5) | copy-start | bytes 61444
  11.2 15.9 %all-to-all-start = ((f32[16,1,5120]{2,1,0:T(1,128)}), f32[16,1,5120]{2,1,0:T(1,128)S(1)}, u32[]{:S(2)}, u32[]{:S(2)}) async-start(f32[16,1,5120]{2,1,0:T(1,128)} %reshape.146), calls=%async_computation | async-start | bytes 655360 | tf_op jit(solution)/shard_map/all_to_all | solution.py:118
  20.0 59.1 %collective-permute-start = (f32[8,10,1,256]{3,0,2,1:T(8,128)}, f32[8,10,1,256]{3,0,2,1:T(8,128)}, u32[]{:S(2)}, u32[]{:S(2)}) collective-permute-start(f32[8,10,1,256]{3,0,2,1:T(8,128)} %get-tuple-element.59), channel_id=1, source_target_pairs={{0,1},{1,2},{2,3},{3,4},{4,5},{5,6},{6,7},{7,8},{8,9},{9,10},{10,1... | collective-permute-start | bytes 245768 | tf_op jit(solution)/shard_map/ppermute | solution.py:25
  22.5 56.7 %collective-permute-start.1 = (f32[8,10,1,256]{3,0,2,1:T(8,128)}, f32[8,10,1,256]{3,0,2,1:T(8,128)}, u32[]{:S(2)}, u32[]{:S(2)}) collective-permute-start(f32[8,10,1,256]{3,0,2,1:T(8,128)} %get-tuple-element.60), channel_id=1, source_target_pairs={{1,0},{2,1},{3,2},{4,3},{5,4},{6,5},{7,6},{8,7},{9,8},{10,9},{11,1... | collective-permute-start | bytes 245768 | tf_op jit(solution)/shard_map/ppermute | solution.py:27
  50.0 14.5 %all-to-all-start.1 = ((f32[16,1,5120]{2,1,0:T(1,128)}), f32[16,1,5120]{2,1,0:T(1,128)S(1)}, u32[]{:S(2)}, u32[]{:S(2)}) async-start(f32[16,1,5120]{2,1,0:T(1,128)} %reshape.148), calls=%async_computation.1 | async-start | bytes 655360 | tf_op jit(solution)/shard_map/all_to_all | solution.py:124
  76.5 2.8 copy-start.13
  76.5 4.0 %copy-start.5 = (f32[5,4,256]{2,1,0:T(4,128)S(1)}, f32[5,4,256]{2,1,0:T(4,128)}, u32[]{:S(2)}) copy-start(f32[5,4,256]{2,1,0:T(4,128)} %param.5) | copy-start | bytes 61444
  76.5 4.0 %copy-start.7 = (f32[5,4,256]{2,1,0:T(4,128)S(1)}, f32[5,4,256]{2,1,0:T(4,128)}, u32[]{:S(2)}) copy-start(f32[5,4,256]{2,1,0:T(4,128)} %mul.488) | copy-start | bytes 61444
  80.7 8.8 %collective-permute-start.2 = (f32[8,10,1,256]{3,0,2,1:T(8,128)S(1)}, f32[8,10,1,256]{3,0,2,1:T(8,128)S(1)}, u32[]{:S(2)}, u32[]{:S(2)}) collective-permute-start(f32[8,10,1,256]{3,0,2,1:T(8,128)S(1)} %get-tuple-element.55), channel_id=1, source_target_pairs={{0,1},{1,2},{2,3},{3,4},{4,5},{5,6},{6,7},{7,8},{8,9},{9,10},{10,1... | collective-permute-start | bytes 245768 | tf_op jit(solution)/shard_map/ppermute | solution.py:25
  84.4 5.3 %collective-permute-start.3 = (f32[8,10,1,256]{3,0,2,1:T(8,128)S(1)}, f32[8,10,1,256]{3,0,2,1:T(8,128)S(1)}, u32[]{:S(2)}, u32[]{:S(2)}) collective-permute-start(f32[8,10,1,256]{3,0,2,1:T(8,128)S(1)} %get-tuple-element.56), channel_id=1, source_target_pairs={{1,0},{2,1},{3,2},{4,3},{5,4},{6,5},{7,6},{8,7},{9,8},{10,9},{11,1... | collective-permute-start | bytes 245768 | tf_op jit(solution)/shard_map/ppermute | solution.py:27
  90.2 4.9 %collective-permute-start.4 = (f32[8,10,1,256]{3,0,2,1:T(8,128)S(1)}, f32[8,10,1,256]{3,0,2,1:T(8,128)S(1)}, u32[]{:S(2)}, u32[]{:S(2)}) collective-permute-start(f32[8,10,1,256]{3,0,2,1:T(8,128)S(1)} %get-tuple-element.53), channel_id=1, source_target_pairs={{0,1},{1,2},{2,3},{3,4},{4,5},{5,6},{6,7},{7,8},{8,9},{9,10},{10,1... | collective-permute-start | bytes 245768 | tf_op jit(solution)/shard_map/ppermute | solution.py:25
  90.2 5.1 %collective-permute-start.5 = (f32[8,10,1,256]{3,0,2,1:T(8,128)S(1)}, f32[8,10,1,256]{3,0,2,1:T(8,128)S(1)}, u32[]{:S(2)}, u32[]{:S(2)}) collective-permute-start(f32[8,10,1,256]{3,0,2,1:T(8,128)S(1)} %get-tuple-element.54), channel_id=1, source_target_pairs={{1,0},{2,1},{3,2},{4,3},{5,4},{6,5},{7,6},{8,7},{9,8},{10,9},{11,1... | collective-permute-start | bytes 245768 | tf_op jit(solution)/shard_map/ppermute | solution.py:27
  95.8 4.9 %collective-permute-start.6 = (f32[8,10,1,256]{3,0,2,1:T(8,128)S(1)}, f32[8,10,1,256]{3,0,2,1:T(8,128)S(1)}, u32[]{:S(2)}, u32[]{:S(2)}) collective-permute-start(f32[8,10,1,256]{3,0,2,1:T(8,128)S(1)} %get-tuple-element.51), channel_id=1, source_target_pairs={{0,1},{1,2},{2,3},{3,4},{4,5},{5,6},{6,7},{7,8},{8,9},{9,10},{10,1... | collective-permute-start | bytes 245768 | tf_op jit(solution)/shard_map/ppermute | solution.py:25
  95.8 5.1 %collective-permute-start.7 = (f32[8,10,1,256]{3,0,2,1:T(8,128)S(1)}, f32[8,10,1,256]{3,0,2,1:T(8,128)S(1)}, u32[]{:S(2)}, u32[]{:S(2)}) collective-permute-start(f32[8,10,1,256]{3,0,2,1:T(8,128)S(1)} %get-tuple-element.52), channel_id=1, source_target_pairs={{1,0},{2,1},{3,2},{4,3},{5,4},{6,5},{7,6},{8,7},{9,8},{10,9},{11,1... | collective-permute-start | bytes 245768 | tf_op jit(solution)/shard_map/ppermute | solution.py:27
  161.3 11.6 %all-to-all-start.2 = ((f32[16,1,5120]{2,1,0:T(1,128)}), f32[16,1,5120]{2,1,0:T(1,128)S(1)}, u32[]{:S(2)}, u32[]{:S(2)}) async-start(f32[16,1,5120]{2,1,0:T(1,128)} %reshape.150), calls=%async_computation.2 | async-start | bytes 655360 | tf_op jit(solution)/shard_map/all_to_all | solution.py:118
  165.7 55.8 %collective-permute-start.8 = (f32[8,10,1,256]{3,0,2,1:T(8,128)}, f32[8,10,1,256]{3,0,2,1:T(8,128)}, u32[]{:S(2)}, u32[]{:S(2)}) collective-permute-start(f32[8,10,1,256]{3,0,2,1:T(8,128)} %get-tuple-element.49), channel_id=1, source_target_pairs={{0,1},{1,2},{2,3},{3,4},{4,5},{5,6},{6,7},{7,8},{8,9},{9,10},{10,1... | collective-permute-start | bytes 245768 | tf_op jit(solution)/shard_map/ppermute | solution.py:25
  167.4 54.1 %collective-permute-start.9 = (f32[8,10,1,256]{3,0,2,1:T(8,128)}, f32[8,10,1,256]{3,0,2,1:T(8,128)}, u32[]{:S(2)}, u32[]{:S(2)}) collective-permute-start(f32[8,10,1,256]{3,0,2,1:T(8,128)} %get-tuple-element.50), channel_id=1, source_target_pairs={{1,0},{2,1},{3,2},{4,3},{5,4},{6,5},{7,6},{8,7},{9,8},{10,9},{11,1... | collective-permute-start | bytes 245768 | tf_op jit(solution)/shard_map/ppermute | solution.py:27
  195.2 11.6 %all-to-all-start.3 = ((f32[16,1,5120]{2,1,0:T(1,128)}), f32[16,1,5120]{2,1,0:T(1,128)S(1)}, u32[]{:S(2)}, u32[]{:S(2)}) async-start(f32[16,1,5120]{2,1,0:T(1,128)} %reshape.152), calls=%async_computation.3 | async-start | bytes 655360 | tf_op jit(solution)/shard_map/all_to_all | solution.py:124
  218.8 2.8 copy-start.1
  218.8 2.8 copy-start.11
  218.8 2.8 copy-start.12
  218.8 4.0 %copy-start.6 = (f32[5,4,256]{2,1,0:T(4,128)S(1)}, f32[5,4,256]{2,1,0:T(4,128)}, u32[]{:S(2)}) copy-start(f32[5,4,256]{2,1,0:T(4,128)} %param.5) | copy-start | bytes 61444
  218.8 4.0 %copy-start.8 = (f32[5,4,256]{2,1,0:T(4,128)S(1)}, f32[5,4,256]{2,1,0:T(4,128)}, u32[]{:S(2)}) copy-start(f32[5,4,256]{2,1,0:T(4,128)} %mul.488) | copy-start | bytes 61444
  223.0 6.7 %collective-permute-start.10 = (f32[8,10,1,256]{3,0,2,1:T(8,128)S(1)}, f32[8,10,1,256]{3,0,2,1:T(8,128)S(1)}, u32[]{:S(2)}, u32[]{:S(2)}) collective-permute-start(f32[8,10,1,256]{3,0,2,1:T(8,128)S(1)} %get-tuple-element.45), channel_id=1, source_target_pairs={{0,1},{1,2},{2,3},{3,4},{4,5},{5,6},{6,7},{7,8},{8,9},{9,10},{10,1... | collective-permute-start | bytes 245768 | tf_op jit(solution)/shard_map/ppermute | solution.py:25
  227.0 3.9 %collective-permute-start.11 = (f32[8,10,1,256]{3,0,2,1:T(8,128)S(1)}, f32[8,10,1,256]{3,0,2,1:T(8,128)S(1)}, u32[]{:S(2)}, u32[]{:S(2)}) collective-permute-start(f32[8,10,1,256]{3,0,2,1:T(8,128)S(1)} %get-tuple-element.46), channel_id=1, source_target_pairs={{1,0},{2,1},{3,2},{4,3},{5,4},{6,5},{7,6},{8,7},{9,8},{10,9},{11,1... | collective-permute-start | bytes 245768 | tf_op jit(solution)/shard_map/ppermute | solution.py:27
  231.4 3.8 %collective-permute-start.12 = (f32[8,10,1,256]{3,0,2,1:T(8,128)S(1)}, f32[8,10,1,256]{3,0,2,1:T(8,128)S(1)}, u32[]{:S(2)}, u32[]{:S(2)}) collective-permute-start(f32[8,10,1,256]{3,0,2,1:T(8,128)S(1)} %get-tuple-element.43), channel_id=1, source_target_pairs={{0,1},{1,2},{2,3},{3,4},{4,5},{5,6},{6,7},{7,8},{8,9},{9,10},{10,1... | collective-permute-start | bytes 245768 | tf_op jit(solution)/shard_map/ppermute | solution.py:25
  231.4 4.0 %collective-permute-start.13 = (f32[8,10,1,256]{3,0,2,1:T(8,128)S(1)}, f32[8,10,1,256]{3,0,2,1:T(8,128)S(1)}, u32[]{:S(2)}, u32[]{:S(2)}) collective-permute-start(f32[8,10,1,256]{3,0,2,1:T(8,128)S(1)} %get-tuple-element.44), channel_id=1, source_target_pairs={{1,0},{2,1},{3,2},{4,3},{5,4},{6,5},{7,6},{8,7},{9,8},{10,9},{11,1... | collective-permute-start | bytes 245768 | tf_op jit(solution)/shard_map/ppermute | solution.py:27
  235.9 4.9 %collective-permute-start.14 = (f32[8,10,1,256]{3,0,2,1:T(8,128)S(1)}, f32[8,10,1,256]{3,0,2,1:T(8,128)S(1)}, u32[]{:S(2)}, u32[]{:S(2)}) collective-permute-start(f32[8,10,1,256]{3,0,2,1:T(8,128)S(1)} %get-tuple-element.41), channel_id=1, source_target_pairs={{0,1},{1,2},{2,3},{3,4},{4,5},{5,6},{6,7},{7,8},{8,9},{9,10},{10,1... | collective-permute-start | bytes 245768 | tf_op jit(solution)/shard_map/ppermute | solution.py:25
  235.9 5.1 %collective-permute-start.15 = (f32[8,10,1,256]{3,0,2,1:T(8,128)S(1)}, f32[8,10,1,256]{3,0,2,1:T(8,128)S(1)}, u32[]{:S(2)}, u32[]{:S(2)}) collective-permute-start(f32[8,10,1,256]{3,0,2,1:T(8,128)S(1)} %get-tuple-element.42), channel_id=1, source_target_pairs={{1,0},{2,1},{3,2},{4,3},{5,4},{6,5},{7,6},{8,7},{9,8},{10,9},{11,1... | collective-permute-start | bytes 245768 | tf_op jit(solution)/shard_map/ppermute | solution.py:27
  (4 other events, 9.1 us)
where the time goes:
time: 297 us; the launch traced here: 292 us
  blocking collectives  98.7 us (33%)
  local copies, waits for them, and re-layouts  86 us (29%)
  starting transfers between devices  58 us (20%)
  waiting for transfers between devices  24.7 us (8%)
  other arithmetic  20.4 us (7%)
  matrix products  3.53 us (1%)
    psum x2, blocking collectives, shards(): totals = lax.psum(correction_terms(iterate, q_old), 'tile')  98.7 us
    unnamed x42, local copies, waits for them, and re-layouts  39.7 us
    ppermute x8, starting transfers between devices, extended(): lax.ppermute(head, axis, [((i + 1) % count, i) for i in range(count)])  23.9 us
    all_to_all x2, waiting for transfers between devices, shards(): lax.all_to_all(forced, 'harm', split_axis=0, concat_axis=3, tiled=True)  13.7 us
    mul x6, local copies, waits for them, and re-layouts, shards(): source = marching * q_old + forcing_gain * forcing  12.8 us
    ppermute x8, starting transfers between devices, extended(): lax.ppermute(tail, axis, [(i, (i + 1) % count) for i in range(count)])  12 us
    all_to_all x2, starting transfers between devices, shards(): lax.all_to_all(field, 'harm', split_axis=3, concat_axis=0, tiled=True)  11.7 us
    all_to_all x3, local copies, waits for them, and re-layouts, shards(): lax.all_to_all(field, 'harm', split_axis=3, concat_axis=0, tiled=True)  10.7 us
  transfers between devices with their start and end apart: 20, of which 16 were waited for; matrix products, arithmetic and copies ran while one was open for 28% of the time, Pallas kernels for 0%

commit v1 on v0

--- a/solution.py
+++ b/solution.py
@@ -29,6 +29,17 @@
             axis=dim,
         )
     return cells
+
+
+def tile_sum(values, axis):
+    count = lax.axis_size(axis)
+    if count & (count - 1):
+        return lax.psum(values, axis)
+    step = 1
+    while step < count:
+        values = values + lax.ppermute(values, axis, [(i, i ^ step) for i in range(count)])
+        step *= 2
+    return values
 
 
 def build_tables(frequencies):
@@ -131,7 +142,7 @@
                 iterate, iterate[..., :1] * keep_mask, jnp.zeros_like(iterate[..., :1])
             )
             iterate = relax(source, base_rate, frequency, beside)
-        totals = lax.psum(correction_terms(iterate, q_old), "tile")
+        totals = tile_sum(jnp.stack(correction_terms(iterate, q_old)), "tile")
         field = apply_correction(iterate, q_old, totals)
     return field
 

time: 297 us -> 279 us (0.939)
  the two profiles are of different devices: /device:TPU:1 before, /device:TPU:32 now
where the time goes in v1:
time: 279 us; the launch traced here: 275 us
  starting transfers between devices  99.4 us (36%)
  local copies, waits for them, and re-layouts  85.9 us (31%)
  waiting for transfers between devices  64.4 us (23%)
  other arithmetic  20.5 us (7%)
  matrix products  3.52 us (1%)
    ppermute x10, starting transfers between devices, tile_sum(): lax.ppermute(values, axis, [(i, i ^ step) for i in range(count)])  63.2 us
    unnamed x42, local copies, waits for them, and re-layouts  39.7 us
    ppermute x10, waiting for transfers between devices, tile_sum(): lax.ppermute(values, axis, [(i, i ^ step) for i in range(count)])  25.1 us
    all_to_all x2, waiting for transfers between devices, shards(): lax.all_to_all(forced, 'harm', split_axis=0, concat_axis=3, tiled=True)  16.8 us
    mul x6, local copies, waits for them, and re-layouts, shards(): source = marching * q_old + forcing_gain * forcing  12.8 us
    ppermute x8, waiting for transfers between devices, extended(): lax.ppermute(tail, axis, [(i, (i + 1) % count) for i in range(count)])  12.5 us
    all_to_all x2, starting transfers between devices, shards(): lax.all_to_all(field, 'harm', split_axis=3, concat_axis=0, tiled=True)  11.2 us
    all_to_all x3, local copies, waits for them, and re-layouts, shards(): lax.all_to_all(field, 'harm', split_axis=3, concat_axis=0, tiled=True)  10.7 us
  transfers between devices with their start and end apart: 30, of which 20 were waited for; matrix products, arithmetic and copies ran while one was open for 30% of the time, Pallas kernels for 0%

profile of v1, /device:TPU:32, one launch (start us, length us, event | category | flops | bytes accessed | tf_op | source)
XLA Modules:
  0.0 274.8 jit_solution(11606577289665239868)
XLA Ops:
  0.0 5.3 %copy.123 = f32[8,10,4,256]{1,0,2,3:T(8,128)} copy(f32[8,10,4,256]{3,2,1,0:T(4,128)} %param.4) | data formatting | bytes 655360 | tf_op args[0]
  5.3 5.9 %reshape.186 = f32[16,1,5120]{2,1,0:T(1,128)} reshape(f32[256,4,8,10]{3,2,1,0:T(8,128)} %bitcast.64) | data formatting | bytes 655360
  11.2 7.5 %all-to-all-start = ((f32[16,1,5120]{2,1,0:T(1,128)}), f32[16,1,5120]{2,1,0:T(1,128)S(1)}, u32[]{:S(2)}, u32[]{:S(2)}) async-start(f32[16,1,5120]{2,1,0:T(1,128)} %reshape.186), calls=%async_computation | async-start | bytes 655360 | tf_op jit(solution)/shard_map/all_to_all | solution.py:129
  24.6 3.4 %all-to-all-done = f32[16,1,5120]{2,1,0:T(1,128)S(1)} async-done(((f32[16,1,5120]{2,1,0:T(1,128)}), f32[16,1,5120]{2,1,0:T(1,128)S(1)}, u32[]{:S(2)}, u32[]{:S(2)}) %all-to-all-start) | async-done | bytes 327712 | tf_op jit(solution)/shard_map/all_to_all | solution.py:129
  29.9 5.8 %reshape.187 = f32[256,4,8,10]{3,2,1,0:T(8,128)} reshape(f32[16,5120]{1,0:T(8,128)S(1)} %reduce) | data formatting | bytes 655360
  35.7 5.1 %copy.124 = f32[8,10,4,16,16]{4,2,1,0,3:T(4,128)S(1)} copy(f32[8,10,4,16,16]{1,0,2,4,3:T(8,128)} %bitcast.65) | data formatting | bytes 655360 | tf_op jit(solution)/shard_map/all_to_all | solution.py:129
  50.9 4.4 %all-to-all-start.1 = ((f32[16,1,5120]{2,1,0:T(1,128)}), f32[16,1,5120]{2,1,0:T(1,128)S(1)}, u32[]{:S(2)}, u32[]{:S(2)}) async-start(f32[16,1,5120]{2,1,0:T(1,128)} %reshape.188), calls=%async_computation.1 | async-start | bytes 655360 | tf_op jit(solution)/shard_map/all_to_all | solution.py:135
  56.3 8.8 %all-to-all-done.1 = f32[16,1,5120]{2,1,0:T(1,128)S(1)} async-done(((f32[16,1,5120]{2,1,0:T(1,128)}), f32[16,1,5120]{2,1,0:T(1,128)S(1)}, u32[]{:S(2)}, u32[]{:S(2)}) %all-to-all-start.1) | async-done | bytes 327712 | tf_op jit(solution)/shard_map/all_to_all | solution.py:135
  67.2 2.8 %reshape.189 = f32[128,10,4,16]{3,2,1,0:T(4,128)S(1)} reshape(f32[16,5120]{1,0:T(8,128)} %reduce.1) | data formatting | bytes 655360
  97.2 5.0 %collective-permute-start.8 = (f32[3,8]{1,0:T(4,128)S(1)}, f32[3,8]{1,0:T(4,128)S(1)}, u32[]{:S(2)}, u32[]{:S(2)}) collective-permute-start(f32[3,8]{1,0:T(4,128)S(1)} %pad_maximum_fusion.34), channel_id=1, source_target_pairs={{0,1},{1,0},{2,3},{3,2},{4,5},{5,4},{6,7},{7,6},{8,9},{9,8},{10,11... | collective-permute-start | bytes 296 | tf_op jit(solution)/shard_map/ppermute | solution.py:40
  103.1 6.1 %collective-permute-start.9 = (f32[3,8]{1,0:T(4,128)S(1)}, f32[3,8]{1,0:T(4,128)S(1)}, u32[]{:S(2)}, u32[]{:S(2)}) collective-permute-start(f32[3,8]{1,0:T(4,128)S(1)} %fusion.87), channel_id=1, source_target_pairs={{0,2},{1,3},{2,0},{3,1},{4,6},{5,7},{6,4},{7,5},{8,10},{9,11},{10,... | collective-permute-start | bytes 296 | tf_op jit(solution)/shard_map/ppermute | solution.py:40
  110.8 4.6 %collective-permute-start.10 = (f32[3,8]{1,0:T(4,128)S(1)}, f32[3,8]{1,0:T(4,128)S(1)}, u32[]{:S(2)}, u32[]{:S(2)}) collective-permute-start(f32[3,8]{1,0:T(4,128)S(1)} %fusion.101), channel_id=1, source_target_pairs={{0,4},{1,5},{2,6},{3,7},{4,0},{5,1},{6,2},{7,3},{8,12},{9,13},{10,... | collective-permute-start | bytes 296 | tf_op jit(solution)/shard_map/ppermute | solution.py:40
  117.1 8.8 %collective-permute-start.11 = (f32[3,8]{1,0:T(4,128)S(1)}, f32[3,8]{1,0:T(4,128)S(1)}, u32[]{:S(2)}, u32[]{:S(2)}) collective-permute-start(f32[3,8]{1,0:T(4,128)S(1)} %add.300), channel_id=1, source_target_pairs={{0,8},{1,9},{2,10},{3,11},{4,12},{5,13},{6,14},{7,15},{8,0},{9,1},... | collective-permute-start | bytes 296 | tf_op jit(solution)/shard_map/ppermute | solution.py:40
  127.5 9.6 %collective-permute-start.12 = (f32[3,8]{1,0:T(4,128)S(1)}, f32[3,8]{1,0:T(4,128)S(1)}, u32[]{:S(2)}, u32[]{:S(2)}) collective-permute-start(f32[3,8]{1,0:T(4,128)S(1)} %add.301), channel_id=1, source_target_pairs={{0,16},{1,17},{2,18},{3,19},{4,20},{5,21},{6,22},{7,23},{8,24},{9,... | collective-permute-start | bytes 296 | tf_op jit(solution)/shard_map/ppermute | solution.py:40
  137.2 4.5 %collective-permute-done.12 = f32[3,8]{1,0:T(4,128)S(1)} collective-permute-done((f32[3,8]{1,0:T(4,128)S(1)}, f32[3,8]{1,0:T(4,128)S(1)}, u32[]{:S(2)}, u32[]{:S(2)}) %collective-permute-start.12) | collective-permute-done | bytes 128 | tf_op jit(solution)/shard_map/ppermute | solution.py:40
  141.9 4.5 %copy.141 = f32[8,10,4,256]{1,0,2,3:T(8,128)} copy(f32[8,10,4,256]{3,0,2,1:T(8,128)S(1)} %pad_maximum_fusion) | data formatting | bytes 655360 | tf_op jit(solution)/shard_map/concatenate | solution.py:117
  146.4 5.8 %reshape.190 = f32[16,1,5120]{2,1,0:T(1,128)} reshape(f32[256,4,8,10]{3,2,1,0:T(8,128)} %bitcast.63) | data formatting | bytes 655360
  152.2 3.7 %all-to-all-start.2 = ((f32[16,1,5120]{2,1,0:T(1,128)}), f32[16,1,5120]{2,1,0:T(1,128)S(1)}, u32[]{:S(2)}, u32[]{:S(2)}) async-start(f32[16,1,5120]{2,1,0:T(1,128)} %reshape.190), calls=%async_computation.2 | async-start | bytes 655360 | tf_op jit(solution)/shard_map/all_to_all | solution.py:129
  158.4 6.6 %all-to-all-done.2 = f32[16,1,5120]{2,1,0:T(1,128)S(1)} async-done(((f32[16,1,5120]{2,1,0:T(1,128)}), f32[16,1,5120]{2,1,0:T(1,128)S(1)}, u32[]{:S(2)}, u32[]{:S(2)}) %all-to-all-start.2) | async-done | bytes 327712 | tf_op jit(solution)/shard_map/all_to_all | solution.py:129
  166.3 5.8 %reshape.191 = f32[256,4,8,10]{3,2,1,0:T(8,128)} reshape(f32[16,5120]{1,0:T(8,128)S(1)} %reduce.2) | data formatting | bytes 655360
  172.1 5.1 %copy.142 = f32[8,10,4,16,16]{4,2,1,0,3:T(4,128)S(1)} copy(f32[8,10,4,16,16]{1,0,2,4,3:T(8,128)} %bitcast.66) | data formatting | bytes 655360 | tf_op jit(solution)/shard_map/all_to_all | solution.py:129
  187.3 3.8 %all-to-all-start.3 = ((f32[16,1,5120]{2,1,0:T(1,128)}), f32[16,1,5120]{2,1,0:T(1,128)S(1)}, u32[]{:S(2)}, u32[]{:S(2)}) async-start(f32[16,1,5120]{2,1,0:T(1,128)} %reshape.192), calls=%async_computation.3 | async-start | bytes 655360 | tf_op jit(solution)/shard_map/all_to_all | solution.py:135
  192.1 8.0 %all-to-all-done.3 = f32[16,1,5120]{2,1,0:T(1,128)S(1)} async-done(((f32[16,1,5120]{2,1,0:T(1,128)}), f32[16,1,5120]{2,1,0:T(1,128)S(1)}, u32[]{:S(2)}, u32[]{:S(2)}) %all-to-all-start.3) | async-done | bytes 327712 | tf_op jit(solution)/shard_map/all_to_all | solution.py:135
  202.1 2.8 %reshape.193 = f32[128,10,4,16]{3,2,1,0:T(4,128)S(1)} reshape(f32[16,5120]{1,0:T(8,128)} %reduce.3) | data formatting | bytes 655360
  212.1 2.7 mul.527
  229.6 5.7 %collective-permute-start.21 = (f32[3,8]{1,0:T(4,128)S(1)}, f32[3,8]{1,0:T(4,128)S(1)}, u32[]{:S(2)}, u32[]{:S(2)}) collective-permute-start(f32[3,8]{1,0:T(4,128)S(1)} %pad_maximum_fusion.33), channel_id=1, source_target_pairs={{0,1},{1,0},{2,3},{3,2},{4,5},{5,4},{6,7},{7,6},{8,9},{9,8},{10,11... | collective-permute-start | bytes 296 | tf_op jit(solution)/shard_map/ppermute | solution.py:40
  236.1 2.9 %collective-permute-start.22 = (f32[3,8]{1,0:T(4,128)S(1)}, f32[3,8]{1,0:T(4,128)S(1)}, u32[]{:S(2)}, u32[]{:S(2)}) collective-permute-start(f32[3,8]{1,0:T(4,128)S(1)} %fusion.88), channel_id=1, source_target_pairs={{0,2},{1,3},{2,0},{3,1},{4,6},{5,7},{6,4},{7,5},{8,10},{9,11},{10,... | collective-permute-start | bytes 296 | tf_op jit(solution)/shard_map/ppermute | solution.py:40
  241.6 6.8 %collective-permute-start.23 = (f32[3,8]{1,0:T(4,128)S(1)}, f32[3,8]{1,0:T(4,128)S(1)}, u32[]{:S(2)}, u32[]{:S(2)}) collective-permute-start(f32[3,8]{1,0:T(4,128)S(1)} %fusion.100), channel_id=1, source_target_pairs={{0,4},{1,5},{2,6},{3,7},{4,0},{5,1},{6,2},{7,3},{8,12},{9,13},{10,... | collective-permute-start | bytes 296 | tf_op jit(solution)/shard_map/ppermute | solution.py:40
  250.0 5.9 %collective-permute-start.24 = (f32[3,8]{1,0:T(4,128)S(1)}, f32[3,8]{1,0:T(4,128)S(1)}, u32[]{:S(2)}, u32[]{:S(2)}) collective-permute-start(f32[3,8]{1,0:T(4,128)S(1)} %add.328), channel_id=1, source_target_pairs={{0,8},{1,9},{2,10},{3,11},{4,12},{5,13},{6,14},{7,15},{8,0},{9,1},... | collective-permute-start | bytes 296 | tf_op jit(solution)/shard_map/ppermute | solution.py:40
  255.9 3.5 %collective-permute-done.24 = f32[3,8]{1,0:T(4,128)S(1)} collective-permute-done((f32[3,8]{1,0:T(4,128)S(1)}, f32[3,8]{1,0:T(4,128)S(1)}, u32[]{:S(2)}, u32[]{:S(2)}) %collective-permute-start.24) | collective-permute-done | bytes 128 | tf_op jit(solution)/shard_map/ppermute | solution.py:40
  259.4 7.7 %collective-permute-start.25 = (f32[3,8]{1,0:T(4,128)S(1)}, f32[3,8]{1,0:T(4,128)S(1)}, u32[]{:S(2)}, u32[]{:S(2)}) collective-permute-start(f32[3,8]{1,0:T(4,128)S(1)} %add.329), channel_id=1, source_target_pairs={{0,16},{1,17},{2,18},{3,19},{4,20},{5,21},{6,22},{7,23},{8,24},{9,... | collective-permute-start | bytes 296 | tf_op jit(solution)/shard_map/ppermute | solution.py:40
  267.1 6.5 %collective-permute-done.25 = f32[3,8]{1,0:T(4,128)S(1)} collective-permute-done((f32[3,8]{1,0:T(4,128)S(1)}, f32[3,8]{1,0:T(4,128)S(1)}, u32[]{:S(2)}, u32[]{:S(2)}) %collective-permute-start.25) | collective-permute-done | bytes 128 | tf_op jit(solution)/shard_map/ppermute | solution.py:40
  (177 shorter events, 98.4 us)
Async XLA Ops:
  5.3 15.9 %copy-start.14 = (s32[128]{0:T(128)S(1)}, s32[128]{0:T(128)}, u32[]{:S(2)}) copy-start(s32[128]{0:T(128)} %param.6) | copy-start | bytes 1540
  5.3 16.5 %copy-start.15 = (s32[4]{0:T(128)S(1)}, s32[4]{0:T(128)}, u32[]{:S(2)}) copy-start(s32[4]{0:T(128)} %param.7) | copy-start | bytes 52
  11.2 16.8 %all-to-all-start = ((f32[16,1,5120]{2,1,0:T(1,128)}), f32[16,1,5120]{2,1,0:T(1,128)S(1)}, u32[]{:S(2)}, u32[]{:S(2)}) async-start(f32[16,1,5120]{2,1,0:T(1,128)} %reshape.186), calls=%async_computation | async-start | bytes 655360 | tf_op jit(solution)/shard_map/all_to_all | solution.py:129
  19.5 60.3 %collective-permute-start = (f32[8,10,1,256]{3,0,2,1:T(8,128)}, f32[8,10,1,256]{3,0,2,1:T(8,128)}, u32[]{:S(2)}, u32[]{:S(2)}) collective-permute-start(f32[8,10,1,256]{3,0,2,1:T(8,128)} %get-tuple-element.54), channel_id=1, source_target_pairs={{0,1},{1,2},{2,3},{3,4},{4,5},{5,6},{6,7},{7,8},{8,9},{9,10},{10,1... | collective-permute-start | bytes 245768 | tf_op jit(solution)/shard_map/ppermute | solution.py:25
  19.5 60.3 %collective-permute-start.1 = (f32[8,10,1,256]{3,0,2,1:T(8,128)}, f32[8,10,1,256]{3,0,2,1:T(8,128)}, u32[]{:S(2)}, u32[]{:S(2)}) collective-permute-start(f32[8,10,1,256]{3,0,2,1:T(8,128)} %get-tuple-element.55), channel_id=1, source_target_pairs={{1,0},{2,1},{3,2},{4,3},{5,4},{6,5},{7,6},{8,7},{9,8},{10,9},{11,1... | collective-permute-start | bytes 245768 | tf_op jit(solution)/shard_map/ppermute | solution.py:27
  50.9 14.2 %all-to-all-start.1 = ((f32[16,1,5120]{2,1,0:T(1,128)}), f32[16,1,5120]{2,1,0:T(1,128)S(1)}, u32[]{:S(2)}, u32[]{:S(2)}) async-start(f32[16,1,5120]{2,1,0:T(1,128)} %reshape.188), calls=%async_computation.1 | async-start | bytes 655360 | tf_op jit(solution)/shard_map/all_to_all | solution.py:135
  81.4 3.9 %collective-permute-start.2 = (f32[8,10,1,256]{3,0,2,1:T(8,128)S(1)}, f32[8,10,1,256]{3,0,2,1:T(8,128)S(1)}, u32[]{:S(2)}, u32[]{:S(2)}) collective-permute-start(f32[8,10,1,256]{3,0,2,1:T(8,128)S(1)} %get-tuple-element.50), channel_id=1, source_target_pairs={{0,1},{1,2},{2,3},{3,4},{4,5},{5,6},{6,7},{7,8},{8,9},{9,10},{10,1... | collective-permute-start | bytes 245768 | tf_op jit(solution)/shard_map/ppermute | solution.py:25
  81.4 3.9 %collective-permute-start.3 = (f32[8,10,1,256]{3,0,2,1:T(8,128)S(1)}, f32[8,10,1,256]{3,0,2,1:T(8,128)S(1)}, u32[]{:S(2)}, u32[]{:S(2)}) collective-permute-start(f32[8,10,1,256]{3,0,2,1:T(8,128)S(1)} %get-tuple-element.51), channel_id=1, source_target_pairs={{1,0},{2,1},{3,2},{4,3},{5,4},{6,5},{7,6},{8,7},{9,8},{10,9},{11,1... | collective-permute-start | bytes 245768 | tf_op jit(solution)/shard_map/ppermute | solution.py:27
  85.7 5.3 %collective-permute-start.4 = (f32[8,10,1,256]{3,0,2,1:T(8,128)S(1)}, f32[8,10,1,256]{3,0,2,1:T(8,128)S(1)}, u32[]{:S(2)}, u32[]{:S(2)}) collective-permute-start(f32[8,10,1,256]{3,0,2,1:T(8,128)S(1)} %get-tuple-element.48), channel_id=1, source_target_pairs={{0,1},{1,2},{2,3},{3,4},{4,5},{5,6},{6,7},{7,8},{8,9},{9,10},{10,1... | collective-permute-start | bytes 245768 | tf_op jit(solution)/shard_map/ppermute | solution.py:25
  87.8 3.2 %collective-permute-start.5 = (f32[8,10,1,256]{3,0,2,1:T(8,128)S(1)}, f32[8,10,1,256]{3,0,2,1:T(8,128)S(1)}, u32[]{:S(2)}, u32[]{:S(2)}) collective-permute-start(f32[8,10,1,256]{3,0,2,1:T(8,128)S(1)} %get-tuple-element.49), channel_id=1, source_target_pairs={{1,0},{2,1},{3,2},{4,3},{5,4},{6,5},{7,6},{8,7},{9,8},{10,9},{11,1... | collective-permute-start | bytes 245768 | tf_op jit(solution)/shard_map/ppermute | solution.py:27
  91.5 5.1 %collective-permute-start.6 = (f32[8,10,1,256]{3,0,2,1:T(8,128)S(1)}, f32[8,10,1,256]{3,0,2,1:T(8,128)S(1)}, u32[]{:S(2)}, u32[]{:S(2)}) collective-permute-start(f32[8,10,1,256]{3,0,2,1:T(8,128)S(1)} %get-tuple-element.46), channel_id=1, source_target_pairs={{0,1},{1,2},{2,3},{3,4},{4,5},{5,6},{6,7},{7,8},{8,9},{9,10},{10,1... | collective-permute-start | bytes 245768 | tf_op jit(solution)/shard_map/ppermute | solution.py:25
  93.2 3.4 %collective-permute-start.7 = (f32[8,10,1,256]{3,0,2,1:T(8,128)S(1)}, f32[8,10,1,256]{3,0,2,1:T(8,128)S(1)}, u32[]{:S(2)}, u32[]{:S(2)}) collective-permute-start(f32[8,10,1,256]{3,0,2,1:T(8,128)S(1)} %get-tuple-element.47), channel_id=1, source_target_pairs={{1,0},{2,1},{3,2},{4,3},{5,4},{6,5},{7,6},{8,7},{9,8},{10,9},{11,1... | collective-permute-start | bytes 245768 | tf_op jit(solution)/shard_map/ppermute | solution.py:27
  97.2 5.8 %collective-permute-start.8 = (f32[3,8]{1,0:T(4,128)S(1)}, f32[3,8]{1,0:T(4,128)S(1)}, u32[]{:S(2)}, u32[]{:S(2)}) collective-permute-start(f32[3,8]{1,0:T(4,128)S(1)} %pad_maximum_fusion.34), channel_id=1, source_target_pairs={{0,1},{1,0},{2,3},{3,2},{4,5},{5,4},{6,7},{7,6},{8,9},{9,8},{10,11... | collective-permute-start | bytes 296 | tf_op jit(solution)/shard_map/ppermute | solution.py:40
  103.1 7.7 %collective-permute-start.9 = (f32[3,8]{1,0:T(4,128)S(1)}, f32[3,8]{1,0:T(4,128)S(1)}, u32[]{:S(2)}, u32[]{:S(2)}) collective-permute-start(f32[3,8]{1,0:T(4,128)S(1)} %fusion.87), channel_id=1, source_target_pairs={{0,2},{1,3},{2,0},{3,1},{4,6},{5,7},{6,4},{7,5},{8,10},{9,11},{10,... | collective-permute-start | bytes 296 | tf_op jit(solution)/shard_map/ppermute | solution.py:40
  110.8 6.4 %collective-permute-start.10 = (f32[3,8]{1,0:T(4,128)S(1)}, f32[3,8]{1,0:T(4,128)S(1)}, u32[]{:S(2)}, u32[]{:S(2)}) collective-permute-start(f32[3,8]{1,0:T(4,128)S(1)} %fusion.101), channel_id=1, source_target_pairs={{0,4},{1,5},{2,6},{3,7},{4,0},{5,1},{6,2},{7,3},{8,12},{9,13},{10,... | collective-permute-start | bytes 296 | tf_op jit(solution)/shard_map/ppermute | solution.py:40
  117.1 10.4 %collective-permute-start.11 = (f32[3,8]{1,0:T(4,128)S(1)}, f32[3,8]{1,0:T(4,128)S(1)}, u32[]{:S(2)}, u32[]{:S(2)}) collective-permute-start(f32[3,8]{1,0:T(4,128)S(1)} %add.300), channel_id=1, source_target_pairs={{0,8},{1,9},{2,10},{3,11},{4,12},{5,13},{6,14},{7,15},{8,0},{9,1},... | collective-permute-start | bytes 296 | tf_op jit(solution)/shard_map/ppermute | solution.py:40
  127.5 14.2 %collective-permute-start.12 = (f32[3,8]{1,0:T(4,128)S(1)}, f32[3,8]{1,0:T(4,128)S(1)}, u32[]{:S(2)}, u32[]{:S(2)}) collective-permute-start(f32[3,8]{1,0:T(4,128)S(1)} %add.301), channel_id=1, source_target_pairs={{0,16},{1,17},{2,18},{3,19},{4,20},{5,21},{6,22},{7,23},{8,24},{9,... | collective-permute-start | bytes 296 | tf_op jit(solution)/shard_map/ppermute | solution.py:40
  152.2 12.7 %all-to-all-start.2 = ((f32[16,1,5120]{2,1,0:T(1,128)}), f32[16,1,5120]{2,1,0:T(1,128)S(1)}, u32[]{:S(2)}, u32[]{:S(2)}) async-start(f32[16,1,5120]{2,1,0:T(1,128)} %reshape.190), calls=%async_computation.2 | async-start | bytes 655360 | tf_op jit(solution)/shard_map/all_to_all | solution.py:129
  156.7 58.1 %collective-permute-start.13 = (f32[8,10,1,256]{3,0,2,1:T(8,128)}, f32[8,10,1,256]{3,0,2,1:T(8,128)}, u32[]{:S(2)}, u32[]{:S(2)}) collective-permute-start(f32[8,10,1,256]{3,0,2,1:T(8,128)} %get-tuple-element.44), channel_id=1, source_target_pairs={{0,1},{1,2},{2,3},{3,4},{4,5},{5,6},{6,7},{7,8},{8,9},{9,10},{10,1... | collective-permute-start | bytes 245768 | tf_op jit(solution)/shard_map/ppermute | solution.py:25
  156.7 58.1 %collective-permute-start.14 = (f32[8,10,1,256]{3,0,2,1:T(8,128)}, f32[8,10,1,256]{3,0,2,1:T(8,128)}, u32[]{:S(2)}, u32[]{:S(2)}) collective-permute-start(f32[8,10,1,256]{3,0,2,1:T(8,128)} %get-tuple-element.45), channel_id=1, source_target_pairs={{1,0},{2,1},{3,2},{4,3},{5,4},{6,5},{7,6},{8,7},{9,8},{10,9},{11,1... | collective-permute-start | bytes 245768 | tf_op jit(solution)/shard_map/ppermute | solution.py:27
  187.3 12.8 %all-to-all-start.3 = ((f32[16,1,5120]{2,1,0:T(1,128)}), f32[16,1,5120]{2,1,0:T(1,128)S(1)}, u32[]{:S(2)}, u32[]{:S(2)}) async-start(f32[16,1,5120]{2,1,0:T(1,128)} %reshape.192), calls=%async_computation.3 | async-start | bytes 655360 | tf_op jit(solution)/shard_map/all_to_all | solution.py:135
  216.3 3.9 %collective-permute-start.15 = (f32[8,10,1,256]{3,0,2,1:T(8,128)S(1)}, f32[8,10,1,256]{3,0,2,1:T(8,128)S(1)}, u32[]{:S(2)}, u32[]{:S(2)}) collective-permute-start(f32[8,10,1,256]{3,0,2,1:T(8,128)S(1)} %get-tuple-element.40), channel_id=1, source_target_pairs={{0,1},{1,2},{2,3},{3,4},{4,5},{5,6},{6,7},{7,8},{8,9},{9,10},{10,1... | collective-permute-start | bytes 245768 | tf_op jit(solution)/shard_map/ppermute | solution.py:25
  216.3 3.9 %collective-permute-start.16 = (f32[8,10,1,256]{3,0,2,1:T(8,128)S(1)}, f32[8,10,1,256]{3,0,2,1:T(8,128)S(1)}, u32[]{:S(2)}, u32[]{:S(2)}) collective-permute-start(f32[8,10,1,256]{3,0,2,1:T(8,128)S(1)} %get-tuple-element.41), channel_id=1, source_target_pairs={{1,0},{2,1},{3,2},{4,3},{5,4},{6,5},{7,6},{8,7},{9,8},{10,9},{11,1... | collective-permute-start | bytes 245768 | tf_op jit(solution)/shard_map/ppermute | solution.py:27
  220.6 4.1 %collective-permute-start.17 = (f32[8,10,1,256]{3,0,2,1:T(8,128)S(1)}, f32[8,10,1,256]{3,0,2,1:T(8,128)S(1)}, u32[]{:S(2)}, u32[]{:S(2)}) collective-permute-start(f32[8,10,1,256]{3,0,2,1:T(8,128)S(1)} %get-tuple-element.38), channel_id=1, source_target_pairs={{0,1},{1,2},{2,3},{3,4},{4,5},{5,6},{6,7},{7,8},{8,9},{9,10},{10,1... | collective-permute-start | bytes 245768 | tf_op jit(solution)/shard_map/ppermute | solution.py:25
  222.2 2.5 collective-permute-start.18
  225.2 3.9 %collective-permute-start.19 = (f32[8,10,1,256]{3,0,2,1:T(8,128)S(1)}, f32[8,10,1,256]{3,0,2,1:T(8,128)S(1)}, u32[]{:S(2)}, u32[]{:S(2)}) collective-permute-start(f32[8,10,1,256]{3,0,2,1:T(8,128)S(1)} %get-tuple-element.36), channel_id=1, source_target_pairs={{0,1},{1,2},{2,3},{3,4},{4,5},{5,6},{6,7},{7,8},{8,9},{9,10},{10,1... | collective-permute-start | bytes 245768 | tf_op jit(solution)/shard_map/ppermute | solution.py:25
  227.0 2.1 collective-permute-start.20
  229.6 6.5 %collective-permute-start.21 = (f32[3,8]{1,0:T(4,128)S(1)}, f32[3,8]{1,0:T(4,128)S(1)}, u32[]{:S(2)}, u32[]{:S(2)}) collective-permute-start(f32[3,8]{1,0:T(4,128)S(1)} %pad_maximum_fusion.33), channel_id=1, source_target_pairs={{0,1},{1,0},{2,3},{3,2},{4,5},{5,4},{6,7},{7,6},{8,9},{9,8},{10,11... | collective-permute-start | bytes 296 | tf_op jit(solution)/shard_map/ppermute | solution.py:40
  236.1 5.5 %collective-permute-start.22 = (f32[3,8]{1,0:T(4,128)S(1)}, f32[3,8]{1,0:T(4,128)S(1)}, u32[]{:S(2)}, u32[]{:S(2)}) collective-permute-start(f32[3,8]{1,0:T(4,128)S(1)} %fusion.88), channel_id=1, source_target_pairs={{0,2},{1,3},{2,0},{3,1},{4,6},{5,7},{6,4},{7,5},{8,10},{9,11},{10,... | collective-permute-start | bytes 296 | tf_op jit(solution)/shard_map/ppermute | solution.py:40
  241.6 8.3 %collective-permute-start.23 = (f32[3,8]{1,0:T(4,128)S(1)}, f32[3,8]{1,0:T(4,128)S(1)}, u32[]{:S(2)}, u32[]{:S(2)}) collective-permute-start(f32[3,8]{1,0:T(4,128)S(1)} %fusion.100), channel_id=1, source_target_pairs={{0,4},{1,5},{2,6},{3,7},{4,0},{5,1},{6,2},{7,3},{8,12},{9,13},{10,... | collective-permute-start | bytes 296 | tf_op jit(solution)/shard_map/ppermute | solution.py:40
  250.0 9.4 %collective-permute-start.24 = (f32[3,8]{1,0:T(4,128)S(1)}, f32[3,8]{1,0:T(4,128)S(1)}, u32[]{:S(2)}, u32[]{:S(2)}) collective-permute-start(f32[3,8]{1,0:T(4,128)S(1)} %add.328), channel_id=1, source_target_pairs={{0,8},{1,9},{2,10},{3,11},{4,12},{5,13},{6,14},{7,15},{8,0},{9,1},... | collective-permute-start | bytes 296 | tf_op jit(solution)/shard_map/ppermute | solution.py:40
  259.4 14.2 %collective-permute-start.25 = (f32[3,8]{1,0:T(4,128)S(1)}, f32[3,8]{1,0:T(4,128)S(1)}, u32[]{:S(2)}, u32[]{:S(2)}) collective-permute-start(f32[3,8]{1,0:T(4,128)S(1)} %add.329), channel_id=1, source_target_pairs={{0,16},{1,17},{2,18},{3,19},{4,20},{5,21},{6,22},{7,23},{8,24},{9,... | collective-permute-start | bytes 296 | tf_op jit(solution)/shard_map/ppermute | solution.py:40
  (14 other events, 61.4 us)

commit v2 on v0

--- a/solution.py
+++ b/solution.py
@@ -106,6 +106,39 @@
     return jnp.concatenate([new_real, new_imag], axis=1)
 
 
+def tile_sum(values, axis):
+    count = lax.axis_size(axis)
+    spread = jnp.broadcast_to(values[None], (count,) + values.shape)
+    return lax.all_to_all(spread, axis, 0, 0, tiled=True).sum(axis=0)
+
+
+def spectral_slabs(field, forward, backward):
+    harms, chans, rows, depth = field.shape
+    groups = lax.axis_size("harm")
+    width = depth // groups
+    var_count = chans // 2
+    cols = field.reshape(harms * chans * rows, depth).T.reshape(groups, width, harms * chans * rows)
+    slabs = lax.all_to_all(cols, "harm", 0, 0, tiled=True)
+    slabs = slabs.reshape(groups, width, harms, 2, var_count, rows)
+    samples = jnp.einsum(
+        "mshp,szhpvy->mvyz",
+        forward.reshape(forward.shape[0], groups, harms, 2),
+        slabs,
+        precision=lax.Precision.HIGHEST,
+        preferred_element_type=jnp.float32,
+    )
+    product = jnp.roll(samples, -1, axis=1) * jnp.roll(samples, -2, axis=1)
+    folded = jnp.einsum(
+        "shpm,mvyz->szhpvy",
+        backward.reshape(groups, harms, 2, backward.shape[1]),
+        product,
+        precision=lax.Precision.HIGHEST,
+        preferred_element_type=jnp.float32,
+    )
+    back = lax.all_to_all(folded.reshape(groups, width, harms * chans * rows), "harm", 0, 0, tiled=True)
+    return back.reshape(depth, harms * chans * rows).T.reshape(harms, chans, rows, depth)
+
+
 def shards(q_old, base_rate, freq_table, wall_flags):
     forward, backward = build_tables(freq_table)
     frequency_all = freq_table.astype(jnp.float32) * (frequency_scale / freq_table.shape[0])
@@ -115,13 +148,7 @@
     keep_mask = (1 - wall_flags).astype(jnp.float32)[None, None, :, None]
     field = q_old
     for outer_step in range(ITERS):
-        slab_block = lax.all_to_all(field, "harm", split_axis=3, concat_axis=0, tiled=True)
-        harm_count, chan_count, row_count, depth = slab_block.shape
-        forced = spectral_forcing(
-            slab_block.reshape(harm_count, chan_count, row_count * depth), forward, backward
-        )
-        forced = forced.reshape(harm_count, chan_count, row_count, depth)
-        forcing = lax.all_to_all(forced, "harm", split_axis=0, concat_axis=3, tiled=True)
+        forcing = spectral_slabs(field, forward, backward)
         source = marching * q_old + forcing_gain * forcing
         iterate = field
         for sweep_step in range(SWEEPS):
@@ -131,7 +158,7 @@
                 iterate, iterate[..., :1] * keep_mask, jnp.zeros_like(iterate[..., :1])
             )
             iterate = relax(source, base_rate, frequency, beside)
-        totals = lax.psum(correction_terms(iterate, q_old), "tile")
+        totals = tile_sum(jnp.stack(correction_terms(iterate, q_old)), "tile")
         field = apply_correction(iterate, q_old, totals)
     return field
 

time: 297 us -> 187 us (0.63); the launches traced: 292 us -> 186 us
  blocking collectives: 98.7 us -> 27.1 us
  local copies, waits for them, and re-layouts: 86 us -> 24.8 us
  waiting for transfers between devices: 24.7 us -> 45.6 us
  matrix products: 3.53 us -> 13.9 us
  other arithmetic: 20.4 us -> 14.8 us
    psum x2 -> x0, blocking collectives: 98.7 us -> none  [shards(): totals = lax.psum(correction_terms(iterate, q_old), 'tile')]
    unnamed x42 -> x22, local copies, waits for them, and re-layouts: 39.7 us -> 0.76 us
    all_to_all x0 -> x1, blocking collectives: none -> 27.1 us  [tile_sum(): return lax.all_to_all(spread, axis, 0, 0, tiled=True).sum(axis=0)]
    all_to_all x4 -> x5, waiting for transfers between devices: 18.2 us -> 34.2 us  [the longest x2 15.5 us: spectral_slabs(): lax.all_to_all(folded.reshape(groups, width, harms * chans * rows), 'harm...]
    mul x6 -> x4, local copies, waits for them, and re-layouts: 12.8 us -> 0.48 us  [shards(): source = marching * q_old + forcing_gain * forcing]
    all_to_all x5 -> x1, local copies, waits for them, and re-layouts: 14 us -> 2.49 us  [spectral_slabs(): slabs = lax.all_to_all(cols, 'harm', 0, 0, tiled=True)]
    reshape x0 -> x6, local copies, waits for them, and re-layouts: none -> 11 us  [the longest x2 7.15 us: spectral_slabs(): folded.reshape(groups, width, harms * chans * rows)]
    dot_general x4, matrix products: 3.53 us -> 13.9 us  [the longest x2 9.39 us: spectral_slabs(): jnp.einsum('mshp,szhpvy->mvyz', forward.reshape(forward.shape[0], groups,...]
  transfers between devices with their start and end apart: 20 -> 21, of which waited for: 16 -> 16; matrix products, arithmetic and copies ran while one was open for 28% -> 21% of each run, Pallas kernels for 0% -> 0%
where the time goes in v2:
time: 187 us; the launch traced here: 186 us
  starting transfers between devices  59 us (32%)
  waiting for transfers between devices  45.6 us (24%)
  blocking collectives  27.1 us (14%)
  local copies, waits for them, and re-layouts  24.8 us (13%)
  other arithmetic  14.8 us (8%)
  matrix products  13.9 us (7%)
    all_to_all x1, blocking collectives, tile_sum(): return lax.all_to_all(spread, axis, 0, 0, tiled=True).sum(axis=0)  27.1 us
    ppermute x8, starting transfers between devices, extended(): lax.ppermute(head, axis, [((i + 1) % count, i) for i in range(count)])  16 us
    all_to_all x2, waiting for transfers between devices, spectral_slabs(): lax.all_to_all(folded.reshape(groups, width, harms * chans * rows), 'harm...  15.5 us
    all_to_all x1, waiting for transfers between devices, tile_sum(): return lax.all_to_all(spread, axis, 0, 0, tiled=True).sum(axis=0)  13 us
    all_to_all x2, starting transfers between devices, spectral_slabs(): slabs = lax.all_to_all(cols, 'harm', 0, 0, tiled=True)  12 us
    ppermute x8, starting transfers between devices, extended(): lax.ppermute(tail, axis, [(i, (i + 1) % count) for i in range(count)])  11.7 us
    all_to_all x2, starting transfers between devices, spectral_slabs(): lax.all_to_all(folded.reshape(groups, width, harms * chans * rows), 'harm...  10.8 us
    dot_general x2, matrix products, spectral_slabs(): jnp.einsum('mshp,szhpvy->mvyz', forward.reshape(forward.shape[0], groups,...  9.39 us
  transfers between devices with their start and end apart: 21, of which 16 were waited for; matrix products, arithmetic and copies ran while one was open for 21% of the time, Pallas kernels for 0%

profile of v2, /device:TPU:1, one launch (start us, length us, event | category | flops | bytes accessed | tf_op | source)
XLA Modules:
  0.0 186.0 jit_solution(16434640090757757276)
XLA Ops:
  2.1 7.6 %all-to-all-start = ((f32[16,16,320]{2,1,0:T(8,128)}), f32[16,16,320]{2,1,0:T(8,128)}, u32[]{:S(2)}, u32[]{:S(2)}) async-start(f32[16,16,320]{2,1,0:T(8,128)} %bitcast.3), calls=%async_computation | async-start | bytes 786432 | tf_op jit(solution)/shard_map/all_to_all | solution.py:121
  9.7 1.9 %fusion.116 = (f32[8,10,1,256]{3,2,1,0:T(1,128)}, f32[8,10,1,256]{3,2,1,0:T(1,128)}) fusion(f32[8,10,4,256]{3,2,1,0:T(4,128)} %param.4), kind=kLoop, calls=%fused_computation.265 | loop fusion | bytes 327680 | tf_op jit(solution)/shard_map/slice | solution.py:22
  11.6 2.5 %collective-permute-start = (f32[8,10,1,256]{3,2,1,0:T(1,128)}, f32[8,10,1,256]{3,2,1,0:T(1,128)}, u32[]{:S(2)}, u32[]{:S(2)}) collective-permute-start(f32[8,10,1,256]{3,2,1,0:T(1,128)} %get-tuple-element.54), channel_id=1, source_target_pairs={{0,1},{1,2},{2,3},{3,4},{4,5},{5,6},{6,7},{7,8},{8,9},{9,10},{10,1... | collective-permute-start | bytes 245768 | tf_op jit(solution)/shard_map/ppermute | solution.py:25
  19.1 2.5 %copy.85 = f32[16,16,320]{1,0,2:T(8,128)S(1)} copy(f32[16,16,320]{2,1,0:T(8,128)} %all-to-all-done) | data formatting | bytes 655360 | tf_op jit(solution)/shard_map/all_to_all | solution.py:121
  21.6 4.2 %convolution_bitcast_fusion.2 = f32[256,5,4,16]{0,3,2,1:T(8,128)S(1)} fusion(f32[16,16,8,2,5,4]{1,0,5,4,3,2:T(8,128)S(1)} %bitcast.82, f32[256,16,8,1]{0,1,3,2:T(8,128)S(1)} %get-tuple-element.57, f32[256,16,8,1]{0,1,3,2:T(8,128)S(1)} %get-tuple-element.56), kind=kOutput, calls=%fused_computation.2 | convolution fusion | flops 251789312 | bytes 917504 | tf_op jit(solution)/shard_map/mshp,szhpvy->mvyz/dot_general | solution.py:123
  25.9 2.3 %convolution_bitcast_fusion.1 = f32[16,16,8,2,5,4]{0,1,3,2,5,4:T(8,128)S(1)} fusion(f32[256,1,4,16]{0,3,2,1:T(8,128)S(1)} %slice.355, f32[256,4,4,16]{0,3,2,1:T(8,128)S(1)} %slice.354, f32[256,2,4,16]{0,3,2,1:T(8,128)S(1)} %slice.357, f32[256,3,4,16]{0,3,2,1:T(8,128)S(1)} %slice.356, f32[16,8,2,256,1,1]{3,2,1,0,5,4:T(2,128)S(1)} %bitcast.85), kind=kOutput, calls=%fused_computation.1 | convolution fusion | flops 251904000 | bytes 1245184 | tf_op jit(solution)/shard_map/shpm,mvyz->szhpvy/dot_general | solution.py:131
  28.2 2.1 %copy.89 = f32[16,16,8,2,5,4]{1,0,5,4,3,2:T(8,128)} copy(f32[16,16,8,2,5,4]{0,1,3,2,5,4:T(8,128)S(1)} %convolution_bitcast_fusion.1) | data formatting | bytes 655360 | tf_op jit(solution)/shard_map/shpm,mvyz->szhpvy/transpose | solution.py:131
  30.3 3.6 %copy.90 = f32[16,16,320]{2,1,0:T(8,128)} copy(f32[16,16,320]{1,0,2:T(8,128)} %bitcast.83) | data formatting | bytes 655360 | tf_op jit(solution)/shard_map/reshape | solution.py:138
  33.8 7.0 %all-to-all-start.1 = ((f32[16,16,320]{2,1,0:T(8,128)}), f32[16,16,320]{2,1,0:T(8,128)S(1)}, u32[]{:S(2)}, u32[]{:S(2)}) async-start(f32[16,16,320]{2,1,0:T(8,128)} %copy.90), calls=%async_computation.1 | async-start | bytes 786432 | tf_op jit(solution)/shard_map/all_to_all | solution.py:138
  41.1 7.9 %all-to-all-done.1 = f32[16,16,320]{2,1,0:T(8,128)S(1)} async-done(((f32[16,16,320]{2,1,0:T(8,128)}), f32[16,16,320]{2,1,0:T(8,128)S(1)}, u32[]{:S(2)}, u32[]{:S(2)}) %all-to-all-start.1) | async-done | bytes 327712 | tf_op jit(solution)/shard_map/all_to_all | solution.py:138
  49.4 1.5 fusion.45
  51.3 3.5 %collective-permute-start.2 = (f32[8,10,1,256]{3,2,1,0:T(1,128)S(1)}, f32[8,10,1,256]{3,2,1,0:T(1,128)S(1)}, u32[]{:S(2)}, u32[]{:S(2)}) collective-permute-start(f32[8,10,1,256]{3,2,1,0:T(1,128)S(1)} %get-tuple-element.50), channel_id=1, source_target_pairs={{0,1},{1,2},{2,3},{3,4},{4,5},{5,6},{6,7},{7,8},{8,9},{9,10},{10,1... | collective-permute-start | bytes 245768 | tf_op jit(solution)/shard_map/ppermute | solution.py:25
  54.7 4.0 %collective-permute-start.3 = (f32[8,10,1,256]{3,2,1,0:T(1,128)S(1)}, f32[8,10,1,256]{3,2,1,0:T(1,128)S(1)}, u32[]{:S(2)}, u32[]{:S(2)}) collective-permute-start(f32[8,10,1,256]{3,2,1,0:T(1,128)S(1)} %get-tuple-element.51), channel_id=1, source_target_pairs={{1,0},{2,1},{3,2},{4,3},{5,4},{6,5},{7,6},{8,7},{9,8},{10,9},{11,1... | collective-permute-start | bytes 245768 | tf_op jit(solution)/shard_map/ppermute | solution.py:27
  60.7 4.1 %collective-permute-start.5 = (f32[8,10,1,256]{3,2,1,0:T(1,128)S(1)}, f32[8,10,1,256]{3,2,1,0:T(1,128)S(1)}, u32[]{:S(2)}, u32[]{:S(2)}) collective-permute-start(f32[8,10,1,256]{3,2,1,0:T(1,128)S(1)} %get-tuple-element.49), channel_id=1, source_target_pairs={{1,0},{2,1},{3,2},{4,3},{5,4},{6,5},{7,6},{8,7},{9,8},{10,9},{11,1... | collective-permute-start | bytes 245768 | tf_op jit(solution)/shard_map/ppermute | solution.py:27
  66.8 4.1 %collective-permute-start.7 = (f32[8,10,1,256]{3,2,1,0:T(1,128)S(1)}, f32[8,10,1,256]{3,2,1,0:T(1,128)S(1)}, u32[]{:S(2)}, u32[]{:S(2)}) collective-permute-start(f32[8,10,1,256]{3,2,1,0:T(1,128)S(1)} %get-tuple-element.47), channel_id=1, source_target_pairs={{1,0},{2,1},{3,2},{4,3},{5,4},{6,5},{7,6},{8,7},{9,8},{10,9},{11,1... | collective-permute-start | bytes 245768 | tf_op jit(solution)/shard_map/ppermute | solution.py:27
  73.0 27.1 %all_to_all.30 = f32[32,3,8]{2,1,0:T(4,128)S(1)} all-to-all(f32[32,3,8]{2,1,0:T(4,128)S(1)} %broadcast_in_dim.4), channel_id=1, replica_groups=mesh['harm'=16,'tile'=32] {'tile'}, dimensions={0} | all-to-all | bytes 6144 | tf_op jit(solution)/shard_map/all_to_all | solution.py:112
  101.4 4.4 %all-to-all-start.3 = ((f32[16,16,320]{2,1,0:T(8,128)}), f32[16,16,320]{2,1,0:T(8,128)}, u32[]{:S(2)}, u32[]{:S(2)}) async-start(f32[16,16,320]{2,1,0:T(8,128)} %bitcast.25), calls=%async_computation.3 | async-start | bytes 786432 | tf_op jit(solution)/shard_map/all_to_all | solution.py:121
  106.7 1.8 collective-permute-start.8
  108.5 5.7 %all-to-all-done.3 = f32[16,16,320]{2,1,0:T(8,128)} async-done(((f32[16,16,320]{2,1,0:T(8,128)}), f32[16,16,320]{2,1,0:T(8,128)}, u32[]{:S(2)}, u32[]{:S(2)}) %all-to-all-start.3) | async-done | bytes 327712 | tf_op jit(solution)/shard_map/all_to_all | solution.py:121
  114.1 2.5 %copy.115 = f32[16,16,320]{1,0,2:T(8,128)S(1)} copy(f32[16,16,320]{2,1,0:T(8,128)} %all-to-all-done.3) | data formatting | bytes 655360 | tf_op jit(solution)/shard_map/reshape | solution.py:122
  116.6 5.2 %convolution_bitcast_fusion.3 = f32[256,5,4,16]{0,3,2,1:T(8,128)S(1)} fusion(f32[16,16,8,2,5,4]{1,0,5,4,3,2:T(8,128)S(1)} %bitcast.81, f32[256,16,8,1]{0,1,3,2:T(8,128)} %copy-done.6, f32[256,16,8,1]{0,1,3,2:T(8,128)} %copy-done.5), kind=kOutput, calls=%fused_computation.3 | convolution fusion | flops 251789312 | bytes 917504 | tf_op jit(solution)/shard_map/mshp,szhpvy->mvyz/dot_general | solution.py:123
  121.9 2.3 %convolution_bitcast_fusion = f32[16,16,8,2,5,4]{0,1,3,2,5,4:T(8,128)S(1)} fusion(f32[256,1,4,16]{0,3,2,1:T(8,128)S(1)} %slice.391, f32[256,4,4,16]{0,3,2,1:T(8,128)S(1)} %slice.390, f32[256,2,4,16]{0,3,2,1:T(8,128)S(1)} %slice.393, f32[256,3,4,16]{0,3,2,1:T(8,128)S(1)} %slice.392, f32[16,8,2,256,1,1]{3,2,1,0,5,4:T(2,128)S(1)} %bitcast.86), kind=kOutput, calls=%fused_computation | convolution fusion | flops 251904000 | bytes 1245184 | tf_op jit(solution)/shard_map/shpm,mvyz->szhpvy/dot_general | solution.py:131
  124.1 2.1 %copy.97 = f32[16,16,8,2,5,4]{1,0,5,4,3,2:T(8,128)} copy(f32[16,16,8,2,5,4]{0,1,3,2,5,4:T(8,128)S(1)} %convolution_bitcast_fusion) | data formatting | bytes 655360 | tf_op jit(solution)/shard_map/shpm,mvyz->szhpvy/transpose | solution.py:131
  126.2 3.6 %copy.98 = f32[16,16,320]{2,1,0:T(8,128)} copy(f32[16,16,320]{1,0,2:T(8,128)} %bitcast.84) | data formatting | bytes 655360 | tf_op jit(solution)/shard_map/reshape | solution.py:138
  129.8 3.8 %all-to-all-start.4 = ((f32[16,16,320]{2,1,0:T(8,128)}), f32[16,16,320]{2,1,0:T(8,128)S(1)}, u32[]{:S(2)}, u32[]{:S(2)}) async-start(f32[16,16,320]{2,1,0:T(8,128)} %copy.98), calls=%async_computation.4 | async-start | bytes 786432 | tf_op jit(solution)/shard_map/all_to_all | solution.py:138
  134.0 7.6 %all-to-all-done.4 = f32[16,16,320]{2,1,0:T(8,128)S(1)} async-done(((f32[16,16,320]{2,1,0:T(8,128)}), f32[16,16,320]{2,1,0:T(8,128)S(1)}, u32[]{:S(2)}, u32[]{:S(2)}) %all-to-all-start.4) | async-done | bytes 327712 | tf_op jit(solution)/shard_map/all_to_all | solution.py:138
  143.8 3.9 %collective-permute-start.10 = (f32[8,10,1,256]{3,2,1,0:T(1,128)S(1)}, f32[8,10,1,256]{3,2,1,0:T(1,128)S(1)}, u32[]{:S(2)}, u32[]{:S(2)}) collective-permute-start(f32[8,10,1,256]{3,2,1,0:T(1,128)S(1)} %get-tuple-element.40), channel_id=1, source_target_pairs={{0,1},{1,2},{2,3},{3,4},{4,5},{5,6},{6,7},{7,8},{8,9},{9,10},{10,1... | collective-permute-start | bytes 245768 | tf_op jit(solution)/shard_map/ppermute | solution.py:25
  149.2 2.7 %collective-permute-done.11 = f32[8,10,1,256]{3,2,1,0:T(1,128)S(1)} collective-permute-done((f32[8,10,1,256]{3,2,1,0:T(1,128)S(1)}, f32[8,10,1,256]{3,2,1,0:T(1,128)S(1)}, u32[]{:S(2)}, u32[]{:S(2)}) %collective-permute-start.11) | collective-permute-done | bytes 81952 | tf_op jit(solution)/shard_map/ppermute | solution.py:27
  154.5 2.3 %collective-permute-done.13 = f32[8,10,1,256]{3,2,1,0:T(1,128)S(1)} collective-permute-done((f32[8,10,1,256]{3,2,1,0:T(1,128)S(1)}, f32[8,10,1,256]{3,2,1,0:T(1,128)S(1)}, u32[]{:S(2)}, u32[]{:S(2)}) %collective-permute-start.13) | collective-permute-done | bytes 81952 | tf_op jit(solution)/shard_map/ppermute | solution.py:27
  157.9 2.0 %collective-permute-start.15 = (f32[8,10,1,256]{3,2,1,0:T(1,128)S(1)}, f32[8,10,1,256]{3,2,1,0:T(1,128)S(1)}, u32[]{:S(2)}, u32[]{:S(2)}) collective-permute-start(f32[8,10,1,256]{3,2,1,0:T(1,128)S(1)} %get-tuple-element.37), channel_id=1, source_target_pairs={{1,0},{2,1},{3,2},{4,3},{5,4},{6,5},{7,6},{8,7},{9,8},{10,9},{11,1... | collective-permute-start | bytes 245768 | tf_op jit(solution)/shard_map/ppermute | solution.py:27
  163.4 8.5 %all-to-all-start.5 = ((f32[32,3,8]{2,1,0:T(4,128)}), f32[32,3,8]{2,1,0:T(4,128)S(1)}, u32[]{:S(2)}, u32[]{:S(2)}) async-start(f32[32,3,8]{2,1,0:T(4,128)} %broadcast_in_dim.5), calls=%async_computation.5 | async-start | bytes 131072 | tf_op jit(solution)/shard_map/all_to_all | solution.py:112
  171.9 13.0 %all-to-all-done.5 = f32[32,3,8]{2,1,0:T(4,128)S(1)} async-done(((f32[32,3,8]{2,1,0:T(4,128)}), f32[32,3,8]{2,1,0:T(4,128)S(1)}, u32[]{:S(2)}, u32[]{:S(2)}) %all-to-all-start.5) | async-done | bytes 3104 | tf_op jit(solution)/shard_map/all_to_all | solution.py:112
  (125 shorter events, 28.2 us)
Async XLA Ops:
  0.0 18.3 %copy-start = (f32[8,10,4,256]{3,2,1,0:T(4,128)S(1)}, f32[8,10,4,256]{3,2,1,0:T(4,128)}, u32[]{:S(2)}) copy-start(f32[8,10,4,256]{3,2,1,0:T(4,128)} %param.4) | copy-start | bytes 983044
  0.0 17.0 %copy-start.8 = (s32[128]{0:T(128)S(1)}, s32[128]{0:T(128)}, u32[]{:S(2)}) copy-start(s32[128]{0:T(128)} %param.6) | copy-start | bytes 1540
  0.0 17.7 %copy-start.10 = (s32[4]{0:T(128)S(1)}, s32[4]{0:T(128)}, u32[]{:S(2)}) copy-start(s32[4]{0:T(128)} %param.7) | copy-start | bytes 52
  0.0 18.2 %copy-start.1 = (f32[5,4,256]{2,1,0:T(4,128)S(1)}, f32[5,4,256]{2,1,0:T(4,128)}, u32[]{:S(2)}) copy-start(f32[5,4,256]{2,1,0:T(4,128)} %param.5) | copy-start | bytes 61444
  2.1 17.0 %all-to-all-start = ((f32[16,16,320]{2,1,0:T(8,128)}), f32[16,16,320]{2,1,0:T(8,128)}, u32[]{:S(2)}, u32[]{:S(2)}) async-start(f32[16,16,320]{2,1,0:T(8,128)} %bitcast.3), calls=%async_computation | async-start | bytes 786432 | tf_op jit(solution)/shard_map/all_to_all | solution.py:121
  11.6 37.7 %collective-permute-start = (f32[8,10,1,256]{3,2,1,0:T(1,128)}, f32[8,10,1,256]{3,2,1,0:T(1,128)}, u32[]{:S(2)}, u32[]{:S(2)}) collective-permute-start(f32[8,10,1,256]{3,2,1,0:T(1,128)} %get-tuple-element.54), channel_id=1, source_target_pairs={{0,1},{1,2},{2,3},{3,4},{4,5},{5,6},{6,7},{7,8},{8,9},{9,10},{10,1... | collective-permute-start | bytes 245768 | tf_op jit(solution)/shard_map/ppermute | solution.py:25
  14.1 35.3 %collective-permute-start.1 = (f32[8,10,1,256]{3,2,1,0:T(1,128)}, f32[8,10,1,256]{3,2,1,0:T(1,128)}, u32[]{:S(2)}, u32[]{:S(2)}) collective-permute-start(f32[8,10,1,256]{3,2,1,0:T(1,128)} %get-tuple-element.55), channel_id=1, source_target_pairs={{1,0},{2,1},{3,2},{4,3},{5,4},{6,5},{7,6},{8,7},{9,8},{10,9},{11,1... | collective-permute-start | bytes 245768 | tf_op jit(solution)/shard_map/ppermute | solution.py:27
  17.7 3.9 %copy-start.5 = (f32[256,16,8,1]{0,1,3,2:T(8,128)}, f32[256,16,8,1]{0,1,3,2:T(8,128)S(1)}, u32[]{:S(2)}) copy-start(f32[256,16,8,1]{0,1,3,2:T(8,128)S(1)} %get-tuple-element.56) | copy-start | bytes 393220
  17.7 3.9 %copy-start.6 = (f32[256,16,8,1]{0,1,3,2:T(8,128)}, f32[256,16,8,1]{0,1,3,2:T(8,128)S(1)}, u32[]{:S(2)}) copy-start(f32[256,16,8,1]{0,1,3,2:T(8,128)S(1)} %get-tuple-element.57) | copy-start | bytes 393220
  18.3 54.2 %copy-start.3 = (f32[5,4,256]{2,1,0:T(4,128)}, f32[5,4,256]{2,1,0:T(4,128)S(1)}, u32[]{:S(2)}) copy-start(f32[5,4,256]{2,1,0:T(4,128)S(1)} %mul.513) | copy-start | bytes 61444
  33.8 15.5 %copy-start.7 = (f32[8,10,4,1]{3,2,1,0:T(4,128)S(1)}, f32[8,10,4,1]{3,2,1,0:T(4,128)}, u32[]{:S(2)}) copy-start(f32[8,10,4,1]{3,2,1,0:T(4,128)} %slice_multiply_fusion) | copy-start | bytes 3844
  33.8 15.2 %all-to-all-start.1 = ((f32[16,16,320]{2,1,0:T(8,128)}), f32[16,16,320]{2,1,0:T(8,128)S(1)}, u32[]{:S(2)}, u32[]{:S(2)}) async-start(f32[16,16,320]{2,1,0:T(8,128)} %copy.90), calls=%async_computation.1 | async-start | bytes 786432 | tf_op jit(solution)/shard_map/all_to_all | solution.py:138
  51.3 8.2 %collective-permute-start.2 = (f32[8,10,1,256]{3,2,1,0:T(1,128)S(1)}, f32[8,10,1,256]{3,2,1,0:T(1,128)S(1)}, u32[]{:S(2)}, u32[]{:S(2)}) collective-permute-start(f32[8,10,1,256]{3,2,1,0:T(1,128)S(1)} %get-tuple-element.50), channel_id=1, source_target_pairs={{0,1},{1,2},{2,3},{3,4},{4,5},{5,6},{6,7},{7,8},{8,9},{9,10},{10,1... | collective-permute-start | bytes 245768 | tf_op jit(solution)/shard_map/ppermute | solution.py:25
  54.7 4.9 %collective-permute-start.3 = (f32[8,10,1,256]{3,2,1,0:T(1,128)S(1)}, f32[8,10,1,256]{3,2,1,0:T(1,128)S(1)}, u32[]{:S(2)}, u32[]{:S(2)}) collective-permute-start(f32[8,10,1,256]{3,2,1,0:T(1,128)S(1)} %get-tuple-element.51), channel_id=1, source_target_pairs={{1,0},{2,1},{3,2},{4,3},{5,4},{6,5},{7,6},{8,7},{9,8},{10,9},{11,1... | collective-permute-start | bytes 245768 | tf_op jit(solution)/shard_map/ppermute | solution.py:27
  60.7 4.9 %collective-permute-start.4 = (f32[8,10,1,256]{3,2,1,0:T(1,128)S(1)}, f32[8,10,1,256]{3,2,1,0:T(1,128)S(1)}, u32[]{:S(2)}, u32[]{:S(2)}) collective-permute-start(f32[8,10,1,256]{3,2,1,0:T(1,128)S(1)} %get-tuple-element.48), channel_id=1, source_target_pairs={{0,1},{1,2},{2,3},{3,4},{4,5},{5,6},{6,7},{7,8},{8,9},{9,10},{10,1... | collective-permute-start | bytes 245768 | tf_op jit(solution)/shard_map/ppermute | solution.py:25
  60.7 5.1 %collective-permute-start.5 = (f32[8,10,1,256]{3,2,1,0:T(1,128)S(1)}, f32[8,10,1,256]{3,2,1,0:T(1,128)S(1)}, u32[]{:S(2)}, u32[]{:S(2)}) collective-permute-start(f32[8,10,1,256]{3,2,1,0:T(1,128)S(1)} %get-tuple-element.49), channel_id=1, source_target_pairs={{1,0},{2,1},{3,2},{4,3},{5,4},{6,5},{7,6},{8,7},{9,8},{10,9},{11,1... | collective-permute-start | bytes 245768 | tf_op jit(solution)/shard_map/ppermute | solution.py:27
  66.8 4.9 %collective-permute-start.6 = (f32[8,10,1,256]{3,2,1,0:T(1,128)S(1)}, f32[8,10,1,256]{3,2,1,0:T(1,128)S(1)}, u32[]{:S(2)}, u32[]{:S(2)}) collective-permute-start(f32[8,10,1,256]{3,2,1,0:T(1,128)S(1)} %get-tuple-element.46), channel_id=1, source_target_pairs={{0,1},{1,2},{2,3},{3,4},{4,5},{5,6},{6,7},{7,8},{8,9},{9,10},{10,1... | collective-permute-start | bytes 245768 | tf_op jit(solution)/shard_map/ppermute | solution.py:25
  66.8 5.1 %collective-permute-start.7 = (f32[8,10,1,256]{3,2,1,0:T(1,128)S(1)}, f32[8,10,1,256]{3,2,1,0:T(1,128)S(1)}, u32[]{:S(2)}, u32[]{:S(2)}) collective-permute-start(f32[8,10,1,256]{3,2,1,0:T(1,128)S(1)} %get-tuple-element.47), channel_id=1, source_target_pairs={{1,0},{2,1},{3,2},{4,3},{5,4},{6,5},{7,6},{8,7},{9,8},{10,9},{11,1... | collective-permute-start | bytes 245768 | tf_op jit(solution)/shard_map/ppermute | solution.py:27
  101.4 12.7 %all-to-all-start.3 = ((f32[16,16,320]{2,1,0:T(8,128)}), f32[16,16,320]{2,1,0:T(8,128)}, u32[]{:S(2)}, u32[]{:S(2)}) async-start(f32[16,16,320]{2,1,0:T(8,128)} %bitcast.25), calls=%async_computation.3 | async-start | bytes 786432 | tf_op jit(solution)/shard_map/all_to_all | solution.py:121
  106.7 35.2 %collective-permute-start.8 = (f32[8,10,1,256]{3,2,1,0:T(1,128)}, f32[8,10,1,256]{3,2,1,0:T(1,128)}, u32[]{:S(2)}, u32[]{:S(2)}) collective-permute-start(f32[8,10,1,256]{3,2,1,0:T(1,128)} %get-tuple-element.44), channel_id=1, source_target_pairs={{0,1},{1,2},{2,3},{3,4},{4,5},{5,6},{6,7},{7,8},{8,9},{9,10},{10,1... | collective-permute-start | bytes 245768 | tf_op jit(solution)/shard_map/ppermute | solution.py:25
  108.4 33.4 %collective-permute-start.9 = (f32[8,10,1,256]{3,2,1,0:T(1,128)}, f32[8,10,1,256]{3,2,1,0:T(1,128)}, u32[]{:S(2)}, u32[]{:S(2)}) collective-permute-start(f32[8,10,1,256]{3,2,1,0:T(1,128)} %get-tuple-element.45), channel_id=1, source_target_pairs={{1,0},{2,1},{3,2},{4,3},{5,4},{6,5},{7,6},{8,7},{9,8},{10,9},{11,1... | collective-permute-start | bytes 245768 | tf_op jit(solution)/shard_map/ppermute | solution.py:27
  129.8 11.8 %all-to-all-start.4 = ((f32[16,16,320]{2,1,0:T(8,128)}), f32[16,16,320]{2,1,0:T(8,128)S(1)}, u32[]{:S(2)}, u32[]{:S(2)}) async-start(f32[16,16,320]{2,1,0:T(8,128)} %copy.98), calls=%async_computation.4 | async-start | bytes 786432 | tf_op jit(solution)/shard_map/all_to_all | solution.py:138
  133.9 9.5 %copy-start.2 = (f32[5,4,256]{2,1,0:T(4,128)S(1)}, f32[5,4,256]{2,1,0:T(4,128)}, u32[]{:S(2)}) copy-start(f32[5,4,256]{2,1,0:T(4,128)} %param.5) | copy-start | bytes 61444
  133.9 9.5 %copy-start.4 = (f32[5,4,256]{2,1,0:T(4,128)S(1)}, f32[5,4,256]{2,1,0:T(4,128)}, u32[]{:S(2)}) copy-start(f32[5,4,256]{2,1,0:T(4,128)} %copy-done.3) | copy-start | bytes 61444
  143.8 5.4 %collective-permute-start.10 = (f32[8,10,1,256]{3,2,1,0:T(1,128)S(1)}, f32[8,10,1,256]{3,2,1,0:T(1,128)S(1)}, u32[]{:S(2)}, u32[]{:S(2)}) collective-permute-start(f32[8,10,1,256]{3,2,1,0:T(1,128)S(1)} %get-tuple-element.40), channel_id=1, source_target_pairs={{0,1},{1,2},{2,3},{3,4},{4,5},{5,6},{6,7},{7,8},{8,9},{9,10},{10,1... | collective-permute-start | bytes 245768 | tf_op jit(solution)/shard_map/ppermute | solution.py:25
  147.7 4.2 %collective-permute-start.11 = (f32[8,10,1,256]{3,2,1,0:T(1,128)S(1)}, f32[8,10,1,256]{3,2,1,0:T(1,128)S(1)}, u32[]{:S(2)}, u32[]{:S(2)}) collective-permute-start(f32[8,10,1,256]{3,2,1,0:T(1,128)S(1)} %get-tuple-element.41), channel_id=1, source_target_pairs={{1,0},{2,1},{3,2},{4,3},{5,4},{6,5},{7,6},{8,7},{9,8},{10,9},{11,1... | collective-permute-start | bytes 245768 | tf_op jit(solution)/shard_map/ppermute | solution.py:27
  152.9 1.6 collective-permute-start.12
  152.9 3.9 %collective-permute-start.13 = (f32[8,10,1,256]{3,2,1,0:T(1,128)S(1)}, f32[8,10,1,256]{3,2,1,0:T(1,128)S(1)}, u32[]{:S(2)}, u32[]{:S(2)}) collective-permute-start(f32[8,10,1,256]{3,2,1,0:T(1,128)S(1)} %get-tuple-element.39), channel_id=1, source_target_pairs={{1,0},{2,1},{3,2},{4,3},{5,4},{6,5},{7,6},{8,7},{9,8},{10,9},{11,1... | collective-permute-start | bytes 245768 | tf_op jit(solution)/shard_map/ppermute | solution.py:27
  157.8 2.8 %collective-permute-start.14 = (f32[8,10,1,256]{3,2,1,0:T(1,128)S(1)}, f32[8,10,1,256]{3,2,1,0:T(1,128)S(1)}, u32[]{:S(2)}, u32[]{:S(2)}) collective-permute-start(f32[8,10,1,256]{3,2,1,0:T(1,128)S(1)} %get-tuple-element.36), channel_id=1, source_target_pairs={{0,1},{1,2},{2,3},{3,4},{4,5},{5,6},{6,7},{7,8},{8,9},{9,10},{10,1... | collective-permute-start | bytes 245768 | tf_op jit(solution)/shard_map/ppermute | solution.py:25
  157.9 3.9 %collective-permute-start.15 = (f32[8,10,1,256]{3,2,1,0:T(1,128)S(1)}, f32[8,10,1,256]{3,2,1,0:T(1,128)S(1)}, u32[]{:S(2)}, u32[]{:S(2)}) collective-permute-start(f32[8,10,1,256]{3,2,1,0:T(1,128)S(1)} %get-tuple-element.37), channel_id=1, source_target_pairs={{1,0},{2,1},{3,2},{4,3},{5,4},{6,5},{7,6},{8,7},{9,8},{10,9},{11,1... | collective-permute-start | bytes 245768 | tf_op jit(solution)/shard_map/ppermute | solution.py:27
  163.4 21.6 %all-to-all-start.5 = ((f32[32,3,8]{2,1,0:T(4,128)}), f32[32,3,8]{2,1,0:T(4,128)S(1)}, u32[]{:S(2)}, u32[]{:S(2)}) async-start(f32[32,3,8]{2,1,0:T(4,128)} %broadcast_in_dim.5), calls=%async_computation.5 | async-start | bytes 131072 | tf_op jit(solution)/shard_map/all_to_all | solution.py:112
  185.2 0.7 copy-start.9

commit v3 on v2

--- a/solution.py
+++ b/solution.py
@@ -139,27 +139,70 @@
     return back.reshape(depth, harms * chans * rows).T.reshape(harms, chans, rows, depth)
 
 
+def span_halo(block, width):
+    count = lax.axis_size("tile")
+    rows = block.shape[-2]
+    from_left = lax.ppermute(
+        block[..., rows - width :, :], "tile", [(i, (i + 1) % count) for i in range(count)]
+    )
+    from_right = lax.ppermute(block[..., :width, :], "tile", [((i + 1) % count, i) for i in range(count)])
+    return from_left, from_right
+
+
+def with_halo(block, halo):
+    return jnp.concatenate([halo[0], block, halo[1]], axis=-2)
+
+
+def sweep(iterate, source, base_rate, keep, frequency):
+    center = iterate[:, :, 1:-1]
+    beside = iterate[:, :, :-2] + iterate[:, :, 2:]
+    beside = beside + normal_sum(center, center[..., :1] * keep, jnp.zeros_like(center[..., :1]))
+    return relax(source, base_rate, frequency, beside)
+
+
 def shards(q_old, base_rate, freq_table, wall_flags):
     forward, backward = build_tables(freq_table)
     frequency_all = freq_table.astype(jnp.float32) * (frequency_scale / freq_table.shape[0])
     harm_rank = lax.axis_index("harm")
     local_harms = q_old.shape[0]
     frequency = lax.dynamic_slice_in_dim(frequency_all, harm_rank * local_harms, local_harms)
-    keep_mask = (1 - wall_flags).astype(jnp.float32)[None, None, :, None]
+    rows = q_old.shape[2]
+    assert rows >= SWEEPS
+    keep = (1 - wall_flags).astype(jnp.float32)[:, None]
+    keep_ext = with_halo(keep, span_halo(keep, SWEEPS))[None, None]
+    base_ext = with_halo(base_rate, span_halo(base_rate, SWEEPS))
+    q_halo = span_halo(q_old, SWEEPS)
+    q_ext = with_halo(q_old, q_halo)
     field = q_old
+    field_ext = q_ext
     for outer_step in range(ITERS):
         forcing = spectral_slabs(field, forward, backward)
-        source = marching * q_old + forcing_gain * forcing
-        iterate = field
-        for sweep_step in range(SWEEPS):
-            span_padded = extended(iterate, (("tile", 2),), 1)
-            beside = span_padded[:, :, :-2] + span_padded[:, :, 2:]
-            beside = beside + normal_sum(
-                iterate, iterate[..., :1] * keep_mask, jnp.zeros_like(iterate[..., :1])
+        forcing_ext = with_halo(forcing, span_halo(forcing, SWEEPS - 1))
+        source_ext = marching * q_ext[:, :, 1:-1] + forcing_gain * forcing_ext
+        iterate = field_ext
+        for sweep_step in range(1, SWEEPS + 1):
+            low, high = sweep_step, rows + 2 * SWEEPS - sweep_step
+            iterate = sweep(
+                iterate,
+                source_ext[:, :, low - 1 : high - 1],
+                base_ext[:, low:high],
+                keep_ext[:, :, low:high],
+                frequency,
             )
-            iterate = relax(source, base_rate, frequency, beside)
+        last = outer_step == ITERS - 1
+        if not last:
+            it_halo = span_halo(iterate, SWEEPS)
         totals = tile_sum(jnp.stack(correction_terms(iterate, q_old)), "tile")
         field = apply_correction(iterate, q_old, totals)
+        if not last:
+            field_ext = jnp.concatenate(
+                [
+                    apply_correction(it_halo[0], q_halo[0], totals),
+                    field,
+                    apply_correction(it_halo[1], q_halo[1], totals),
+                ],
+                axis=2,
+            )
     return field
 
 

time: 187 us -> 187 us (level)
  local copies, waits for them, and re-layouts: 24.8 us -> 34.9 us
  waiting for transfers between devices: 45.6 us -> 36.8 us
  starting transfers between devices: 59 us -> 51.1 us
  other arithmetic: 14.8 us -> 18.3 us
  matrix products: 13.9 us -> 16.1 us
    all_to_all x2, waiting for transfers between devices: 15.5 us -> 9.87 us  [spectral_slabs(): lax.all_to_all(folded.reshape(groups, width, harms * chans * rows), 'harm...]
    ppermute x16 -> x12, starting transfers between devices: 27.7 us -> 23.5 us  [the longest x6 14.8 us: span_halo(): lax.ppermute(block[..., :width, :], 'tile', [((i + 1) % count, i) for i i...]
    slice x1 -> x2, local copies, waits for them, and re-layouts: 0.23 us -> 3.55 us  [normal_sum(): high_side = jnp.concatenate([iterate[..., 1:], above_edge], axis=-1)]
    ppermute x16 -> x12, waiting for transfers between devices: 11.4 us -> 8.28 us  [the longest x6 4.21 us: span_halo(): lax.ppermute(block[..., rows - width:, :], 'tile', [(i, (i + 1) % count)...]
    unnamed x22 -> x80, local copies, waits for them, and re-layouts: 0.76 us -> 3.58 us
    transpose x0 -> x2, local copies, waits for them, and re-layouts: none -> 2.75 us  [spectral_slabs(): back.reshape(depth, harms * chans * rows)]
    all_to_all x1, starting transfers between devices: 8.54 us -> 6.12 us  [tile_sum(): return lax.all_to_all(spread, axis, 0, 0, tiled=True).sum(axis=0)]
    reshape x0 -> x2, local copies, waits for them, and re-layouts: none -> 2.13 us  [spectral_slabs(): back.reshape(depth, harms * chans * rows)]
  transfers between devices with their start and end apart: 21 -> 17, of which waited for: 16 -> 8; matrix products, arithmetic and copies ran while one was open for 21% -> 27% of each run, Pallas kernels for 0% -> 0%
where the time goes in v3:
time: 187 us; the launch traced here: 186 us
  starting transfers between devices  51.1 us (27%)
  waiting for transfers between devices  36.8 us (20%)
  local copies, waits for them, and re-layouts  34.9 us (19%)
  blocking collectives  27.7 us (15%)
  other arithmetic  18.3 us (10%)
  matrix products  16.1 us (9%)
    all_to_all x1, blocking collectives, tile_sum(): return lax.all_to_all(spread, axis, 0, 0, tiled=True).sum(axis=0)  27.7 us
    ppermute x6, starting transfers between devices, span_halo(): lax.ppermute(block[..., :width, :], 'tile', [((i + 1) % count, i) for i i...  14.8 us
    all_to_all x1, waiting for transfers between devices, tile_sum(): return lax.all_to_all(spread, axis, 0, 0, tiled=True).sum(axis=0)  13 us
    all_to_all x2, starting transfers between devices, spectral_slabs(): lax.all_to_all(folded.reshape(groups, width, harms * chans * rows), 'harm...  10.9 us
    all_to_all x2, starting transfers between devices, spectral_slabs(): slabs = lax.all_to_all(cols, 'harm', 0, 0, tiled=True)  10.5 us
    dot_general x2, matrix products, spectral_slabs(): jnp.einsum('mshp,szhpvy->mvyz', forward.reshape(forward.shape[0], groups,...  10.1 us
    all_to_all x2, waiting for transfers between devices, spectral_slabs(): lax.all_to_all(folded.reshape(groups, width, harms * chans * rows), 'harm...  9.87 us
    ppermute x6, starting transfers between devices, span_halo(): lax.ppermute(block[..., rows - width:, :], 'tile', [(i, (i + 1) % count)...  8.72 us
  transfers between devices with their start and end apart: 17, of which 8 were waited for; matrix products, arithmetic and copies ran while one was open for 27% of the time, Pallas kernels for 0%

profile of v3, /device:TPU:1, one launch (start us, length us, event | category | flops | bytes accessed | tf_op | source)
XLA Modules:
  0.0 185.7 jit_solution(8094794457342790623)
XLA Ops:
  0.7 3.0 %collective-permute-start.4 = (f32[4,1]{0,1:T(1,128)S(1)}, f32[4,1]{0,1:T(1,128)S(1)}, u32[]{:S(2)}, u32[]{:S(2)}) collective-permute-start(f32[4,1]{0,1:T(1,128)S(1)} %convert_bitcast_fusion), channel_id=1, source_target_pairs={{0,1},{1,2},{2,3},{3,4},{4,5},{5,6},{6,7},{7,8},{8,9},{9,10},{10,1... | collective-permute-start | bytes 56 | tf_op jit(solution)/shard_map/ppermute | solution.py:145
  3.7 3.8 %collective-permute-start.5 = (f32[4,1]{0,1:T(1,128)S(1)}, f32[4,1]{0,1:T(1,128)S(1)}, u32[]{:S(2)}, u32[]{:S(2)}) collective-permute-start(f32[4,1]{0,1:T(1,128)S(1)} %convert_bitcast_fusion), channel_id=1, source_target_pairs={{1,0},{2,1},{3,2},{4,3},{5,4},{6,5},{7,6},{8,7},{9,8},{10,9},{11,1... | collective-permute-start | bytes 56 | tf_op jit(solution)/shard_map/ppermute | solution.py:148
  7.5 3.6 %collective-permute-start.1 = (f32[8,10,4,256]{3,2,1,0:T(4,128)}, f32[8,10,4,256]{3,2,1,0:T(4,128)}, u32[]{:S(2)}, u32[]{:S(2)}) collective-permute-start(f32[8,10,4,256]{3,2,1,0:T(4,128)} %param.4), channel_id=1, source_target_pairs={{1,0},{2,1},{3,2},{4,3},{5,4},{6,5},{7,6},{8,7},{9,8},{10,9},{11,1... | collective-permute-start | bytes 983048 | tf_op jit(solution)/shard_map/ppermute | solution.py:148
  13.1 6.8 %all-to-all-start = ((f32[16,16,320]{2,1,0:T(8,128)}), f32[16,16,320]{2,1,0:T(8,128)S(1)}, u32[]{:S(2)}, u32[]{:S(2)}) async-start(f32[16,16,320]{2,1,0:T(8,128)} %bitcast.3), calls=%async_computation | async-start | bytes 786432 | tf_op jit(solution)/shard_map/all_to_all | solution.py:121
  22.5 3.3 %collective-permute-start.7 = (f32[5,4,256]{2,1,0:T(4,128)S(1)}, f32[5,4,256]{2,1,0:T(4,128)S(1)}, u32[]{:S(2)}, u32[]{:S(2)}) collective-permute-start(f32[5,4,256]{2,1,0:T(4,128)S(1)} %copy-done.16), channel_id=1, source_target_pairs={{1,0},{2,1},{3,2},{4,3},{5,4},{6,5},{7,6},{8,7},{9,8},{10,9},{11,1... | collective-permute-start | bytes 61448 | tf_op jit(solution)/shard_map/ppermute | solution.py:148
  29.3 1.5 copy.89
  30.8 4.2 %convolution_bitcast_fusion.2 = f32[256,5,4,16]{0,3,2,1:T(8,128)S(1)} fusion(f32[16,16,8,2,5,4]{1,0,5,4,3,2:T(8,128)S(1)} %bitcast.94, f32[256,16,8,1]{0,1,3,2:T(8,128)S(1)} %get-tuple-element.55, f32[256,16,8,1]{0,1,3,2:T(8,128)S(1)} %get-tuple-element.54), kind=kOutput, calls=%fused_computation.38 | convolution fusion | flops 251789312 | bytes 917504 | tf_op jit(solution)/shard_map/mshp,szhpvy->mvyz/dot_general | solution.py:123
  35.1 2.3 %convolution_bitcast_fusion.1 = f32[16,16,8,2,5,4]{0,1,3,2,5,4:T(8,128)S(1)} fusion(f32[256,1,4,16]{0,3,2,1:T(8,128)S(1)} %slice.420, f32[256,4,4,16]{0,3,2,1:T(8,128)S(1)} %slice.419, f32[256,2,4,16]{0,3,2,1:T(8,128)S(1)} %slice.422, f32[256,3,4,16]{0,3,2,1:T(8,128)S(1)} %slice.421, f32[16,8,2,256,1,1]{3,2,1,0,5,4:T(2,128)S(1)} %bitcast.97), kind=kOutput, calls=%fused_computation.17 | convolution fusion | flops 251904000 | bytes 1245184 | tf_op jit(solution)/shard_map/shpm,mvyz->szhpvy/dot_general | solution.py:131
  37.4 2.1 %copy.93 = f32[16,16,8,2,5,4]{1,0,5,4,3,2:T(8,128)} copy(f32[16,16,8,2,5,4]{0,1,3,2,5,4:T(8,128)S(1)} %convolution_bitcast_fusion.1) | data formatting | bytes 655360 | tf_op jit(solution)/shard_map/shpm,mvyz->szhpvy/transpose | solution.py:131
  39.5 3.6 %copy.94 = f32[16,16,320]{2,1,0:T(8,128)} copy(f32[16,16,320]{1,0,2:T(8,128)} %bitcast.95) | data formatting | bytes 655360 | tf_op jit(solution)/shard_map/reshape | solution.py:138
  43.1 7.0 %all-to-all-start.1 = ((f32[16,16,320]{2,1,0:T(8,128)}), f32[16,16,320]{2,1,0:T(8,128)}, u32[]{:S(2)}, u32[]{:S(2)}) async-start(f32[16,16,320]{2,1,0:T(8,128)} %copy.94), calls=%async_computation.1 | async-start | bytes 786432 | tf_op jit(solution)/shard_map/all_to_all | solution.py:138
  51.4 1.6 fusion.112
  53.0 5.6 %all-to-all-done.1 = f32[16,16,320]{2,1,0:T(8,128)} async-done(((f32[16,16,320]{2,1,0:T(8,128)}), f32[16,16,320]{2,1,0:T(8,128)}, u32[]{:S(2)}, u32[]{:S(2)}) %all-to-all-start.1) | async-done | bytes 327712 | tf_op jit(solution)/shard_map/all_to_all | solution.py:138
  58.6 1.9 %copy.95 = f32[320,256]{1,0:T(8,128)} copy(f32[320,256]{0,1:T(8,128)} %bitcast.17) | data formatting | bytes 655360 | tf_op jit(solution)/shard_map/transpose | solution.py:139
  61.7 4.1 %collective-permute-start.3 = (f32[8,10,3,256]{3,2,1,0:T(4,128)S(1)}, f32[8,10,3,256]{3,2,1,0:T(4,128)S(1)}, u32[]{:S(2)}, u32[]{:S(2)}) collective-permute-start(f32[8,10,3,256]{3,2,1,0:T(4,128)S(1)} %get-tuple-element.47), channel_id=1, source_target_pairs={{1,0},{2,1},{3,2},{4,3},{5,4},{6,5},{7,6},{8,7},{9,8},{10,9},{11,1... | collective-permute-start | bytes 737288 | tf_op jit(solution)/shard_map/ppermute | solution.py:148
  73.4 27.7 %all_to_all.30 = f32[32,3,8]{2,1,0:T(4,128)S(1)} all-to-all(f32[32,3,8]{2,1,0:T(4,128)S(1)} %broadcast_in_dim.10), channel_id=1, replica_groups=mesh['harm'=16,'tile'=32] {'tile'}, dimensions={0} | all-to-all | bytes 6144 | tf_op jit(solution)/shard_map/all_to_all | solution.py:112
  102.5 3.8 %all-to-all-start.3 = ((f32[16,16,320]{2,1,0:T(8,128)}), f32[16,16,320]{2,1,0:T(8,128)S(1)}, u32[]{:S(2)}, u32[]{:S(2)}) async-start(f32[16,16,320]{2,1,0:T(8,128)} %bitcast.31), calls=%async_computation.3 | async-start | bytes 786432 | tf_op jit(solution)/shard_map/all_to_all | solution.py:121
  107.1 1.8 collective-permute-start.10
  108.9 5.6 %all-to-all-done.3 = f32[16,16,320]{2,1,0:T(8,128)S(1)} async-done(((f32[16,16,320]{2,1,0:T(8,128)}), f32[16,16,320]{2,1,0:T(8,128)S(1)}, u32[]{:S(2)}, u32[]{:S(2)}) %all-to-all-start.3) | async-done | bytes 327712 | tf_op jit(solution)/shard_map/all_to_all | solution.py:121
  114.5 2.8 %copy.119 = f32[16,16,320]{1,0,2:T(8,128)} copy(f32[16,16,320]{2,1,0:T(8,128)S(1)} %all-to-all-done.3) | data formatting | bytes 655360 | tf_op jit(solution)/shard_map/reshape | solution.py:122
  117.3 5.9 %convolution_bitcast_fusion.3 = f32[256,5,4,16]{0,3,2,1:T(8,128)S(1)} fusion(f32[16,16,8,2,5,4]{1,0,5,4,3,2:T(8,128)} %bitcast.93, f32[256,16,8,1]{0,1,3,2:T(8,128)S(1)} %copy-done.11, f32[256,16,8,1]{0,1,3,2:T(8,128)S(1)} %copy-done.9), kind=kOutput, calls=%fused_computation.39 | convolution fusion | flops 251789312 | bytes 917504 | tf_op jit(solution)/shard_map/mshp,szhpvy->mvyz/dot_general | solution.py:123
  123.3 3.7 %convolution_bitcast_fusion = f32[16,16,8,2,5,4]{0,1,3,2,5,4:T(8,128)} fusion(f32[256,1,4,16]{0,3,2,1:T(8,128)S(1)} %slice.469, f32[256,4,4,16]{0,3,2,1:T(8,128)S(1)} %slice.468, f32[256,2,4,16]{0,3,2,1:T(8,128)S(1)} %slice.471, f32[256,3,4,16]{0,3,2,1:T(8,128)S(1)} %slice.470, f32[16,8,2,256,1,1]{3,2,1,0,5,4:T(2,128)S(1)} %bitcast.98), kind=kOutput, calls=%fused_computation.16 | convolution fusion | flops 251904000 | bytes 1245184 | tf_op jit(solution)/shard_map/shpm,mvyz->szhpvy/dot_general | solution.py:131
  127.1 3.2 %copy.101 = f32[16,16,8,2,5,4]{1,0,5,4,3,2:T(8,128)} copy(f32[16,16,8,2,5,4]{0,1,3,2,5,4:T(8,128)} %convolution_bitcast_fusion) | data formatting | bytes 655360 | tf_op jit(solution)/shard_map/shpm,mvyz->szhpvy/transpose | solution.py:131
  130.3 3.6 %copy.102 = f32[16,16,320]{2,1,0:T(8,128)} copy(f32[16,16,320]{1,0,2:T(8,128)} %bitcast.96) | data formatting | bytes 655360 | tf_op jit(solution)/shard_map/reshape | solution.py:138
  133.9 3.9 %all-to-all-start.4 = ((f32[16,16,320]{2,1,0:T(8,128)}), f32[16,16,320]{2,1,0:T(8,128)S(1)}, u32[]{:S(2)}, u32[]{:S(2)}) async-start(f32[16,16,320]{2,1,0:T(8,128)} %copy.102), calls=%async_computation.4 | async-start | bytes 786432 | tf_op jit(solution)/shard_map/all_to_all | solution.py:138
  139.6 1.9 %fusion.111 = (f32[8,10,10,255]{3,2,1,0:T(8,128)}, f32[8,10,10,255]{3,2,1,0:T(8,128)}) fusion(f32[8,10,12,256]{3,2,1,0:T(8,128)S(1)} %maximum_maximum_fusion), kind=kLoop, calls=%fused_computation.239 | loop fusion | bytes 3264000 | tf_op jit(solution)/shard_map/slice | solution.py:69
  141.5 4.3 %all-to-all-done.4 = f32[16,16,320]{2,1,0:T(8,128)S(1)} async-done(((f32[16,16,320]{2,1,0:T(8,128)}), f32[16,16,320]{2,1,0:T(8,128)S(1)}, u32[]{:S(2)}, u32[]{:S(2)}) %all-to-all-start.4) | async-done | bytes 327712 | tf_op jit(solution)/shard_map/all_to_all | solution.py:138
  147.9 3.9 %collective-permute-start.8 = (f32[8,10,3,256]{3,2,1,0:T(4,128)S(1)}, f32[8,10,3,256]{3,2,1,0:T(4,128)S(1)}, u32[]{:S(2)}, u32[]{:S(2)}) collective-permute-start(f32[8,10,3,256]{3,2,1,0:T(4,128)S(1)} %get-tuple-element.44), channel_id=1, source_target_pairs={{0,1},{1,2},{2,3},{3,4},{4,5},{5,6},{6,7},{7,8},{8,9},{9,10},{10,1... | collective-permute-start | bytes 737288 | tf_op jit(solution)/shard_map/ppermute | solution.py:145
  151.9 3.9 %collective-permute-done.8 = f32[8,10,3,256]{3,2,1,0:T(4,128)S(1)} collective-permute-done((f32[8,10,3,256]{3,2,1,0:T(4,128)S(1)}, f32[8,10,3,256]{3,2,1,0:T(4,128)S(1)}, u32[]{:S(2)}, u32[]{:S(2)}) %collective-permute-start.8) | collective-permute-done | bytes 245792 | tf_op jit(solution)/shard_map/ppermute | solution.py:145
  155.8 2.8 %collective-permute-done.9 = f32[8,10,3,256]{3,2,1,0:T(4,128)S(1)} collective-permute-done((f32[8,10,3,256]{3,2,1,0:T(4,128)S(1)}, f32[8,10,3,256]{3,2,1,0:T(4,128)S(1)}, u32[]{:S(2)}, u32[]{:S(2)}) %collective-permute-start.9) | collective-permute-done | bytes 245792 | tf_op jit(solution)/shard_map/ppermute | solution.py:148
  165.6 6.1 %all-to-all-start.5 = ((f32[32,3,8]{2,1,0:T(4,128)}), f32[32,3,8]{2,1,0:T(4,128)S(1)}, u32[]{:S(2)}, u32[]{:S(2)}) async-start(f32[32,3,8]{2,1,0:T(4,128)} %broadcast_in_dim.11), calls=%async_computation.5 | async-start | bytes 131072 | tf_op jit(solution)/shard_map/all_to_all | solution.py:112
  171.7 13.0 %all-to-all-done.5 = f32[32,3,8]{2,1,0:T(4,128)S(1)} async-done(((f32[32,3,8]{2,1,0:T(4,128)}), f32[32,3,8]{2,1,0:T(4,128)S(1)}, u32[]{:S(2)}, u32[]{:S(2)}) %all-to-all-start.5) | async-done | bytes 3104 | tf_op jit(solution)/shard_map/all_to_all | solution.py:112
  (180 shorter events, 32.7 us)
Async XLA Ops:
  0.0 19.9 %copy-start.16 = (f32[5,4,256]{2,1,0:T(4,128)S(1)}, f32[5,4,256]{2,1,0:T(4,128)}, u32[]{:S(2)}) copy-start(f32[5,4,256]{2,1,0:T(4,128)} %param.5) | copy-start | bytes 61444
  0.0 19.9 %copy-start.36 = (s32[128]{0:T(128)S(1)}, s32[128]{0:T(128)}, u32[]{:S(2)}) copy-start(s32[128]{0:T(128)} %param.6) | copy-start | bytes 1540
  0.7 21.8 %collective-permute-start.4 = (f32[4,1]{0,1:T(1,128)S(1)}, f32[4,1]{0,1:T(1,128)S(1)}, u32[]{:S(2)}, u32[]{:S(2)}) collective-permute-start(f32[4,1]{0,1:T(1,128)S(1)} %convert_bitcast_fusion), channel_id=1, source_target_pairs={{0,1},{1,2},{2,3},{3,4},{4,5},{5,6},{6,7},{7,8},{8,9},{9,10},{10,1... | collective-permute-start | bytes 56 | tf_op jit(solution)/shard_map/ppermute | solution.py:145
  3.7 22.1 %collective-permute-start.5 = (f32[4,1]{0,1:T(1,128)S(1)}, f32[4,1]{0,1:T(1,128)S(1)}, u32[]{:S(2)}, u32[]{:S(2)}) collective-permute-start(f32[4,1]{0,1:T(1,128)S(1)} %convert_bitcast_fusion), channel_id=1, source_target_pairs={{1,0},{2,1},{3,2},{4,3},{5,4},{6,5},{7,6},{8,7},{9,8},{10,9},{11,1... | collective-permute-start | bytes 56 | tf_op jit(solution)/shard_map/ppermute | solution.py:148
  7.5 42.6 %collective-permute-start = (f32[8,10,4,256]{3,2,1,0:T(4,128)}, f32[8,10,4,256]{3,2,1,0:T(4,128)}, u32[]{:S(2)}, u32[]{:S(2)}) collective-permute-start(f32[8,10,4,256]{3,2,1,0:T(4,128)} %param.4), channel_id=1, source_target_pairs={{0,1},{1,2},{2,3},{3,4},{4,5},{5,6},{6,7},{7,8},{8,9},{9,10},{10,1... | collective-permute-start | bytes 983048 | tf_op jit(solution)/shard_map/ppermute | solution.py:145
  7.5 42.6 %collective-permute-start.1 = (f32[8,10,4,256]{3,2,1,0:T(4,128)}, f32[8,10,4,256]{3,2,1,0:T(4,128)}, u32[]{:S(2)}, u32[]{:S(2)}) collective-permute-start(f32[8,10,4,256]{3,2,1,0:T(4,128)} %param.4), channel_id=1, source_target_pairs={{1,0},{2,1},{3,2},{4,3},{5,4},{6,5},{7,6},{8,7},{9,8},{10,9},{11,1... | collective-permute-start | bytes 983048 | tf_op jit(solution)/shard_map/ppermute | solution.py:148
  13.1 16.1 %all-to-all-start = ((f32[16,16,320]{2,1,0:T(8,128)}), f32[16,16,320]{2,1,0:T(8,128)S(1)}, u32[]{:S(2)}, u32[]{:S(2)}) async-start(f32[16,16,320]{2,1,0:T(8,128)} %bitcast.3), calls=%async_computation | async-start | bytes 786432 | tf_op jit(solution)/shard_map/all_to_all | solution.py:121
  19.9 7.4 %collective-permute-start.6 = (f32[5,4,256]{2,1,0:T(4,128)S(1)}, f32[5,4,256]{2,1,0:T(4,128)S(1)}, u32[]{:S(2)}, u32[]{:S(2)}) collective-permute-start(f32[5,4,256]{2,1,0:T(4,128)S(1)} %copy-done.16), channel_id=1, source_target_pairs={{0,1},{1,2},{2,3},{3,4},{4,5},{5,6},{6,7},{7,8},{8,9},{9,10},{10,1... | collective-permute-start | bytes 61448 | tf_op jit(solution)/shard_map/ppermute | solution.py:145
  21.9 8.9 %copy-start.8 = (f32[256,16,8,1]{0,1,3,2:T(8,128)}, f32[256,16,8,1]{0,1,3,2:T(8,128)S(1)}, u32[]{:S(2)}) copy-start(f32[256,16,8,1]{0,1,3,2:T(8,128)S(1)} %get-tuple-element.54) | copy-start | bytes 393220
  21.9 8.9 %copy-start.10 = (f32[256,16,8,1]{0,1,3,2:T(8,128)}, f32[256,16,8,1]{0,1,3,2:T(8,128)S(1)}, u32[]{:S(2)}) copy-start(f32[256,16,8,1]{0,1,3,2:T(8,128)S(1)} %get-tuple-element.55) | copy-start | bytes 393220
  22.5 4.8 %collective-permute-start.7 = (f32[5,4,256]{2,1,0:T(4,128)S(1)}, f32[5,4,256]{2,1,0:T(4,128)S(1)}, u32[]{:S(2)}, u32[]{:S(2)}) collective-permute-start(f32[5,4,256]{2,1,0:T(4,128)S(1)} %copy-done.16), channel_id=1, source_target_pairs={{1,0},{2,1},{3,2},{4,3},{5,4},{6,5},{7,6},{8,7},{9,8},{10,9},{11,1... | collective-permute-start | bytes 61448 | tf_op jit(solution)/shard_map/ppermute | solution.py:148
  26.5 43.3 %copy-start.33 = (f32[8]{0:T(128)}, f32[8]{0:T(128)S(1)}, u32[]{:S(2)}) copy-start(f32[8]{0:T(128)S(1)} %slice_bitcast_fusion.2) | copy-start | bytes 100
  26.6 44.4 %copy-start.31 = (f32[6]{0:T(128)}, f32[6]{0:T(128)S(1)}, u32[]{:S(2)}) copy-start(f32[6]{0:T(128)S(1)} %slice_bitcast_fusion.1) | copy-start | bytes 76
  39.5 10.7 %copy-start = (f32[8,10,4,256]{3,2,1,0:T(4,128)S(1)}, f32[8,10,4,256]{3,2,1,0:T(4,128)}, u32[]{:S(2)}) copy-start(f32[8,10,4,256]{3,2,1,0:T(4,128)} %param.4) | copy-start | bytes 983044
  43.1 15.5 %all-to-all-start.1 = ((f32[16,16,320]{2,1,0:T(8,128)}), f32[16,16,320]{2,1,0:T(8,128)}, u32[]{:S(2)}, u32[]{:S(2)}) async-start(f32[16,16,320]{2,1,0:T(8,128)} %copy.94), calls=%async_computation.1 | async-start | bytes 786432 | tf_op jit(solution)/shard_map/all_to_all | solution.py:138
  61.6 6.7 %copy-start.3 = (f32[8,10,10,255]{3,2,1,0:T(8,128)S(1)}, f32[8,10,10,255]{3,2,1,0:T(8,128)}, u32[]{:S(2)}) copy-start(f32[8,10,10,255]{3,2,1,0:T(8,128)} %get-tuple-element.27) | copy-start | bytes 2448004
  61.7 5.3 %collective-permute-start.2 = (f32[8,10,3,256]{3,2,1,0:T(4,128)S(1)}, f32[8,10,3,256]{3,2,1,0:T(4,128)S(1)}, u32[]{:S(2)}, u32[]{:S(2)}) collective-permute-start(f32[8,10,3,256]{3,2,1,0:T(4,128)S(1)} %get-tuple-element.46), channel_id=1, source_target_pairs={{0,1},{1,2},{2,3},{3,4},{4,5},{5,6},{6,7},{7,8},{8,9},{9,10},{10,1... | collective-permute-start | bytes 737288 | tf_op jit(solution)/shard_map/ppermute | solution.py:145
  61.7 6.5 %collective-permute-start.3 = (f32[8,10,3,256]{3,2,1,0:T(4,128)S(1)}, f32[8,10,3,256]{3,2,1,0:T(4,128)S(1)}, u32[]{:S(2)}, u32[]{:S(2)}) collective-permute-start(f32[8,10,3,256]{3,2,1,0:T(4,128)S(1)} %get-tuple-element.47), channel_id=1, source_target_pairs={{1,0},{2,1},{3,2},{4,3},{5,4},{6,5},{7,6},{8,7},{9,8},{10,9},{11,1... | collective-permute-start | bytes 737288 | tf_op jit(solution)/shard_map/ppermute | solution.py:148
  102.5 12.0 %all-to-all-start.3 = ((f32[16,16,320]{2,1,0:T(8,128)}), f32[16,16,320]{2,1,0:T(8,128)S(1)}, u32[]{:S(2)}, u32[]{:S(2)}) async-start(f32[16,16,320]{2,1,0:T(8,128)} %bitcast.31), calls=%async_computation.3 | async-start | bytes 786432 | tf_op jit(solution)/shard_map/all_to_all | solution.py:121
  107.1 10.2 %copy-start.9 = (f32[256,16,8,1]{0,1,3,2:T(8,128)S(1)}, f32[256,16,8,1]{0,1,3,2:T(8,128)}, u32[]{:S(2)}) copy-start(f32[256,16,8,1]{0,1,3,2:T(8,128)} %copy-done.8) | copy-start | bytes 393220
  107.1 10.2 %copy-start.11 = (f32[256,16,8,1]{0,1,3,2:T(8,128)S(1)}, f32[256,16,8,1]{0,1,3,2:T(8,128)}, u32[]{:S(2)}) copy-start(f32[256,16,8,1]{0,1,3,2:T(8,128)} %copy-done.10) | copy-start | bytes 393220
  107.1 30.7 %collective-permute-start.10 = (f32[8,10,4,256]{3,2,1,0:T(4,128)}, f32[8,10,4,256]{3,2,1,0:T(4,128)S(1)}, u32[]{:S(2)}, u32[]{:S(2)}) collective-permute-start(f32[8,10,4,256]{3,2,1,0:T(4,128)} %pad_maximum_fusion.2), channel_id=1, source_target_pairs={{0,1},{1,2},{2,3},{3,4},{4,5},{5,6},{6,7},{7,8},{8,9},{9,10},{10,1... | collective-permute-start | bytes 983048 | tf_op jit(solution)/shard_map/ppermute | solution.py:145
  108.9 28.9 %collective-permute-start.11 = (f32[8,10,4,256]{3,2,1,0:T(4,128)}, f32[8,10,4,256]{3,2,1,0:T(4,128)S(1)}, u32[]{:S(2)}, u32[]{:S(2)}) collective-permute-start(f32[8,10,4,256]{3,2,1,0:T(4,128)} %pad_maximum_fusion.2), channel_id=1, source_target_pairs={{1,0},{2,1},{3,2},{4,3},{5,4},{6,5},{7,6},{8,7},{9,8},{10,9},{11,1... | collective-permute-start | bytes 983048 | tf_op jit(solution)/shard_map/ppermute | solution.py:148
  130.3 7.6 %copy-start.30 = (f32[8]{0:T(128)S(1)}, f32[8]{0:T(128)}, u32[]{:S(2)}) copy-start(f32[8]{0:T(128)} %copy-done.29) | copy-start | bytes 100
  133.9 5.4 %copy-start.5 = (f32[8,5,4,256]{3,2,1,0:T(4,128)S(1)}, f32[8,5,4,256]{3,2,1,0:T(4,128)}, u32[]{:S(2)}) copy-start(f32[8,5,4,256]{3,2,1,0:T(4,128)} %copy-done.4) | copy-start | bytes 491524
  133.9 11.9 %all-to-all-start.4 = ((f32[16,16,320]{2,1,0:T(8,128)}), f32[16,16,320]{2,1,0:T(8,128)S(1)}, u32[]{:S(2)}, u32[]{:S(2)}) async-start(f32[16,16,320]{2,1,0:T(8,128)} %copy.102), calls=%async_computation.4 | async-start | bytes 786432 | tf_op jit(solution)/shard_map/all_to_all | solution.py:138
  145.8 6.0 %copy-start.35 = (f32[10]{0:T(128)S(1)}, f32[10]{0:T(128)}, u32[]{:S(2)}) copy-start(f32[10]{0:T(128)} %slice_bitcast_fusion.3) | copy-start | bytes 124
  147.7 10.8 %copy-start.1 = (f32[8,10,10,255]{3,2,1,0:T(8,128)S(1)}, f32[8,10,10,255]{3,2,1,0:T(8,128)}, u32[]{:S(2)}) copy-start(f32[8,10,10,255]{3,2,1,0:T(8,128)} %get-tuple-element.24) | copy-start | bytes 2448004
  147.7 10.8 %copy-start.2 = (f32[8,10,10,255]{3,2,1,0:T(8,128)S(1)}, f32[8,10,10,255]{3,2,1,0:T(8,128)}, u32[]{:S(2)}) copy-start(f32[8,10,10,255]{3,2,1,0:T(8,128)} %get-tuple-element.25) | copy-start | bytes 2448004
  147.9 7.9 %collective-permute-start.8 = (f32[8,10,3,256]{3,2,1,0:T(4,128)S(1)}, f32[8,10,3,256]{3,2,1,0:T(4,128)S(1)}, u32[]{:S(2)}, u32[]{:S(2)}) collective-permute-start(f32[8,10,3,256]{3,2,1,0:T(4,128)S(1)} %get-tuple-element.44), channel_id=1, source_target_pairs={{0,1},{1,2},{2,3},{3,4},{4,5},{5,6},{6,7},{7,8},{8,9},{9,10},{10,1... | collective-permute-start | bytes 737288 | tf_op jit(solution)/shard_map/ppermute | solution.py:145
  151.8 6.8 %collective-permute-start.9 = (f32[8,10,3,256]{3,2,1,0:T(4,128)S(1)}, f32[8,10,3,256]{3,2,1,0:T(4,128)S(1)}, u32[]{:S(2)}, u32[]{:S(2)}) collective-permute-start(f32[8,10,3,256]{3,2,1,0:T(4,128)S(1)} %get-tuple-element.45), channel_id=1, source_target_pairs={{1,0},{2,1},{3,2},{4,3},{5,4},{6,5},{7,6},{8,7},{9,8},{10,9},{11,1... | collective-permute-start | bytes 737288 | tf_op jit(solution)/shard_map/ppermute | solution.py:148
  165.6 19.1 %all-to-all-start.5 = ((f32[32,3,8]{2,1,0:T(4,128)}), f32[32,3,8]{2,1,0:T(4,128)S(1)}, u32[]{:S(2)}, u32[]{:S(2)}) async-start(f32[32,3,8]{2,1,0:T(4,128)} %broadcast_in_dim.11), calls=%async_computation.5 | async-start | bytes 131072 | tf_op jit(solution)/shard_map/all_to_all | solution.py:112
  (25 other events, 22.2 us)

commit v4 on v3

--- a/solution.py
+++ b/solution.py
@@ -3,32 +3,17 @@
 import jax
 import jax.numpy as jnp
 from jax import lax
-from jax.sharding import PartitionSpec as P
+from jax.sharding import Mesh, PartitionSpec as P
 
 ITERS = 2
 SWEEPS = 4
+TILE = ("z", "core")
 
 
 coupling = 0.24
 forcing_gain = 0.5
 marching = 1.0
 frequency_scale = 0.5
-
-
-def extended(cells, sides, width):
-    for axis, dim in sides:
-        count = lax.axis_size(axis)
-        head = lax.slice_in_dim(cells, 0, width, axis=dim)
-        tail = lax.slice_in_dim(cells, cells.shape[dim] - width, cells.shape[dim], axis=dim)
-        cells = jnp.concatenate(
-            [
-                lax.ppermute(tail, axis, [(i, (i + 1) % count) for i in range(count)]),
-                cells,
-                lax.ppermute(head, axis, [((i + 1) % count, i) for i in range(count)]),
-            ],
-            axis=dim,
-        )
-    return cells
 
 
 def build_tables(frequencies):
@@ -106,10 +91,11 @@
     return jnp.concatenate([new_real, new_imag], axis=1)
 
 
-def tile_sum(values, axis):
-    count = lax.axis_size(axis)
+def tile_sum(values):
+    values = values + lax.ppermute(values, "core", [(0, 1), (1, 0)])
+    count = lax.axis_size("z")
     spread = jnp.broadcast_to(values[None], (count,) + values.shape)
-    return lax.all_to_all(spread, axis, 0, 0, tiled=True).sum(axis=0)
+    return lax.all_to_all(spread, "z", 0, 0, tiled=True).sum(axis=0)
 
 
 def spectral_slabs(field, forward, backward):
@@ -139,14 +125,28 @@
     return back.reshape(depth, harms * chans * rows).T.reshape(harms, chans, rows, depth)
 
 
-def span_halo(block, width):
-    count = lax.axis_size("tile")
-    rows = block.shape[-2]
-    from_left = lax.ppermute(
-        block[..., rows - width :, :], "tile", [(i, (i + 1) % count) for i in range(count)]
-    )
-    from_right = lax.ppermute(block[..., :width, :], "tile", [((i + 1) % count, i) for i in range(count)])
-    return from_left, from_right
+def span_halo(blocks, width):
+    count = lax.axis_size(TILE)
+    rows = [block.shape[-2] for block in blocks]
+    if len(blocks) == 1:
+        low, high = blocks[0][..., rows[0] - width :, :], blocks[0][..., :width, :]
+        return [
+            (
+                lax.ppermute(low, TILE, [(i, (i + 1) % count) for i in range(count)]),
+                lax.ppermute(high, TILE, [((i + 1) % count, i) for i in range(count)]),
+            )
+        ]
+    lows = jnp.concatenate([b[..., r - width :, :].reshape(-1) for b, r in zip(blocks, rows)])
+    highs = jnp.concatenate([b[..., :width, :].reshape(-1) for b in blocks])
+    from_left = lax.ppermute(lows, TILE, [(i, (i + 1) % count) for i in range(count)])
+    from_right = lax.ppermute(highs, TILE, [((i + 1) % count, i) for i in range(count)])
+    halos, offset = [], 0
+    for b in blocks:
+        shape = b.shape[:-2] + (width,) + b.shape[-1:]
+        size = math.prod(shape)
+        halos.append((from_left[offset : offset + size].reshape(shape), from_right[offset : offset + size].reshape(shape)))
+        offset += size
+    return halos
 
 
 def with_halo(block, halo):
@@ -169,15 +169,15 @@
     rows = q_old.shape[2]
     assert rows >= SWEEPS
     keep = (1 - wall_flags).astype(jnp.float32)[:, None]
-    keep_ext = with_halo(keep, span_halo(keep, SWEEPS))[None, None]
-    base_ext = with_halo(base_rate, span_halo(base_rate, SWEEPS))
-    q_halo = span_halo(q_old, SWEEPS)
+    q_halo, base_halo, keep_halo = span_halo((q_old, base_rate, keep), SWEEPS)
+    keep_ext = with_halo(keep, keep_halo)[None, None]
+    base_ext = with_halo(base_rate, base_halo)
     q_ext = with_halo(q_old, q_halo)
     field = q_old
     field_ext = q_ext
     for outer_step in range(ITERS):
         forcing = spectral_slabs(field, forward, backward)
-        forcing_ext = with_halo(forcing, span_halo(forcing, SWEEPS - 1))
+        forcing_ext = with_halo(forcing, span_halo((forcing,), SWEEPS - 1)[0])
         source_ext = marching * q_ext[:, :, 1:-1] + forcing_gain * forcing_ext
         iterate = field_ext
         for sweep_step in range(1, SWEEPS + 1):
@@ -191,8 +191,8 @@
             )
         last = outer_step == ITERS - 1
         if not last:
-            it_halo = span_halo(iterate, SWEEPS)
-        totals = tile_sum(jnp.stack(correction_terms(iterate, q_old)), "tile")
+            (it_halo,) = span_halo((iterate,), SWEEPS)
+        totals = tile_sum(jnp.stack(correction_terms(iterate, q_old)))
         field = apply_correction(iterate, q_old, totals)
         if not last:
             field_ext = jnp.concatenate(
@@ -207,7 +207,9 @@
 
 
 def solution(mesh):
-    placed = (P("harm", None, "tile", None), P(None, "tile", None), P(), P("tile"))
+    harms, tiles = mesh.devices.shape
+    split = Mesh(mesh.devices.reshape(harms, tiles // 2, 2), ("harm", "z", "core"))
+    placed = (P("harm", None, TILE, None), P(None, TILE, None), P(), P(TILE))
     return jax.shard_map(
-        shards, mesh=mesh, in_specs=placed, out_specs=P("harm", None, "tile", None), check_vma=False
-    )
+        shards, mesh=split, in_specs=placed, out_specs=P("harm", None, TILE, None), check_vma=False
+    )

time: 187 us -> 192 us (1.027)
  local copies, waits for them, and re-layouts: 34.9 us -> 43.4 us
  blocking collectives: 27.7 us -> 20.8 us
  starting transfers between devices: 51.1 us -> 54.8 us
    ppermute x12 -> x10, starting transfers between devices: 23.5 us -> 30.9 us  [the longest x2 10.1 us: tile_sum(): values = values + lax.ppermute(values, 'core', [(0, 1), (1, 0)])]
    all_to_all x1, blocking collectives: 27.7 us -> 20.8 us  [tile_sum(): return lax.all_to_all(spread, 'z', 0, 0, tiled=True).sum(axis=0)]
    all_to_all x2, waiting for transfers between devices: 5.61 us -> 11.2 us  [spectral_slabs(): slabs = lax.all_to_all(cols, 'harm', 0, 0, tiled=True)]
    all_to_all x2, waiting for transfers between devices: 9.87 us -> 4.85 us  [spectral_slabs(): lax.all_to_all(folded.reshape(groups, width, harms * chans * rows), 'harm...]
    slice x2 -> x6, local copies, waits for them, and re-layouts: 0.26 us -> 3.82 us  [the longest x2 1.84 us: span_halo(): from_right[offset:offset + size].reshape(shape)]
    unnamed x80 -> x90, local copies, waits for them, and re-layouts: 3.58 us -> 6.78 us
    all_to_all x2, starting transfers between devices: 10.9 us -> 8.33 us  [spectral_slabs(): lax.all_to_all(folded.reshape(groups, width, harms * chans * rows), 'harm...]
    ppermute x12 -> x10, waiting for transfers between devices: 8.28 us -> 9.46 us  [the longest x3 4.22 us: span_halo(): lax.ppermute(low, TILE, [(i, (i + 1) % count) for i in range(count)])]
  transfers between devices with their start and end apart: 17 -> 15, of which waited for: 8 -> 10; matrix products, arithmetic and copies ran while one was open for 27% -> 27% of each run, Pallas kernels for 0% -> 0%
where the time goes in v4:
time: 192 us; the launch traced here: 190 us
  starting transfers between devices  54.8 us (29%)
  local copies, waits for them, and re-layouts  43.4 us (23%)
  waiting for transfers between devices  37.1 us (19%)
  blocking collectives  20.8 us (11%)
  other arithmetic  16.8 us (9%)
  matrix products  16.1 us (8%)
    all_to_all x1, blocking collectives, tile_sum(): return lax.all_to_all(spread, 'z', 0, 0, tiled=True).sum(axis=0)  20.8 us
    all_to_all x1, waiting for transfers between devices, tile_sum(): return lax.all_to_all(spread, 'z', 0, 0, tiled=True).sum(axis=0)  11.6 us
    all_to_all x2, waiting for transfers between devices, spectral_slabs(): slabs = lax.all_to_all(cols, 'harm', 0, 0, tiled=True)  11.2 us
    all_to_all x2, starting transfers between devices, spectral_slabs(): slabs = lax.all_to_all(cols, 'harm', 0, 0, tiled=True)  10.9 us
    ppermute x2, starting transfers between devices, tile_sum(): values = values + lax.ppermute(values, 'core', [(0, 1), (1, 0)])  10.1 us
    dot_general x2, matrix products, spectral_slabs(): jnp.einsum('mshp,szhpvy->mvyz', forward.reshape(forward.shape[0], groups,...  10.1 us
    ppermute x3, starting transfers between devices, span_halo(): lax.ppermute(low, TILE, [(i, (i + 1) % count) for i in range(count)])  9.39 us
    all_to_all x2, starting transfers between devices, spectral_slabs(): lax.all_to_all(folded.reshape(groups, width, harms * chans * rows), 'harm...  8.33 us
  transfers between devices with their start and end apart: 15, of which 10 were waited for; matrix products, arithmetic and copies ran while one was open for 27% of the time, Pallas kernels for 0%

profile of v4, /device:TPU:1, one launch (start us, length us, event | category | flops | bytes accessed | tf_op | source)
XLA Modules:
  0.0 189.9 jit_solution(4448776499097777059)
XLA Ops:
  3.4 3.0 %collective-permute-start = (f32[87044]{0:T(1024)}, f32[87044]{0:T(1024)}, u32[]{:S(2)}, u32[]{:S(2)}) collective-permute-start(f32[87044]{0:T(1024)} %pad_maximum_fusion.1), channel_id=1, source_target_pairs={{0,1},{1,2},{2,3},{3,4},{4,5},{5,6},{6,7},{7,8},{8,9},{9,10},{10,1... | collective-permute-start | bytes 1044536 | tf_op jit(solution)/shard_map/ppermute | solution.py:141
  6.4 3.8 %collective-permute-start.1 = (f32[87044]{0:T(1024)}, f32[87044]{0:T(1024)}, u32[]{:S(2)}, u32[]{:S(2)}) collective-permute-start(f32[87044]{0:T(1024)} %pad_maximum_fusion.1), channel_id=1, source_target_pairs={{1,0},{2,1},{3,2},{4,3},{5,4},{6,5},{7,6},{8,7},{9,8},{10,9},{11,1... | collective-permute-start | bytes 1044536 | tf_op jit(solution)/shard_map/ppermute | solution.py:142
  11.3 4.2 %all-to-all-start = ((f32[16,16,320]{2,1,0:T(8,128)}), f32[16,16,320]{2,1,0:T(8,128)}, u32[]{:S(2)}, u32[]{:S(2)}) async-start(f32[16,16,320]{2,1,0:T(8,128)} %bitcast.3), calls=%async_computation | async-start | bytes 786432 | tf_op jit(solution)/shard_map/all_to_all | solution.py:107
  18.0 5.7 %all-to-all-done = f32[16,16,320]{2,1,0:T(8,128)} async-done(((f32[16,16,320]{2,1,0:T(8,128)}), f32[16,16,320]{2,1,0:T(8,128)}, u32[]{:S(2)}, u32[]{:S(2)}) %all-to-all-start) | async-done | bytes 327712 | tf_op jit(solution)/shard_map/all_to_all | solution.py:107
  23.7 2.5 %copy.89 = f32[16,16,320]{1,0,2:T(8,128)S(1)} copy(f32[16,16,320]{2,1,0:T(8,128)} %all-to-all-done) | data formatting | bytes 655360 | tf_op jit(solution)/shard_map/all_to_all | solution.py:107
  26.3 4.2 %convolution_bitcast_fusion.2 = f32[256,5,4,16]{0,3,2,1:T(8,128)S(1)} fusion(f32[16,16,8,2,5,4]{1,0,5,4,3,2:T(8,128)S(1)} %bitcast.103, f32[256,16,8,1]{0,1,3,2:T(8,128)S(1)} %get-tuple-element.55, f32[256,16,8,1]{0,1,3,2:T(8,128)S(1)} %get-tuple-element.54), kind=kOutput, calls=%fused_computation.38 | convolution fusion | flops 251789312 | bytes 917504 | tf_op jit(solution)/shard_map/mshp,szhpvy->mvyz/dot_general | solution.py:109
  30.5 2.3 %convolution_bitcast_fusion.1 = f32[16,16,8,2,5,4]{0,1,3,2,5,4:T(8,128)S(1)} fusion(f32[256,1,4,16]{0,3,2,1:T(8,128)S(1)} %slice.446, f32[256,4,4,16]{0,3,2,1:T(8,128)S(1)} %slice.445, f32[256,2,4,16]{0,3,2,1:T(8,128)S(1)} %slice.448, f32[256,3,4,16]{0,3,2,1:T(8,128)S(1)} %slice.447, f32[16,8,2,256,1,1]{3,2,1,0,5,4:T(2,128)S(1)} %bitcast.106), kind=kOutput, calls=%fused_computation.17 | convolution fusion | flops 251904000 | bytes 1245184 | tf_op jit(solution)/shard_map/shpm,mvyz->szhpvy/dot_general | solution.py:117
  32.8 2.1 %copy.93 = f32[16,16,8,2,5,4]{1,0,5,4,3,2:T(8,128)} copy(f32[16,16,8,2,5,4]{0,1,3,2,5,4:T(8,128)S(1)} %convolution_bitcast_fusion.1) | data formatting | bytes 655360 | tf_op jit(solution)/shard_map/shpm,mvyz->szhpvy/transpose | solution.py:117
  34.9 3.6 %copy.94 = f32[16,16,320]{2,1,0:T(8,128)} copy(f32[16,16,320]{1,0,2:T(8,128)} %bitcast.104) | data formatting | bytes 655360 | tf_op jit(solution)/shard_map/reshape | solution.py:124
  38.5 4.4 %all-to-all-start.1 = ((f32[16,16,320]{2,1,0:T(8,128)}), f32[16,16,320]{2,1,0:T(8,128)}, u32[]{:S(2)}, u32[]{:S(2)}) async-start(f32[16,16,320]{2,1,0:T(8,128)} %copy.94), calls=%async_computation.1 | async-start | bytes 786432 | tf_op jit(solution)/shard_map/all_to_all | solution.py:124
  54.2 1.9 copy.95
  57.3 3.1 %collective-permute-start.2 = (f32[8,10,3,256]{3,2,1,0:T(4,128)S(1)}, f32[8,10,3,256]{3,2,1,0:T(4,128)S(1)}, u32[]{:S(2)}, u32[]{:S(2)}) collective-permute-start(f32[8,10,3,256]{3,2,1,0:T(4,128)S(1)} %get-tuple-element.46), channel_id=1, source_target_pairs={{0,1},{1,2},{2,3},{3,4},{4,5},{5,6},{6,7},{7,8},{8,9},{9,10},{10,1... | collective-permute-start | bytes 737288 | tf_op jit(solution)/shard_map/ppermute | solution.py:135
  60.5 4.5 %collective-permute-start.3 = (f32[8,10,3,256]{3,2,1,0:T(4,128)S(1)}, f32[8,10,3,256]{3,2,1,0:T(4,128)S(1)}, u32[]{:S(2)}, u32[]{:S(2)}) collective-permute-start(f32[8,10,3,256]{3,2,1,0:T(4,128)S(1)} %get-tuple-element.47), channel_id=1, source_target_pairs={{1,0},{2,1},{3,2},{4,3},{5,4},{6,5},{7,6},{8,7},{9,8},{10,9},{11,1... | collective-permute-start | bytes 737288 | tf_op jit(solution)/shard_map/ppermute | solution.py:136
  72.1 7.7 %collective-permute-start.4 = (f32[3,8]{1,0:T(4,128)S(1)}, f32[3,8]{1,0:T(4,128)S(1)}, u32[]{:S(2)}, u32[]{:S(2)}) collective-permute-start(f32[3,8]{1,0:T(4,128)S(1)} %pad_maximum_fusion.7), channel_id=1, source_target_pairs={{0,1},{1,0},{2,3},{3,2},{4,5},{5,4},{6,7},{7,6},{8,9},{9,8},{10,11... | collective-permute-start | bytes 296 | tf_op jit(solution)/shard_map/ppermute | solution.py:95
  80.6 20.8 %all_to_all.30 = f32[16,3,8]{2,1,0:T(4,128)S(1)} all-to-all(f32[16,3,8]{2,1,0:T(4,128)S(1)} %broadcast_in_dim.10), channel_id=1, replica_groups=mesh['harm'=16,'z'=16,'core'=2] {'z'}, dimensions={0} | all-to-all | bytes 3072 | tf_op jit(solution)/shard_map/all_to_all | solution.py:98
  102.8 6.7 %all-to-all-start.3 = ((f32[16,16,320]{2,1,0:T(8,128)}), f32[16,16,320]{2,1,0:T(8,128)S(1)}, u32[]{:S(2)}, u32[]{:S(2)}) async-start(f32[16,16,320]{2,1,0:T(8,128)} %bitcast.33), calls=%async_computation.3 | async-start | bytes 786432 | tf_op jit(solution)/shard_map/all_to_all | solution.py:107
  110.3 2.0 %collective-permute-start.7 = (f32[8,10,4,256]{3,2,1,0:T(4,128)}, f32[8,10,4,256]{3,2,1,0:T(4,128)S(1)}, u32[]{:S(2)}, u32[]{:S(2)}) collective-permute-start(f32[8,10,4,256]{3,2,1,0:T(4,128)} %pad_maximum_fusion.3), channel_id=1, source_target_pairs={{0,1},{1,2},{2,3},{3,4},{4,5},{5,6},{6,7},{7,8},{8,9},{9,10},{10,1... | collective-permute-start | bytes 983048 | tf_op jit(solution)/shard_map/ppermute | solution.py:135
  112.3 5.5 %all-to-all-done.3 = f32[16,16,320]{2,1,0:T(8,128)S(1)} async-done(((f32[16,16,320]{2,1,0:T(8,128)}), f32[16,16,320]{2,1,0:T(8,128)S(1)}, u32[]{:S(2)}, u32[]{:S(2)}) %all-to-all-start.3) | async-done | bytes 327712 | tf_op jit(solution)/shard_map/all_to_all | solution.py:107
  117.8 2.8 %copy.119 = f32[16,16,320]{1,0,2:T(8,128)} copy(f32[16,16,320]{2,1,0:T(8,128)S(1)} %all-to-all-done.3) | data formatting | bytes 655360 | tf_op jit(solution)/shard_map/reshape | solution.py:108
  120.6 5.9 %convolution_bitcast_fusion.3 = f32[256,5,4,16]{0,3,2,1:T(8,128)S(1)} fusion(f32[16,16,8,2,5,4]{1,0,5,4,3,2:T(8,128)} %bitcast.102, f32[256,16,8,1]{0,1,3,2:T(8,128)S(1)} %copy-done.15, f32[256,16,8,1]{0,1,3,2:T(8,128)S(1)} %copy-done.13), kind=kOutput, calls=%fused_computation.39 | convolution fusion | flops 251789312 | bytes 917504 | tf_op jit(solution)/shard_map/mshp,szhpvy->mvyz/dot_general | solution.py:109
  126.7 3.7 %convolution_bitcast_fusion = f32[16,16,8,2,5,4]{0,1,3,2,5,4:T(8,128)} fusion(f32[256,1,4,16]{0,3,2,1:T(8,128)S(1)} %slice.499, f32[256,4,4,16]{0,3,2,1:T(8,128)S(1)} %slice.498, f32[256,2,4,16]{0,3,2,1:T(8,128)S(1)} %slice.501, f32[256,3,4,16]{0,3,2,1:T(8,128)S(1)} %slice.500, f32[16,8,2,256,1,1]{3,2,1,0,5,4:T(2,128)S(1)} %bitcast.107), kind=kOutput, calls=%fused_computation.16 | convolution fusion | flops 251904000 | bytes 1245184 | tf_op jit(solution)/shard_map/shpm,mvyz->szhpvy/dot_general | solution.py:117
  130.4 3.2 %copy.101 = f32[16,16,8,2,5,4]{1,0,5,4,3,2:T(8,128)} copy(f32[16,16,8,2,5,4]{0,1,3,2,5,4:T(8,128)} %convolution_bitcast_fusion) | data formatting | bytes 655360 | tf_op jit(solution)/shard_map/shpm,mvyz->szhpvy/transpose | solution.py:117
  133.6 3.7 %copy.102 = f32[16,16,320]{2,1,0:T(8,128)} copy(f32[16,16,320]{1,0,2:T(8,128)} %bitcast.105) | data formatting | bytes 655360 | tf_op jit(solution)/shard_map/reshape | solution.py:124
  137.3 3.9 %all-to-all-start.4 = ((f32[16,16,320]{2,1,0:T(8,128)}), f32[16,16,320]{2,1,0:T(8,128)S(1)}, u32[]{:S(2)}, u32[]{:S(2)}) async-start(f32[16,16,320]{2,1,0:T(8,128)} %copy.102), calls=%async_computation.4 | async-start | bytes 786432 | tf_op jit(solution)/shard_map/all_to_all | solution.py:124
  142.4 2.0 %fusion.114 = (f32[8,10,10,255]{3,2,1,0:T(8,128)}, f32[8,10,10,255]{3,2,1,0:T(8,128)}) fusion(f32[8,10,12,256]{3,2,1,0:T(8,128)S(1)} %maximum_maximum_fusion), kind=kLoop, calls=%fused_computation.245 | loop fusion | bytes 3264000 | tf_op jit(solution)/shard_map/slice | solution.py:54
  144.3 4.8 %all-to-all-done.4 = f32[16,16,320]{2,1,0:T(8,128)S(1)} async-done(((f32[16,16,320]{2,1,0:T(8,128)}), f32[16,16,320]{2,1,0:T(8,128)S(1)}, u32[]{:S(2)}, u32[]{:S(2)}) %all-to-all-start.4) | async-done | bytes 327712 | tf_op jit(solution)/shard_map/all_to_all | solution.py:124
  151.3 4.3 %collective-permute-start.5 = (f32[8,10,3,256]{3,2,1,0:T(4,128)S(1)}, f32[8,10,3,256]{3,2,1,0:T(4,128)S(1)}, u32[]{:S(2)}, u32[]{:S(2)}) collective-permute-start(f32[8,10,3,256]{3,2,1,0:T(4,128)S(1)} %get-tuple-element.44), channel_id=1, source_target_pairs={{0,1},{1,2},{2,3},{3,4},{4,5},{5,6},{6,7},{7,8},{8,9},{9,10},{10,1... | collective-permute-start | bytes 737288 | tf_op jit(solution)/shard_map/ppermute | solution.py:135
  155.7 3.9 %collective-permute-done.5 = f32[8,10,3,256]{3,2,1,0:T(4,128)S(1)} collective-permute-done((f32[8,10,3,256]{3,2,1,0:T(4,128)S(1)}, f32[8,10,3,256]{3,2,1,0:T(4,128)S(1)}, u32[]{:S(2)}, u32[]{:S(2)}) %collective-permute-start.5) | collective-permute-done | bytes 245792 | tf_op jit(solution)/shard_map/ppermute | solution.py:135
  159.6 2.8 %collective-permute-done.6 = f32[8,10,3,256]{3,2,1,0:T(4,128)S(1)} collective-permute-done((f32[8,10,3,256]{3,2,1,0:T(4,128)S(1)}, f32[8,10,3,256]{3,2,1,0:T(4,128)S(1)}, u32[]{:S(2)}, u32[]{:S(2)}) %collective-permute-start.6) | collective-permute-done | bytes 245792 | tf_op jit(solution)/shard_map/ppermute | solution.py:136
  168.7 2.5 %collective-permute-start.9 = (f32[3,8]{1,0:T(4,128)S(1)}, f32[3,8]{1,0:T(4,128)S(1)}, u32[]{:S(2)}, u32[]{:S(2)}) collective-permute-start(f32[3,8]{1,0:T(4,128)S(1)} %pad_maximum_fusion.6), channel_id=1, source_target_pairs={{0,1},{1,0},{2,3},{3,2},{4,5},{5,4},{6,7},{7,6},{8,9},{9,8},{10,11... | collective-permute-start | bytes 296 | tf_op jit(solution)/shard_map/ppermute | solution.py:95
  172.6 4.7 %all-to-all-start.5 = ((f32[16,3,8]{2,1,0:T(4,128)}), f32[16,3,8]{2,1,0:T(4,128)S(1)}, u32[]{:S(2)}, u32[]{:S(2)}) async-start(f32[16,3,8]{2,1,0:T(4,128)} %broadcast_in_dim.11), calls=%async_computation.5 | async-start | bytes 65536 | tf_op jit(solution)/shard_map/all_to_all | solution.py:98
  177.4 11.6 %all-to-all-done.5 = f32[16,3,8]{2,1,0:T(4,128)S(1)} async-done(((f32[16,3,8]{2,1,0:T(4,128)}), f32[16,3,8]{2,1,0:T(4,128)S(1)}, u32[]{:S(2)}, u32[]{:S(2)}) %all-to-all-start.5) | async-done | bytes 1568 | tf_op jit(solution)/shard_map/all_to_all | solution.py:98
  (199 shorter events, 41.3 us)
Async XLA Ops:
  0.0 10.2 %copy-start = (f32[8,10,4,256]{3,2,1,0:T(4,128)S(1)}, f32[8,10,4,256]{3,2,1,0:T(4,128)}, u32[]{:S(2)}) copy-start(f32[8,10,4,256]{3,2,1,0:T(4,128)} %param.4) | copy-start | bytes 983044
  2.6 12.9 %copy-start.40 = (s32[128]{0:T(128)S(1)}, s32[128]{0:T(128)}, u32[]{:S(2)}) copy-start(s32[128]{0:T(128)} %param.6) | copy-start | bytes 1540
  3.4 12.7 %copy-start.20 = (f32[5,4,256]{2,1,0:T(4,128)S(1)}, f32[5,4,256]{2,1,0:T(4,128)}, u32[]{:S(2)}) copy-start(f32[5,4,256]{2,1,0:T(4,128)} %param.5) | copy-start | bytes 61444
  3.4 40.2 %collective-permute-start = (f32[87044]{0:T(1024)}, f32[87044]{0:T(1024)}, u32[]{:S(2)}, u32[]{:S(2)}) collective-permute-start(f32[87044]{0:T(1024)} %pad_maximum_fusion.1), channel_id=1, source_target_pairs={{0,1},{1,2},{2,3},{3,4},{4,5},{5,6},{6,7},{7,8},{8,9},{9,10},{10,1... | collective-permute-start | bytes 1044536 | tf_op jit(solution)/shard_map/ppermute | solution.py:141
  6.4 36.5 %collective-permute-start.1 = (f32[87044]{0:T(1024)}, f32[87044]{0:T(1024)}, u32[]{:S(2)}, u32[]{:S(2)}) collective-permute-start(f32[87044]{0:T(1024)} %pad_maximum_fusion.1), channel_id=1, source_target_pairs={{1,0},{2,1},{3,2},{4,3},{5,4},{6,5},{7,6},{8,7},{9,8},{10,9},{11,1... | collective-permute-start | bytes 1044536 | tf_op jit(solution)/shard_map/ppermute | solution.py:142
  11.3 12.5 %all-to-all-start = ((f32[16,16,320]{2,1,0:T(8,128)}), f32[16,16,320]{2,1,0:T(8,128)}, u32[]{:S(2)}, u32[]{:S(2)}) async-start(f32[16,16,320]{2,1,0:T(8,128)} %bitcast.3), calls=%async_computation | async-start | bytes 786432 | tf_op jit(solution)/shard_map/all_to_all | solution.py:107
  18.0 8.2 %copy-start.12 = (f32[256,16,8,1]{0,1,3,2:T(8,128)}, f32[256,16,8,1]{0,1,3,2:T(8,128)S(1)}, u32[]{:S(2)}) copy-start(f32[256,16,8,1]{0,1,3,2:T(8,128)S(1)} %get-tuple-element.54) | copy-start | bytes 393220
  18.0 8.2 %copy-start.14 = (f32[256,16,8,1]{0,1,3,2:T(8,128)}, f32[256,16,8,1]{0,1,3,2:T(8,128)S(1)}, u32[]{:S(2)}) copy-start(f32[256,16,8,1]{0,1,3,2:T(8,128)S(1)} %get-tuple-element.55) | copy-start | bytes 393220
  38.5 15.7 %all-to-all-start.1 = ((f32[16,16,320]{2,1,0:T(8,128)}), f32[16,16,320]{2,1,0:T(8,128)}, u32[]{:S(2)}, u32[]{:S(2)}) async-start(f32[16,16,320]{2,1,0:T(8,128)} %copy.94), calls=%async_computation.1 | async-start | bytes 786432 | tf_op jit(solution)/shard_map/all_to_all | solution.py:124
  45.0 23.5 %copy-start.37 = (f32[8]{0:T(128)}, f32[8]{0:T(128)S(1)}, u32[]{:S(2)}) copy-start(f32[8]{0:T(128)S(1)} %slice_bitcast_fusion.4) | copy-start | bytes 100
  47.9 21.8 %copy-start.35 = (f32[6]{0:T(128)}, f32[6]{0:T(128)S(1)}, u32[]{:S(2)}) copy-start(f32[6]{0:T(128)S(1)} %slice_bitcast_fusion.3) | copy-start | bytes 76
  57.2 9.8 %copy-start.3 = (f32[8,10,10,255]{3,2,1,0:T(8,128)S(1)}, f32[8,10,10,255]{3,2,1,0:T(8,128)}, u32[]{:S(2)}) copy-start(f32[8,10,10,255]{3,2,1,0:T(8,128)} %get-tuple-element.27) | copy-start | bytes 2448004
  57.3 8.8 %collective-permute-start.2 = (f32[8,10,3,256]{3,2,1,0:T(4,128)S(1)}, f32[8,10,3,256]{3,2,1,0:T(4,128)S(1)}, u32[]{:S(2)}, u32[]{:S(2)}) collective-permute-start(f32[8,10,3,256]{3,2,1,0:T(4,128)S(1)} %get-tuple-element.46), channel_id=1, source_target_pairs={{0,1},{1,2},{2,3},{3,4},{4,5},{5,6},{6,7},{7,8},{8,9},{9,10},{10,1... | collective-permute-start | bytes 737288 | tf_op jit(solution)/shard_map/ppermute | solution.py:135
  60.5 6.5 %collective-permute-start.3 = (f32[8,10,3,256]{3,2,1,0:T(4,128)S(1)}, f32[8,10,3,256]{3,2,1,0:T(4,128)S(1)}, u32[]{:S(2)}, u32[]{:S(2)}) collective-permute-start(f32[8,10,3,256]{3,2,1,0:T(4,128)S(1)} %get-tuple-element.47), channel_id=1, source_target_pairs={{1,0},{2,1},{3,2},{4,3},{5,4},{6,5},{7,6},{8,7},{9,8},{10,9},{11,1... | collective-permute-start | bytes 737288 | tf_op jit(solution)/shard_map/ppermute | solution.py:136
  72.1 8.5 %collective-permute-start.4 = (f32[3,8]{1,0:T(4,128)S(1)}, f32[3,8]{1,0:T(4,128)S(1)}, u32[]{:S(2)}, u32[]{:S(2)}) collective-permute-start(f32[3,8]{1,0:T(4,128)S(1)} %pad_maximum_fusion.7), channel_id=1, source_target_pairs={{0,1},{1,0},{2,3},{3,2},{4,5},{5,4},{6,7},{7,6},{8,9},{9,8},{10,11... | collective-permute-start | bytes 296 | tf_op jit(solution)/shard_map/ppermute | solution.py:95
  102.8 15.0 %all-to-all-start.3 = ((f32[16,16,320]{2,1,0:T(8,128)}), f32[16,16,320]{2,1,0:T(8,128)S(1)}, u32[]{:S(2)}, u32[]{:S(2)}) async-start(f32[16,16,320]{2,1,0:T(8,128)} %bitcast.33), calls=%async_computation.3 | async-start | bytes 786432 | tf_op jit(solution)/shard_map/all_to_all | solution.py:107
  110.3 10.3 %copy-start.13 = (f32[256,16,8,1]{0,1,3,2:T(8,128)S(1)}, f32[256,16,8,1]{0,1,3,2:T(8,128)}, u32[]{:S(2)}) copy-start(f32[256,16,8,1]{0,1,3,2:T(8,128)} %copy-done.12) | copy-start | bytes 393220
  110.3 10.3 %copy-start.15 = (f32[256,16,8,1]{0,1,3,2:T(8,128)S(1)}, f32[256,16,8,1]{0,1,3,2:T(8,128)}, u32[]{:S(2)}) copy-start(f32[256,16,8,1]{0,1,3,2:T(8,128)} %copy-done.14) | copy-start | bytes 393220
  110.3 30.9 %collective-permute-start.7 = (f32[8,10,4,256]{3,2,1,0:T(4,128)}, f32[8,10,4,256]{3,2,1,0:T(4,128)S(1)}, u32[]{:S(2)}, u32[]{:S(2)}) collective-permute-start(f32[8,10,4,256]{3,2,1,0:T(4,128)} %pad_maximum_fusion.3), channel_id=1, source_target_pairs={{0,1},{1,2},{2,3},{3,4},{4,5},{5,6},{6,7},{7,8},{8,9},{9,10},{10,1... | collective-permute-start | bytes 983048 | tf_op jit(solution)/shard_map/ppermute | solution.py:135
  112.3 29.0 %collective-permute-start.8 = (f32[8,10,4,256]{3,2,1,0:T(4,128)}, f32[8,10,4,256]{3,2,1,0:T(4,128)S(1)}, u32[]{:S(2)}, u32[]{:S(2)}) collective-permute-start(f32[8,10,4,256]{3,2,1,0:T(4,128)} %pad_maximum_fusion.3), channel_id=1, source_target_pairs={{1,0},{2,1},{3,2},{4,3},{5,4},{6,5},{7,6},{8,7},{9,8},{10,9},{11,1... | collective-permute-start | bytes 983048 | tf_op jit(solution)/shard_map/ppermute | solution.py:136
  133.6 7.6 %copy-start.5 = (f32[8,10,4,256]{3,2,1,0:T(4,128)S(1)}, f32[8,10,4,256]{3,2,1,0:T(4,128)}, u32[]{:S(2)}) copy-start(f32[8,10,4,256]{3,2,1,0:T(4,128)} %copy-done.4) | copy-start | bytes 983044
  133.6 7.7 %copy-start.7 = (f32[8,10,4,256]{3,2,1,0:T(4,128)S(1)}, f32[8,10,4,256]{3,2,1,0:T(4,128)}, u32[]{:S(2)}) copy-start(f32[8,10,4,256]{3,2,1,0:T(4,128)} %copy-done.6) | copy-start | bytes 983044
  133.6 7.7 %copy-start.34 = (f32[8]{0:T(128)S(1)}, f32[8]{0:T(128)}, u32[]{:S(2)}) copy-start(f32[8]{0:T(128)} %copy-done.33) | copy-start | bytes 100
  137.3 4.3 %copy-start.9 = (f32[8,5,4,256]{3,2,1,0:T(4,128)S(1)}, f32[8,5,4,256]{3,2,1,0:T(4,128)}, u32[]{:S(2)}) copy-start(f32[8,5,4,256]{3,2,1,0:T(4,128)} %copy-done.8) | copy-start | bytes 491524
  137.3 11.9 %all-to-all-start.4 = ((f32[16,16,320]{2,1,0:T(8,128)}), f32[16,16,320]{2,1,0:T(8,128)S(1)}, u32[]{:S(2)}, u32[]{:S(2)}) async-start(f32[16,16,320]{2,1,0:T(8,128)} %copy.102), calls=%async_computation.4 | async-start | bytes 786432 | tf_op jit(solution)/shard_map/all_to_all | solution.py:124
  149.2 6.4 %copy-start.39 = (f32[10]{0:T(128)S(1)}, f32[10]{0:T(128)}, u32[]{:S(2)}) copy-start(f32[10]{0:T(128)} %slice_bitcast_fusion.5) | copy-start | bytes 124
  151.1 11.2 %copy-start.1 = (f32[8,10,10,255]{3,2,1,0:T(8,128)S(1)}, f32[8,10,10,255]{3,2,1,0:T(8,128)}, u32[]{:S(2)}) copy-start(f32[8,10,10,255]{3,2,1,0:T(8,128)} %get-tuple-element.24) | copy-start | bytes 2448004
  151.1 11.2 %copy-start.2 = (f32[8,10,10,255]{3,2,1,0:T(8,128)S(1)}, f32[8,10,10,255]{3,2,1,0:T(8,128)}, u32[]{:S(2)}) copy-start(f32[8,10,10,255]{3,2,1,0:T(8,128)} %get-tuple-element.25) | copy-start | bytes 2448004
  151.3 8.3 %collective-permute-start.5 = (f32[8,10,3,256]{3,2,1,0:T(4,128)S(1)}, f32[8,10,3,256]{3,2,1,0:T(4,128)S(1)}, u32[]{:S(2)}, u32[]{:S(2)}) collective-permute-start(f32[8,10,3,256]{3,2,1,0:T(4,128)S(1)} %get-tuple-element.44), channel_id=1, source_target_pairs={{0,1},{1,2},{2,3},{3,4},{4,5},{5,6},{6,7},{7,8},{8,9},{9,10},{10,1... | collective-permute-start | bytes 737288 | tf_op jit(solution)/shard_map/ppermute | solution.py:135
  155.5 6.8 %collective-permute-start.6 = (f32[8,10,3,256]{3,2,1,0:T(4,128)S(1)}, f32[8,10,3,256]{3,2,1,0:T(4,128)S(1)}, u32[]{:S(2)}, u32[]{:S(2)}) collective-permute-start(f32[8,10,3,256]{3,2,1,0:T(4,128)S(1)} %get-tuple-element.45), channel_id=1, source_target_pairs={{1,0},{2,1},{3,2},{4,3},{5,4},{6,5},{7,6},{8,7},{9,8},{10,9},{11,1... | collective-permute-start | bytes 737288 | tf_op jit(solution)/shard_map/ppermute | solution.py:136
  168.7 3.3 %collective-permute-start.9 = (f32[3,8]{1,0:T(4,128)S(1)}, f32[3,8]{1,0:T(4,128)S(1)}, u32[]{:S(2)}, u32[]{:S(2)}) collective-permute-start(f32[3,8]{1,0:T(4,128)S(1)} %pad_maximum_fusion.6), channel_id=1, source_target_pairs={{0,1},{1,0},{2,3},{3,2},{4,5},{5,4},{6,7},{7,6},{8,9},{9,8},{10,11... | collective-permute-start | bytes 296 | tf_op jit(solution)/shard_map/ppermute | solution.py:95
  172.6 16.3 %all-to-all-start.5 = ((f32[16,3,8]{2,1,0:T(4,128)}), f32[16,3,8]{2,1,0:T(4,128)S(1)}, u32[]{:S(2)}, u32[]{:S(2)}) async-start(f32[16,3,8]{2,1,0:T(4,128)} %broadcast_in_dim.11), calls=%async_computation.5 | async-start | bytes 65536 | tf_op jit(solution)/shard_map/all_to_all | solution.py:98
  (27 other events, 23.7 us)

commit v5 on v4

--- a/solution.py
+++ b/solution.py
@@ -92,10 +92,9 @@
 
 
 def tile_sum(values):
-    values = values + lax.ppermute(values, "core", [(0, 1), (1, 0)])
-    count = lax.axis_size("z")
+    count = lax.axis_size(TILE)
     spread = jnp.broadcast_to(values[None], (count,) + values.shape)
-    return lax.all_to_all(spread, "z", 0, 0, tiled=True).sum(axis=0)
+    return lax.all_to_all(spread, TILE, 0, 0, tiled=True).sum(axis=0)
 
 
 def spectral_slabs(field, forward, backward):
@@ -160,6 +159,36 @@
     return relax(source, base_rate, frequency, beside)
 
 
+def conj_gain(values, base_rate, frequency):
+    var_count = base_rate.shape[0]
+    rate_col = frequency[:, None, None, None]
+    denominator = base_rate * base_rate + rate_col * rate_col
+    real, imag = values[:, :var_count], values[:, var_count:]
+    return jnp.concatenate(
+        [(real * base_rate - imag * rate_col) / denominator, (imag * base_rate + real * rate_col) / denominator],
+        axis=1,
+    )
+
+
+def adjoint_weights(q_ext, base_ext, keep_ext, frequency, rows):
+    total = rows + 2 * SWEEPS
+    weights = [q_ext]
+    for step in range(1, SWEEPS + 1):
+        low, high = step - 1, total - step + 1
+        scaled = conj_gain(weights[-1], base_ext[:, low:high], frequency)
+        center = scaled[:, :, 1:-1]
+        beside = scaled[:, :, :-2] + scaled[:, :, 2:]
+        beside = beside + normal_sum(
+            center, center[..., :1] * keep_ext[:, :, step : total - step], jnp.zeros_like(center[..., :1])
+        )
+        weights.append(coupling * beside)
+    local = [w[:, :, SWEEPS - j : SWEEPS - j + rows] for j, w in enumerate(weights)]
+    summed = local[0]
+    for w in local[1:SWEEPS]:
+        summed = summed + w
+    return local[SWEEPS], conj_gain(summed, base_ext[:, SWEEPS : SWEEPS + rows], frequency)
+
+
 def shards(q_old, base_rate, freq_table, wall_flags):
     forward, backward = build_tables(freq_table)
     frequency_all = freq_table.astype(jnp.float32) * (frequency_scale / freq_table.shape[0])
@@ -173,10 +202,17 @@
     keep_ext = with_halo(keep, keep_halo)[None, None]
     base_ext = with_halo(base_rate, base_halo)
     q_ext = with_halo(q_old, q_halo)
+    field_weight, source_weight = adjoint_weights(q_ext, base_ext, keep_ext, frequency, rows)
+    norm_old = correction_terms(q_old, q_old)[2]
     field = q_old
     field_ext = q_ext
     for outer_step in range(ITERS):
+        field_proj = correction_terms(field, field_weight)
         forcing = spectral_slabs(field, forward, backward)
+        source_proj = correction_terms(marching * q_old + forcing_gain * forcing, source_weight)
+        totals = tile_sum(
+            jnp.stack([field_proj[0] + source_proj[0], field_proj[1] + source_proj[1], norm_old])
+        )
         forcing_ext = with_halo(forcing, span_halo((forcing,), SWEEPS - 1)[0])
         source_ext = marching * q_ext[:, :, 1:-1] + forcing_gain * forcing_ext
         iterate = field_ext
@@ -192,7 +228,6 @@
         last = outer_step == ITERS - 1
         if not last:
             (it_halo,) = span_halo((iterate,), SWEEPS)
-        totals = tile_sum(jnp.stack(correction_terms(iterate, q_old)))
         field = apply_correction(iterate, q_old, totals)
         if not last:
             field_ext = jnp.concatenate(

time: 192 us -> 194 us (1.010)
  blocking collectives: 20.8 us -> 0 us
  other arithmetic: 16.8 us -> 33.5 us
  starting transfers between devices: 54.8 us -> 60 us
    all_to_all x1 -> x0, blocking collectives: 20.8 us -> none  [tile_sum(): return lax.all_to_all(spread, 'z', 0, 0, tiled=True).sum(axis=0)]
    all_to_all x1 -> x2, starting transfers between devices: 4.69 us -> 22.8 us  [tile_sum(): return lax.all_to_all(spread, TILE, 0, 0, tiled=True).sum(axis=0)]
    ppermute x2 -> x0, starting transfers between devices: 10.1 us -> none  [tile_sum(): values = values + lax.ppermute(values, 'core', [(0, 1), (1, 0)])]
    all_to_all x1 -> x2, waiting for transfers between devices: 11.6 us -> 20.9 us  [tile_sum(): return lax.all_to_all(spread, TILE, 0, 0, tiled=True).sum(axis=0)]
    ppermute x3, waiting for transfers between devices: 4.22 us -> 0.01 us  [span_halo(): lax.ppermute(low, TILE, [(i, (i + 1) % count) for i in range(count)])]
    add x8, other arithmetic: 5.03 us -> 8.99 us  [relax(): numerator = source + coupling * beside]
    ppermute x3, waiting for transfers between devices: 3.63 us -> 0.01 us  [span_halo(): lax.ppermute(high, TILE, [((i + 1) % count, i) for i in range(count)])]
    mul x0 -> x4, other arithmetic: none -> 3.31 us  [adjoint_weights(): weights.append(coupling * beside)]
  transfers between devices with their start and end apart: 15 -> 14, of which waited for: 10 -> 5; matrix products, arithmetic and copies ran while one was open for 27% -> 31% of each run, Pallas kernels for 0% -> 0%
where the time goes in v5:
time: 194 us; the launch traced here: 193 us
  starting transfers between devices  60 us (31%)
  local copies, waits for them, and re-layouts  44.8 us (23%)
  waiting for transfers between devices  37.1 us (19%)
  other arithmetic  33.5 us (17%)
  matrix products  16.1 us (8%)
    all_to_all x2, starting transfers between devices, tile_sum(): return lax.all_to_all(spread, TILE, 0, 0, tiled=True).sum(axis=0)  22.8 us
    all_to_all x2, waiting for transfers between devices, tile_sum(): return lax.all_to_all(spread, TILE, 0, 0, tiled=True).sum(axis=0)  20.9 us
    all_to_all x2, waiting for transfers between devices, spectral_slabs(): slabs = lax.all_to_all(cols, 'harm', 0, 0, tiled=True)  11.1 us
    all_to_all x2, starting transfers between devices, spectral_slabs(): slabs = lax.all_to_all(cols, 'harm', 0, 0, tiled=True)  10.8 us
    dot_general x2, matrix products, spectral_slabs(): jnp.einsum('mshp,szhpvy->mvyz', forward.reshape(forward.shape[0], groups,...  10.1 us
    add x8, other arithmetic, relax(): numerator = source + coupling * beside  8.99 us
    all_to_all x2, starting transfers between devices, spectral_slabs(): lax.all_to_all(folded.reshape(groups, width, harms * chans * rows), 'harm...  8.07 us
    reshape x2, local copies, waits for them, and re-layouts, spectral_slabs(): folded.reshape(groups, width, harms * chans * rows)  7.23 us
  transfers between devices with their start and end apart: 14, of which 5 were waited for; matrix products, arithmetic and copies ran while one was open for 31% of the time, Pallas kernels for 0%

profile of v5, /device:TPU:1, one launch (start us, length us, event | category | flops | bytes accessed | tf_op | source)
XLA Modules:
  0.0 192.6 jit_solution(2915646447997455979)
XLA Ops:
  3.4 3.0 %collective-permute-start = (f32[87044]{0:T(1024)}, f32[87044]{0:T(1024)}, u32[]{:S(2)}, u32[]{:S(2)}) collective-permute-start(f32[87044]{0:T(1024)} %pad_maximum_fusion.1), channel_id=1, source_target_pairs={{0,1},{1,2},{2,3},{3,4},{4,5},{5,6},{6,7},{7,8},{8,9},{9,10},{10,1... | collective-permute-start | bytes 1044536 | tf_op jit(solution)/shard_map/ppermute | solution.py:140
  6.4 3.8 %collective-permute-start.1 = (f32[87044]{0:T(1024)}, f32[87044]{0:T(1024)}, u32[]{:S(2)}, u32[]{:S(2)}) collective-permute-start(f32[87044]{0:T(1024)} %pad_maximum_fusion.1), channel_id=1, source_target_pairs={{1,0},{2,1},{3,2},{4,3},{5,4},{6,5},{7,6},{8,7},{9,8},{10,9},{11,1... | collective-permute-start | bytes 1044536 | tf_op jit(solution)/shard_map/ppermute | solution.py:141
  11.2 4.2 %all-to-all-start = ((f32[16,16,320]{2,1,0:T(8,128)}), f32[16,16,320]{2,1,0:T(8,128)}, u32[]{:S(2)}, u32[]{:S(2)}) async-start(f32[16,16,320]{2,1,0:T(8,128)} %bitcast.3), calls=%async_computation | async-start | bytes 786432 | tf_op jit(solution)/shard_map/all_to_all | solution.py:106
  18.0 5.7 %all-to-all-done = f32[16,16,320]{2,1,0:T(8,128)} async-done(((f32[16,16,320]{2,1,0:T(8,128)}), f32[16,16,320]{2,1,0:T(8,128)}, u32[]{:S(2)}, u32[]{:S(2)}) %all-to-all-start) | async-done | bytes 327712 | tf_op jit(solution)/shard_map/all_to_all | solution.py:106
  23.7 2.5 %copy.91 = f32[16,16,320]{1,0,2:T(8,128)S(1)} copy(f32[16,16,320]{2,1,0:T(8,128)} %all-to-all-done) | data formatting | bytes 655360 | tf_op jit(solution)/shard_map/all_to_all | solution.py:106
  26.2 4.2 %convolution_bitcast_fusion.2 = f32[256,5,4,16]{0,3,2,1:T(8,128)S(1)} fusion(f32[16,16,8,2,5,4]{1,0,5,4,3,2:T(8,128)S(1)} %bitcast.107, f32[256,16,8,1]{0,1,3,2:T(8,128)S(1)} %get-tuple-element.77, f32[256,16,8,1]{0,1,3,2:T(8,128)S(1)} %get-tuple-element.76), kind=kOutput, calls=%fused_computation.65 | convolution fusion | flops 251789312 | bytes 917504 | tf_op jit(solution)/shard_map/mshp,szhpvy->mvyz/dot_general | solution.py:108
  30.5 2.3 %convolution_bitcast_fusion.1 = f32[16,16,8,2,5,4]{0,1,3,2,5,4:T(8,128)S(1)} fusion(f32[256,1,4,16]{0,3,2,1:T(8,128)S(1)} %slice.627, f32[256,4,4,16]{0,3,2,1:T(8,128)S(1)} %slice.626, f32[256,2,4,16]{0,3,2,1:T(8,128)S(1)} %slice.629, f32[256,3,4,16]{0,3,2,1:T(8,128)S(1)} %slice.628, f32[16,8,2,256,1,1]{3,2,1,0,5,4:T(2,128)S(1)} %bitcast.110), kind=kOutput, calls=%fused_computation.39 | convolution fusion | flops 251904000 | bytes 1245184 | tf_op jit(solution)/shard_map/shpm,mvyz->szhpvy/dot_general | solution.py:116
  32.8 2.1 %copy.95 = f32[16,16,8,2,5,4]{1,0,5,4,3,2:T(8,128)} copy(f32[16,16,8,2,5,4]{0,1,3,2,5,4:T(8,128)S(1)} %convolution_bitcast_fusion.1) | data formatting | bytes 655360 | tf_op jit(solution)/shard_map/shpm,mvyz->szhpvy/transpose | solution.py:116
  34.9 3.6 %copy.96 = f32[16,16,320]{2,1,0:T(8,128)} copy(f32[16,16,320]{1,0,2:T(8,128)} %bitcast.108) | data formatting | bytes 655360 | tf_op jit(solution)/shard_map/reshape | solution.py:123
  38.5 4.4 %all-to-all-start.1 = ((f32[16,16,320]{2,1,0:T(8,128)}), f32[16,16,320]{2,1,0:T(8,128)}, u32[]{:S(2)}, u32[]{:S(2)}) async-start(f32[16,16,320]{2,1,0:T(8,128)} %copy.96), calls=%async_computation.1 | async-start | bytes 786432 | tf_op jit(solution)/shard_map/all_to_all | solution.py:123
  54.2 2.0 %fusion.152 = (f32[8,10,10,255]{3,2,1,0:T(8,128)}, f32[8,10,10,255]{3,2,1,0:T(8,128)}) fusion(f32[8,10,12,256]{3,2,1,0:T(8,128)S(1)} %pad_maximum_fusion), kind=kLoop, calls=%fused_computation.341 | loop fusion | bytes 3264000 | tf_op jit(solution)/shard_map/slice | solution.py:54
  59.3 3.2 %collective-permute-start.2 = (f32[8,10,3,256]{3,2,1,0:T(4,128)S(1)}, f32[8,10,3,256]{3,2,1,0:T(4,128)S(1)}, u32[]{:S(2)}, u32[]{:S(2)}) collective-permute-start(f32[8,10,3,256]{3,2,1,0:T(4,128)S(1)} %get-tuple-element.58), channel_id=1, source_target_pairs={{0,1},{1,2},{2,3},{3,4},{4,5},{5,6},{6,7},{7,8},{8,9},{9,10},{10,1... | collective-permute-start | bytes 737288 | tf_op jit(solution)/shard_map/ppermute | solution.py:134
  62.4 4.5 %collective-permute-start.3 = (f32[8,10,3,256]{3,2,1,0:T(4,128)S(1)}, f32[8,10,3,256]{3,2,1,0:T(4,128)S(1)}, u32[]{:S(2)}, u32[]{:S(2)}) collective-permute-start(f32[8,10,3,256]{3,2,1,0:T(4,128)S(1)} %get-tuple-element.59), channel_id=1, source_target_pairs={{1,0},{2,1},{3,2},{4,3},{5,4},{6,5},{7,6},{8,7},{9,8},{10,9},{11,1... | collective-permute-start | bytes 737288 | tf_op jit(solution)/shard_map/ppermute | solution.py:135
  67.0 2.0 %fusion.4 = f32[8,10,10,256]{3,2,1,0:T(8,128)S(1)} fusion(f32[8,5,12,256]{3,2,1,0:T(8,128)S(1)} %get-tuple-element.33, f32[8,5,12,256]{3,2,1,0:T(8,128)S(1)} %get-tuple-element.32, f32[8,10,10,255]{3,2,1,0:T(8,128)S(1)} %copy-done.2, f32[8,10,10,1]{3,2,1,0:T(8,128)} %get-tuple-element.91), kind=kLoop, calls=%fused_computation.44 | loop fusion | flops 2252800 | bytes 2621440 | tf_op jit(solution)/shard_map/mul | solution.py:184
  80.1 15.1 %all-to-all-start.2 = ((f32[32,3,8]{2,1,0:T(4,128)}), f32[32,3,8]{2,1,0:T(4,128)}, u32[]{:S(2)}, u32[]{:S(2)}) async-start(f32[32,3,8]{2,1,0:T(4,128)} %broadcast_in_dim.10), calls=%async_computation.2 | async-start | bytes 131072 | tf_op jit(solution)/shard_map/all_to_all | solution.py:97
  95.3 2.6 %fusion.85 = f32[8,10,4,256]{3,2,1,0:T(4,128)} fusion(f32[8,5,6,256]{3,2,1,0:T(8,128)} %copy-done.1, f32[8,5,6,256]{3,2,1,0:T(8,128)S(1)} %get-tuple-element.42, f32[8,10,10,256]{3,2,1,0:T(8,128)S(1)} %get-tuple-element.25, f32[8,10,4,255]{3,2,1,0:T(4,128)} %fusion.80, f32[8,10,4,1]{3,2,1,0:T(4,128)} %get-tuple-element.84), kind=kLoop, calls=%fused_computation.216 | loop fusion | flops 983040 | bytes 1474560 | tf_op jit(solution)/shard_map/add | solution.py:60
  97.8 10.5 %all-to-all-done.2 = f32[32,3,8]{2,1,0:T(4,128)} async-done(((f32[32,3,8]{2,1,0:T(4,128)}), f32[32,3,8]{2,1,0:T(4,128)}, u32[]{:S(2)}, u32[]{:S(2)}) %all-to-all-start.2) | async-done | bytes 3104 | tf_op jit(solution)/shard_map/all_to_all | solution.py:97
  109.2 2.2 %add_reduce_fusion.1 = (f32[8]{0:T(128)}, f32[8]{0:T(128)}, f32[8,5,4,256]{3,2,1,0:T(4,128)S(1)}, f32[8,5,4,256]{3,2,1,0:T(4,128)S(1)}, f32[8,5,4,256]{3,2,1,0:T(4,128)S(1)}, /*index=5*/f32[8,5,4,256]{3,2,1,0:T(4,128)S(1)}) fusion(f32[8,10,4,256]{3,2,1,0:T(4,128)} %copy-done.9, f32[8,10,4,256]{3,2,1,0:T(4,128)S(1)} %copy-done, f32[8]{0:T(128)S(1)} %get-tuple-element.81, ...), kind=kLoop, calls=%fused_computation.282 | loop fusion | flops 1023984 | bytes 1679552 | tf_op jit(solution)/shard_map/reduce_sum | solution.py:76
  112.5 6.6 %all-to-all-start.3 = ((f32[16,16,320]{2,1,0:T(8,128)}), f32[16,16,320]{2,1,0:T(8,128)S(1)}, u32[]{:S(2)}, u32[]{:S(2)}) async-start(f32[16,16,320]{2,1,0:T(8,128)} %bitcast.33), calls=%async_computation.3 | async-start | bytes 786432 | tf_op jit(solution)/shard_map/all_to_all | solution.py:106
  120.0 2.1 %collective-permute-start.6 = (f32[8,10,4,256]{3,2,1,0:T(4,128)}, f32[8,10,4,256]{3,2,1,0:T(4,128)S(1)}, u32[]{:S(2)}, u32[]{:S(2)}) collective-permute-start(f32[8,10,4,256]{3,2,1,0:T(4,128)} %pad_maximum_fusion.3), channel_id=1, source_target_pairs={{0,1},{1,2},{2,3},{3,4},{4,5},{5,6},{6,7},{7,8},{8,9},{9,10},{10,1... | collective-permute-start | bytes 983048 | tf_op jit(solution)/shard_map/ppermute | solution.py:134
  122.1 5.4 %all-to-all-done.3 = f32[16,16,320]{2,1,0:T(8,128)S(1)} async-done(((f32[16,16,320]{2,1,0:T(8,128)}), f32[16,16,320]{2,1,0:T(8,128)S(1)}, u32[]{:S(2)}, u32[]{:S(2)}) %all-to-all-start.3) | async-done | bytes 327712 | tf_op jit(solution)/shard_map/all_to_all | solution.py:106
  127.5 2.8 %copy.121 = f32[16,16,320]{1,0,2:T(8,128)} copy(f32[16,16,320]{2,1,0:T(8,128)S(1)} %all-to-all-done.3) | data formatting | bytes 655360 | tf_op jit(solution)/shard_map/reshape | solution.py:107
  130.3 5.9 %convolution_bitcast_fusion.3 = f32[256,5,4,16]{0,3,2,1:T(8,128)S(1)} fusion(f32[16,16,8,2,5,4]{1,0,5,4,3,2:T(8,128)} %bitcast.106, f32[256,16,8,1]{0,1,3,2:T(8,128)S(1)} %copy-done.20, f32[256,16,8,1]{0,1,3,2:T(8,128)S(1)} %copy-done.18), kind=kOutput, calls=%fused_computation.66 | convolution fusion | flops 251789312 | bytes 917504 | tf_op jit(solution)/shard_map/mshp,szhpvy->mvyz/dot_general | solution.py:108
  136.3 3.7 %convolution_bitcast_fusion = f32[16,16,8,2,5,4]{0,1,3,2,5,4:T(8,128)} fusion(f32[256,1,4,16]{0,3,2,1:T(8,128)S(1)} %slice.729, f32[256,4,4,16]{0,3,2,1:T(8,128)S(1)} %slice.728, f32[256,2,4,16]{0,3,2,1:T(8,128)S(1)} %slice.731, f32[256,3,4,16]{0,3,2,1:T(8,128)S(1)} %slice.730, f32[16,8,2,256,1,1]{3,2,1,0,5,4:T(2,128)S(1)} %bitcast.111), kind=kOutput, calls=%fused_computation.38 | convolution fusion | flops 251904000 | bytes 1245184 | tf_op jit(solution)/shard_map/shpm,mvyz->szhpvy/dot_general | solution.py:116
  140.0 3.2 %copy.103 = f32[16,16,8,2,5,4]{1,0,5,4,3,2:T(8,128)} copy(f32[16,16,8,2,5,4]{0,1,3,2,5,4:T(8,128)} %convolution_bitcast_fusion) | data formatting | bytes 655360 | tf_op jit(solution)/shard_map/shpm,mvyz->szhpvy/transpose | solution.py:116
  143.3 3.6 %copy.104 = f32[16,16,320]{2,1,0:T(8,128)} copy(f32[16,16,320]{1,0,2:T(8,128)} %bitcast.109) | data formatting | bytes 655360 | tf_op jit(solution)/shard_map/reshape | solution.py:123
  146.9 3.7 %all-to-all-start.4 = ((f32[16,16,320]{2,1,0:T(8,128)}), f32[16,16,320]{2,1,0:T(8,128)S(1)}, u32[]{:S(2)}, u32[]{:S(2)}) async-start(f32[16,16,320]{2,1,0:T(8,128)} %copy.104), calls=%async_computation.4 | async-start | bytes 786432 | tf_op jit(solution)/shard_map/all_to_all | solution.py:123
  151.8 2.0 %fusion.151 = (f32[8,10,10,255]{3,2,1,0:T(8,128)}, f32[8,10,10,255]{3,2,1,0:T(8,128)}) fusion(f32[8,10,12,256]{3,2,1,0:T(8,128)S(1)} %maximum_maximum_fusion), kind=kLoop, calls=%fused_computation.340 | loop fusion | bytes 3264000 | tf_op jit(solution)/shard_map/slice | solution.py:54
  153.7 5.1 %all-to-all-done.4 = f32[16,16,320]{2,1,0:T(8,128)S(1)} async-done(((f32[16,16,320]{2,1,0:T(8,128)}), f32[16,16,320]{2,1,0:T(8,128)S(1)}, u32[]{:S(2)}, u32[]{:S(2)}) %all-to-all-start.4) | async-done | bytes 327712 | tf_op jit(solution)/shard_map/all_to_all | solution.py:123
  162.8 7.6 %all-to-all-start.5 = ((f32[32,3,8]{2,1,0:T(4,128)}), f32[32,3,8]{2,1,0:T(4,128)S(1)}, u32[]{:S(2)}, u32[]{:S(2)}) async-start(f32[32,3,8]{2,1,0:T(4,128)} %broadcast_in_dim.11), calls=%async_computation.5 | async-start | bytes 131072 | tf_op jit(solution)/shard_map/all_to_all | solution.py:97
  173.1 10.4 %all-to-all-done.5 = f32[32,3,8]{2,1,0:T(4,128)S(1)} async-done(((f32[32,3,8]{2,1,0:T(4,128)}), f32[32,3,8]{2,1,0:T(4,128)S(1)}, u32[]{:S(2)}, u32[]{:S(2)}) %all-to-all-start.5) | async-done | bytes 3104 | tf_op jit(solution)/shard_map/all_to_all | solution.py:97
  183.6 3.1 %fusion.8 = (f32[8,10,10,256]{3,2,1,0:T(8,128)S(1)}, f32[8,10,10,256]{3,2,1,0:T(8,128)S(1)}) fusion(f32[8,10,12,256]{3,2,1,0:T(8,128)S(1)} %maximum_maximum_fusion, f32[8,10,10,255]{3,2,1,0:T(8,128)} %get-tuple-element.35, f32[8,10,10,1]{3,2,1,0:T(8,128)} %slice_multiply_fusion, f32[8,10,10,255]{3,2,1,0:T(8,128)} %get-tuple-element.34, ...), kind=kLoop, calls=%fused_computation.49 | loop fusion | flops 2048000 | bytes 6550400 | tf_op jit(solution)/shard_map/add | solution.py:60
  (227 shorter events, 48.4 us)
Async XLA Ops:
  0.0 10.2 %copy-start = (f32[8,10,4,256]{3,2,1,0:T(4,128)S(1)}, f32[8,10,4,256]{3,2,1,0:T(4,128)}, u32[]{:S(2)}) copy-start(f32[8,10,4,256]{3,2,1,0:T(4,128)} %param.4) | copy-start | bytes 983044
  2.6 12.9 %copy-start.44 = (s32[128]{0:T(128)S(1)}, s32[128]{0:T(128)}, u32[]{:S(2)}) copy-start(s32[128]{0:T(128)} %param.6) | copy-start | bytes 1540
  3.4 12.8 %copy-start.21 = (f32[5,4,256]{2,1,0:T(4,128)S(1)}, f32[5,4,256]{2,1,0:T(4,128)}, u32[]{:S(2)}) copy-start(f32[5,4,256]{2,1,0:T(4,128)} %param.5) | copy-start | bytes 61444
  3.4 40.2 %collective-permute-start = (f32[87044]{0:T(1024)}, f32[87044]{0:T(1024)}, u32[]{:S(2)}, u32[]{:S(2)}) collective-permute-start(f32[87044]{0:T(1024)} %pad_maximum_fusion.1), channel_id=1, source_target_pairs={{0,1},{1,2},{2,3},{3,4},{4,5},{5,6},{6,7},{7,8},{8,9},{9,10},{10,1... | collective-permute-start | bytes 1044536 | tf_op jit(solution)/shard_map/ppermute | solution.py:140
  6.4 36.5 %collective-permute-start.1 = (f32[87044]{0:T(1024)}, f32[87044]{0:T(1024)}, u32[]{:S(2)}, u32[]{:S(2)}) collective-permute-start(f32[87044]{0:T(1024)} %pad_maximum_fusion.1), channel_id=1, source_target_pairs={{1,0},{2,1},{3,2},{4,3},{5,4},{6,5},{7,6},{8,7},{9,8},{10,9},{11,1... | collective-permute-start | bytes 1044536 | tf_op jit(solution)/shard_map/ppermute | solution.py:141
  11.2 12.5 %all-to-all-start = ((f32[16,16,320]{2,1,0:T(8,128)}), f32[16,16,320]{2,1,0:T(8,128)}, u32[]{:S(2)}, u32[]{:S(2)}) async-start(f32[16,16,320]{2,1,0:T(8,128)} %bitcast.3), calls=%async_computation | async-start | bytes 786432 | tf_op jit(solution)/shard_map/all_to_all | solution.py:106
  18.0 8.2 %copy-start.17 = (f32[256,16,8,1]{0,1,3,2:T(8,128)}, f32[256,16,8,1]{0,1,3,2:T(8,128)S(1)}, u32[]{:S(2)}) copy-start(f32[256,16,8,1]{0,1,3,2:T(8,128)S(1)} %get-tuple-element.76) | copy-start | bytes 393220
  18.0 8.2 %copy-start.19 = (f32[256,16,8,1]{0,1,3,2:T(8,128)}, f32[256,16,8,1]{0,1,3,2:T(8,128)S(1)}, u32[]{:S(2)}) copy-start(f32[256,16,8,1]{0,1,3,2:T(8,128)S(1)} %get-tuple-element.77) | copy-start | bytes 393220
  38.5 17.7 %all-to-all-start.1 = ((f32[16,16,320]{2,1,0:T(8,128)}), f32[16,16,320]{2,1,0:T(8,128)}, u32[]{:S(2)}, u32[]{:S(2)}) async-start(f32[16,16,320]{2,1,0:T(8,128)} %copy.96), calls=%async_computation.1 | async-start | bytes 786432 | tf_op jit(solution)/shard_map/all_to_all | solution.py:123
  44.4 8.5 %copy-start.49 = (f32[10]{0:T(128)}, f32[10]{0:T(128)S(1)}, u32[]{:S(2)}) copy-start(f32[10]{0:T(128)S(1)} %slice_bitcast_fusion.5) | copy-start | bytes 124
  45.1 28.1 %copy-start.42 = (f32[6]{0:T(128)}, f32[6]{0:T(128)S(1)}, u32[]{:S(2)}) copy-start(f32[6]{0:T(128)S(1)} %slice_bitcast_fusion.3) | copy-start | bytes 76
  46.6 4.6 %copy-start.15 = (f32[5,12,256]{2,1,0:T(8,128)}, f32[5,12,256]{2,1,0:T(8,128)S(1)}, u32[]{:S(2)}) copy-start(f32[5,12,256]{2,1,0:T(8,128)S(1)} %get-tuple-element.74) | copy-start | bytes 184324
  48.1 28.1 %copy-start.45 = (f32[4]{0:T(128)}, f32[4]{0:T(128)S(1)}, u32[]{:S(2)}) copy-start(f32[4]{0:T(128)S(1)} %slice_bitcast_fusion.2) | copy-start | bytes 52
  59.1 7.8 %copy-start.2 = (f32[8,10,10,255]{3,2,1,0:T(8,128)S(1)}, f32[8,10,10,255]{3,2,1,0:T(8,128)}, u32[]{:S(2)}) copy-start(f32[8,10,10,255]{3,2,1,0:T(8,128)} %fusion) | copy-start | bytes 2448004
  59.3 9.8 %collective-permute-start.2 = (f32[8,10,3,256]{3,2,1,0:T(4,128)S(1)}, f32[8,10,3,256]{3,2,1,0:T(4,128)S(1)}, u32[]{:S(2)}, u32[]{:S(2)}) collective-permute-start(f32[8,10,3,256]{3,2,1,0:T(4,128)S(1)} %get-tuple-element.58), channel_id=1, source_target_pairs={{0,1},{1,2},{2,3},{3,4},{4,5},{5,6},{6,7},{7,8},{8,9},{9,10},{10,1... | collective-permute-start | bytes 737288 | tf_op jit(solution)/shard_map/ppermute | solution.py:134
  62.4 6.7 %collective-permute-start.3 = (f32[8,10,3,256]{3,2,1,0:T(4,128)S(1)}, f32[8,10,3,256]{3,2,1,0:T(4,128)S(1)}, u32[]{:S(2)}, u32[]{:S(2)}) collective-permute-start(f32[8,10,3,256]{3,2,1,0:T(4,128)S(1)} %get-tuple-element.59), channel_id=1, source_target_pairs={{1,0},{2,1},{3,2},{4,3},{5,4},{6,5},{7,6},{8,7},{9,8},{10,9},{11,1... | collective-permute-start | bytes 737288 | tf_op jit(solution)/shard_map/ppermute | solution.py:135
  80.1 28.2 %all-to-all-start.2 = ((f32[32,3,8]{2,1,0:T(4,128)}), f32[32,3,8]{2,1,0:T(4,128)}, u32[]{:S(2)}, u32[]{:S(2)}) async-start(f32[32,3,8]{2,1,0:T(4,128)} %broadcast_in_dim.10), calls=%async_computation.2 | async-start | bytes 131072 | tf_op jit(solution)/shard_map/all_to_all | solution.py:97
  112.5 14.9 %all-to-all-start.3 = ((f32[16,16,320]{2,1,0:T(8,128)}), f32[16,16,320]{2,1,0:T(8,128)S(1)}, u32[]{:S(2)}, u32[]{:S(2)}) async-start(f32[16,16,320]{2,1,0:T(8,128)} %bitcast.33), calls=%async_computation.3 | async-start | bytes 786432 | tf_op jit(solution)/shard_map/all_to_all | solution.py:106
  120.0 10.3 %copy-start.18 = (f32[256,16,8,1]{0,1,3,2:T(8,128)S(1)}, f32[256,16,8,1]{0,1,3,2:T(8,128)}, u32[]{:S(2)}) copy-start(f32[256,16,8,1]{0,1,3,2:T(8,128)} %copy-done.17) | copy-start | bytes 393220
  120.0 10.3 %copy-start.20 = (f32[256,16,8,1]{0,1,3,2:T(8,128)S(1)}, f32[256,16,8,1]{0,1,3,2:T(8,128)}, u32[]{:S(2)}) copy-start(f32[256,16,8,1]{0,1,3,2:T(8,128)} %copy-done.19) | copy-start | bytes 393220
  120.0 30.6 %collective-permute-start.6 = (f32[8,10,4,256]{3,2,1,0:T(4,128)}, f32[8,10,4,256]{3,2,1,0:T(4,128)S(1)}, u32[]{:S(2)}, u32[]{:S(2)}) collective-permute-start(f32[8,10,4,256]{3,2,1,0:T(4,128)} %pad_maximum_fusion.3), channel_id=1, source_target_pairs={{0,1},{1,2},{2,3},{3,4},{4,5},{5,6},{6,7},{7,8},{8,9},{9,10},{10,1... | collective-permute-start | bytes 983048 | tf_op jit(solution)/shard_map/ppermute | solution.py:134
  122.1 28.6 %collective-permute-start.7 = (f32[8,10,4,256]{3,2,1,0:T(4,128)}, f32[8,10,4,256]{3,2,1,0:T(4,128)S(1)}, u32[]{:S(2)}, u32[]{:S(2)}) collective-permute-start(f32[8,10,4,256]{3,2,1,0:T(4,128)} %pad_maximum_fusion.3), channel_id=1, source_target_pairs={{1,0},{2,1},{3,2},{4,3},{5,4},{6,5},{7,6},{8,7},{9,8},{10,9},{11,1... | collective-permute-start | bytes 983048 | tf_op jit(solution)/shard_map/ppermute | solution.py:135
  143.3 7.4 %copy-start.6 = (f32[8,10,4,256]{3,2,1,0:T(4,128)S(1)}, f32[8,10,4,256]{3,2,1,0:T(4,128)}, u32[]{:S(2)}) copy-start(f32[8,10,4,256]{3,2,1,0:T(4,128)} %copy-done.5) | copy-start | bytes 983044
  143.3 7.4 %copy-start.8 = (f32[8,10,4,256]{3,2,1,0:T(4,128)S(1)}, f32[8,10,4,256]{3,2,1,0:T(4,128)}, u32[]{:S(2)}) copy-start(f32[8,10,4,256]{3,2,1,0:T(4,128)} %copy-done.7) | copy-start | bytes 983044
  146.9 4.0 %copy-start.12 = (f32[8,5,4,256]{3,2,1,0:T(4,128)S(1)}, f32[8,5,4,256]{3,2,1,0:T(4,128)}, u32[]{:S(2)}) copy-start(f32[8,5,4,256]{3,2,1,0:T(4,128)} %copy-done.11) | copy-start | bytes 491524
  146.9 11.9 %all-to-all-start.4 = ((f32[16,16,320]{2,1,0:T(8,128)}), f32[16,16,320]{2,1,0:T(8,128)S(1)}, u32[]{:S(2)}, u32[]{:S(2)}) async-start(f32[16,16,320]{2,1,0:T(8,128)} %copy.104), calls=%async_computation.4 | async-start | bytes 786432 | tf_op jit(solution)/shard_map/all_to_all | solution.py:123
  160.9 11.2 %copy-start.50 = (f32[10]{0:T(128)S(1)}, f32[10]{0:T(128)}, u32[]{:S(2)}) copy-start(f32[10]{0:T(128)} %copy-done.49) | copy-start | bytes 124
  162.8 20.7 %all-to-all-start.5 = ((f32[32,3,8]{2,1,0:T(4,128)}), f32[32,3,8]{2,1,0:T(4,128)S(1)}, u32[]{:S(2)}, u32[]{:S(2)}) async-start(f32[32,3,8]{2,1,0:T(4,128)} %broadcast_in_dim.11), calls=%async_computation.5 | async-start | bytes 131072 | tf_op jit(solution)/shard_map/all_to_all | solution.py:97
  170.5 13.1 %collective-permute-start.4 = (f32[8,10,3,256]{3,2,1,0:T(4,128)}, f32[8,10,3,256]{3,2,1,0:T(4,128)}, u32[]{:S(2)}, u32[]{:S(2)}) collective-permute-start(f32[8,10,3,256]{3,2,1,0:T(4,128)} %get-tuple-element.56), channel_id=1, source_target_pairs={{0,1},{1,2},{2,3},{3,4},{4,5},{5,6},{6,7},{7,8},{8,9},{9,10},{10,1... | collective-permute-start | bytes 737288 | tf_op jit(solution)/shard_map/ppermute | solution.py:134
  172.1 11.4 %collective-permute-start.5 = (f32[8,10,3,256]{3,2,1,0:T(4,128)}, f32[8,10,3,256]{3,2,1,0:T(4,128)}, u32[]{:S(2)}, u32[]{:S(2)}) collective-permute-start(f32[8,10,3,256]{3,2,1,0:T(4,128)} %get-tuple-element.57), channel_id=1, source_target_pairs={{1,0},{2,1},{3,2},{4,3},{5,4},{6,5},{7,6},{8,7},{9,8},{10,9},{11,1... | collective-permute-start | bytes 737288 | tf_op jit(solution)/shard_map/ppermute | solution.py:135
  183.6 3.1 %copy-start.25 = (f32[5,10,256]{2,1,0:T(8,128)S(1)}, f32[5,10,256]{2,1,0:T(8,128)}, u32[]{:S(2)}) copy-start(f32[5,10,256]{2,1,0:T(8,128)} %copy-done.24) | copy-start | bytes 153604
  183.6 3.1 %copy-start.27 = (f32[5,10,256]{2,1,0:T(8,128)S(1)}, f32[5,10,256]{2,1,0:T(8,128)}, u32[]{:S(2)}) copy-start(f32[5,10,256]{2,1,0:T(8,128)} %copy-done.26) | copy-start | bytes 153604
  (35 other events, 39.3 us)
